TPU v7x, 128 devices: a whole 4x4x4 slice. The times are simulated.
128 devices in a mesh: dp: 128 (over x, y, z, core).
Axes of the slice: x: 4, y: 4, z: 4, core: 2. Of those that a mesh axis runs over, the one named last changes fastest.
Arguments:
- hidden_in: bfloat16 [32768, 4096], P('dp'), may hold values from -24 to 24
- queries: bfloat16 [32768, 2048], P('dp'), may hold values from -16 to 16
- keys: bfloat16 [32768, 512], P('dp'), may hold values from -16 to 16
- values: bfloat16 [32768, 512], P('dp'), may hold values from -6 to 6
- grad_attn: bfloat16 [32768, 2048], P('dp'), may hold values from -6 to 6
- send_rows: int32 [4, 128], replicated, may hold values from -1 to 255, as said below
- slot_docs: int32 [128, 4], P('dp'), may hold values from -1 to 255, as said below
Outputs:
- grad_queries: bfloat16 [32768, 2048], P('dp')
- grad_keys: bfloat16 [32768, 512], P('dp')
- grad_values: bfloat16 [32768, 512], P('dp')
- grad_wv: float32 [4096, 512], P('dp')
Inputs may be any that keep to these rules, and one draw needn't show every extreme that they name: `send_rows`: every owner sends the same local rows to a rank. Each local row appears exactly once. The rows sent to one rank form whole documents at consecutive slots, the local rows of a document consecutive and rising with the slot; a document has at most 4 local rows, and in every draw some rank has all 4 slots used. slot_docs[r, j] is -1 exactly where send_rows[j, r] is -1; slots with the same number hold one document, and distinct documents have distinct numbers.
All inputs are finite; a program needn't handle non-finite values.
Results may differ from a plain program's by a relative error of at most 0.0057.
Values may be sent and summed in bfloat16 or wider, within the bound.
No kernel may reach another device: no remote copies, remote signals or barrier semaphores. Data moves between devices by JAX's collectives and lax.ppermute only.
A program may use at most 128 MiB of HBM per device.

v0:
```python
import math

import jax
import jax.numpy as jnp
from jax import lax
from jax.sharding import Mesh, PartitionSpec as P
import numpy as np
from jax.experimental import pallas as pl
from jax.experimental.pallas import tpu as pltpu

HQ = 16
HK = 4
DH = 128
INTERPRET = False


NT = (((1,), (1,)), ((), ()))
TN = (((0,), (0,)), ((), ()))


def attend_kernel(seg_col_ref, seg_row_ref, q_ref, k_ref, v_ref, o_ref, dq_ref, dk_ref, dv_ref):
    row_count = q_ref.shape[0]
    group_size = HQ // HK
    score_scale = 1.0 / math.sqrt(DH)
    seg_col = seg_col_ref[...]
    live_rows = seg_col >= 0
    row_ids = lax.broadcasted_iota(jnp.int32, (row_count, row_count), 0)
    col_ids = lax.broadcasted_iota(jnp.int32, (row_count, row_count), 1)
    allowed = (seg_col == seg_row_ref[...]) & (col_ids <= row_ids) & live_rows
    k_group = k_ref[...]
    v_group = v_ref[...]
    dk_acc = jnp.zeros((row_count, DH), jnp.float32)
    dv_acc = jnp.zeros((row_count, DH), jnp.float32)
    for head in range(group_size):
        cols = slice(head * DH, (head + 1) * DH)
        q_head = q_ref[:, cols]
        o_head = o_ref[:, cols]
        scores = lax.dot_general(q_head, k_group, NT, preferred_element_type=jnp.float32)
        scores = jnp.where(allowed, scores * score_scale, jnp.float32(-1000000000.0))
        row_max = jnp.max(scores, axis=1, keepdims=True)
        weights = jnp.exp(scores - row_max)
        attn_probs = weights / jnp.sum(weights, axis=1, keepdims=True)
        attn_probs = jnp.where(live_rows, attn_probs, jnp.float32(0.0))
        probs_b = attn_probs.astype(jnp.bfloat16)
        dv_acc = dv_acc + lax.dot_general(probs_b, o_head, TN, preferred_element_type=jnp.float32)
        dprob = lax.dot_general(o_head, v_group, NT, preferred_element_type=jnp.float32)
        row_delta = jnp.sum(attn_probs * dprob, axis=1, keepdims=True)
        dscore = (attn_probs * (dprob - row_delta) * score_scale).astype(jnp.bfloat16)
        dq_ref[:, cols] = jnp.dot(dscore, k_group, preferred_element_type=jnp.float32).astype(
            dq_ref.dtype
        )
        dk_acc = dk_acc + lax.dot_general(dscore, q_head, TN, preferred_element_type=jnp.float32)
    dk_ref[...] = dk_acc.astype(dk_ref.dtype)
    dv_ref[...] = dv_acc.astype(dv_ref.dtype)


def attend_rows(q_rows, k_rows, v_rows, o_rows, segment):
    row_count = q_rows.shape[0]
    q_w = (HQ // HK) * DH
    seg = segment.astype(jnp.int32)
    whole = lambda g: (0, 0)
    q_spec = pl.BlockSpec((row_count, q_w), lambda g: (0, g))
    kv_spec = pl.BlockSpec((row_count, DH), lambda g: (0, g))
    return pl.pallas_call(
        attend_kernel,
        grid=(HK,),
        in_specs=[
            pl.BlockSpec((row_count, 1), whole),
            pl.BlockSpec((1, row_count), whole),
            q_spec,
            kv_spec,
            kv_spec,
            q_spec,
        ],
        out_specs=[q_spec, kv_spec, kv_spec],
        out_shape=[
            jax.ShapeDtypeStruct(q_rows.shape, jnp.bfloat16),
            jax.ShapeDtypeStruct(k_rows.shape, jnp.bfloat16),
            jax.ShapeDtypeStruct(v_rows.shape, jnp.bfloat16),
        ],
        compiler_params=pltpu.CompilerParams(dimension_semantics=("arbitrary",)),
        interpret=INTERPRET,
    )(seg.reshape(row_count, 1), seg.reshape(1, row_count), q_rows, k_rows, v_rows, o_rows)


CHIP, CORE = "chip", "core"
DP = (CHIP, CORE)


def local(hidden_in, queries, keys, values, grad_attn, send_rows, slot_docs):
    chips, cores = lax.axis_size(CHIP), lax.axis_size(CORE)
    owners = chips * cores
    slot_count = send_rows.shape[0]
    tok_rows = queries.shape[0]
    live_send = send_rows >= 0
    pick_rows = jnp.maximum(send_rows, 0)
    grad_scale = 1.0 / math.sqrt(tok_rows * owners)

    def pack_rows(table):
        return jnp.where(live_send[:, :, None], table[pick_rows], jnp.zeros((), table.dtype))

    def flatten(block):
        return block.reshape(slot_count * owners, block.shape[2])

    def unflatten(block):
        return block.reshape(slot_count, owners, block.shape[1])

    targets = jnp.where(live_send, send_rows, tok_rows).reshape(-1)

    def place_rows(block):
        return (
            jnp.zeros((tok_rows, block.shape[2]), block.dtype)
            .at[targets]
            .set(flatten(block), mode="drop")
        )

    q_in, k_in, v_in, o_in = (
        lax.all_to_all(pack_rows(queries), DP, split_axis=1, concat_axis=1, tiled=True),
        lax.all_to_all(pack_rows(keys), DP, split_axis=1, concat_axis=1, tiled=True),
        lax.all_to_all(pack_rows(values), DP, split_axis=1, concat_axis=1, tiled=True),
        lax.all_to_all(pack_rows(grad_attn), DP, split_axis=1, concat_axis=1, tiled=True),
    )
    segment = jnp.broadcast_to(slot_docs[0][:, None], (slot_count, owners)).reshape(-1)
    grad_q_rows, grad_k_rows, grad_v_rows = attend_rows(
        flatten(q_in), flatten(k_in), flatten(v_in), flatten(o_in), segment
    )
    q_home, k_home, v_home = (
        lax.all_to_all(unflatten(grad_q_rows), DP, split_axis=1, concat_axis=1, tiled=True),
        lax.all_to_all(unflatten(grad_k_rows), DP, split_axis=1, concat_axis=1, tiled=True),
        lax.all_to_all(unflatten(grad_v_rows), DP, split_axis=1, concat_axis=1, tiled=True),
    )
    grad_queries = place_rows(q_home)
    grad_keys = place_rows(k_home)
    grad_values = place_rows(v_home)
    core = lax.axis_index(CORE)
    swap = [(0, 1), (1, 0)]
    blocks = hidden_in.reshape(tok_rows, chips, cores, -1)
    mine = lax.dynamic_index_in_dim(blocks, core, axis=2, keepdims=False)
    theirs = lax.dynamic_index_in_dim(blocks, 1 - core, axis=2, keepdims=False)
    from_partner = lax.ppermute(theirs, CORE, swap)
    hidden_pair = jnp.concatenate((mine, from_partner), axis=0).reshape(2 * tok_rows, -1)
    grad_pair = jnp.concatenate((grad_values, lax.ppermute(grad_values, CORE, swap)), axis=0)
    partial = jnp.einsum("td,tc->dc", hidden_pair, grad_pair, preferred_element_type=jnp.float32)
    partial = partial.reshape(chips, partial.shape[0] // chips, partial.shape[1])
    grad_wv = lax.all_to_all(partial, CHIP, 0, 0, tiled=True).sum(0) * grad_scale
    return (grad_queries, grad_keys, grad_values, grad_wv)


def solution(mesh):
    devices = np.asarray(mesh.devices).reshape(-1)
    pair_mesh = Mesh(devices.reshape(-1, 2), DP)
    rows = P(DP, None)
    placed = (rows, rows, rows, rows, rows, P(), rows)
    return jax.shard_map(
        local,
        mesh=pair_mesh,
        in_specs=placed,
        out_specs=(rows, rows, rows, rows),
        check_vma=False,
    )
```

profile of v0, /device:TPU:0, one launch (start us, length us, event | category | flops | bytes accessed | tf_op | source)
XLA Modules:
  0.0 283.5 jit_solution(8280064193333740096)
XLA Ops:
  0.6 0.0 copy-start
  0.6 0.8 broadcast_compare_fusion
  1.4 0.7 maximum_bitcast_fusion.2
  2.1 0.1 copy.31
  2.3 0.0 copy-start.2
  2.3 3.0 %gather_fusion.2 = bf16[512,512]{1,0:T(8,128)(2,1)S(1)} fusion(bf16[256,512]{1,0:T(8,128)(2,1)} %param.10, s32[1024]{0:T(1024)S(1)} %pad_clamp_fusion), kind=kCustom, calls=%fused_computation.2 | custom fusion | bytes 1050624 | tf_op jit(solution)/shard_map/gather | solution.py:100
  5.3 0.0 copy-done.2
  5.3 2.0 gather_fusion.1
  7.3 1.9 copy_select_fusion.2
  9.1 11.2 %all-to-all-start.2 = ((bf16[4,128,512]{2,0,1:T(4,128)(2,1)}), bf16[4,128,512]{2,0,1:T(4,128)(2,1)S(1)}, u32[]{:S(2)}, u32[]{:S(2)}) async-start(bf16[4,128,512]{2,0,1:T(4,128)(2,1)} %get-tuple-element.14), calls=%async_computation.2 | async-start | bytes 1048576 | tf_op jit(solution)/shard_map/all_to_all | solution.py:120
  20.3 0.0 copy-done
  20.3 0.0 copy-start.1
  20.3 3.3 %gather_fusion.3 = bf16[512,2048]{1,0:T(8,128)(2,1)} fusion(bf16[256,2048]{1,0:T(8,128)(2,1)S(1)} %copy-done, s32[1024]{0:T(1024)S(1)} %pad_clamp_fusion), kind=kCustom, calls=%fused_computation.3 | custom fusion | bytes 4196352 | tf_op jit(solution)/shard_map/gather | solution.py:100
  23.6 0.0 copy-done.1
  23.6 3.3 %gather_fusion = bf16[512,2048]{1,0:T(8,128)(2,1)} fusion(bf16[256,2048]{1,0:T(8,128)(2,1)S(1)} %copy-done.1, s32[1024]{0:T(1024)S(1)} %pad_clamp_fusion), kind=kCustom, calls=%fused_computation | custom fusion | bytes 4196352 | tf_op jit(solution)/shard_map/gather | solution.py:100
  26.9 7.1 %all-to-all-done.2 = bf16[4,128,512]{2,0,1:T(4,128)(2,1)S(1)} async-done(((bf16[4,128,512]{2,0,1:T(4,128)(2,1)}), bf16[4,128,512]{2,0,1:T(4,128)(2,1)S(1)}, u32[]{:S(2)}, u32[]{:S(2)}) %all-to-all-start.2) | async-done | bytes 524320 | tf_op jit(solution)/shard_map/all_to_all | solution.py:120
  34.0 0.0 copy-start.4
  34.0 5.7 %all-to-all-start.1 = ((bf16[4,128,512]{2,0,1:T(4,128)(2,1)}), bf16[4,128,512]{2,0,1:T(4,128)(2,1)}, u32[]{:S(2)}, u32[]{:S(2)}) async-start(bf16[4,128,512]{2,0,1:T(4,128)(2,1)} %get-tuple-element.15), calls=%async_computation.1 | async-start | bytes 1048576 | tf_op jit(solution)/shard_map/all_to_all | solution.py:119
  39.8 0.0 copy-done.4
  39.8 7.5 %copy_select_fusion = (bf16[4,128,2048]{2,0,1:T(4,128)(2,1)S(1)}, bf16[4,128,2048]{2,0,1:T(4,128)(2,1)}) fusion(bf16[4,128,2048]{2,1,0:T(8,128)(2,1)} %bitcast.39, pred[4,128]{0,1:T(8,128)(4,1)S(1)} %copy.31, bf16[4,128,2048]{2,1,0:T(8,128)(2,1)} %bitcast.40), kind=kLoop, calls=%fused_computation.8 | loop fusion | flops 2097152 | bytes 8389120 | tf_op jit(solution)/shard_map/jit(_where)/select_n | solution.py:100
  47.3 5.8 %all-to-all-done.1 = bf16[4,128,512]{2,0,1:T(4,128)(2,1)} async-done(((bf16[4,128,512]{2,0,1:T(4,128)(2,1)}), bf16[4,128,512]{2,0,1:T(4,128)(2,1)}, u32[]{:S(2)}, u32[]{:S(2)}) %all-to-all-start.1) | async-done | bytes 524320 | tf_op jit(solution)/shard_map/all_to_all | solution.py:119
  53.1 35.2 %all_to_all.40 = bf16[4,128,2048]{2,0,1:T(4,128)(2,1)} all-to-all(bf16[4,128,2048]{2,0,1:T(4,128)(2,1)S(1)} %get-tuple-element.12), channel_id=1, replica_groups=mesh['chip'=64,'core'=2] {'chip','core'}, dimensions={1} | all-to-all | bytes 4194304 | tf_op jit(solution)/shard_map/all_to_all | solution.py:121
  88.3 0.0 copy-start.7
  88.3 5.0 %all-to-all-start = ((bf16[4,128,2048]{2,0,1:T(4,128)(2,1)}), bf16[4,128,2048]{2,0,1:T(4,128)(2,1)S(1)}, u32[]{:S(2)}, u32[]{:S(2)}) async-start(bf16[4,128,2048]{2,0,1:T(4,128)(2,1)} %get-tuple-element.13), calls=%async_computation | async-start | bytes 4194304 | tf_op jit(solution)/shard_map/all_to_all | solution.py:118
  93.3 0.0 copy-done.7
  93.3 0.1 broadcast_in_dim.62
  93.4 0.9 copy.41.seg_col_ref
  94.2 1.9 copy.38
  96.2 1.9 copy.36
  98.1 4.1 %copy.40 = bf16[4,128,2048]{2,1,0:T(8,128)(2,1)} copy(bf16[4,128,2048]{2,0,1:T(4,128)(2,1)} %all_to_all.40) | data formatting | bytes 4194304 | tf_op jit(solution)/shard_map/all_to_all | solution.py:121
  102.1 0.0 copy-done.6
  102.1 21.6 %all-to-all-done = bf16[4,128,2048]{2,0,1:T(4,128)(2,1)S(1)} async-done(((bf16[4,128,2048]{2,0,1:T(4,128)(2,1)}), bf16[4,128,2048]{2,0,1:T(4,128)(2,1)S(1)}, u32[]{:S(2)}, u32[]{:S(2)}) %all-to-all-start) | async-done | bytes 2097184 | tf_op jit(solution)/shard_map/all_to_all | solution.py:118
  123.7 2.5 copy.33
  126.2 20.9 %shard_map.102 = (bf16[512,2048]{1,0:T(8,128)(2,1)}, bf16[512,512]{1,0:T(8,128)(2,1)}, bf16[512,512]{1,0:T(8,128)(2,1)}) custom-call(s32[512,1]{1,0:T(8,128)} %copy.41.seg_col_ref, s32[1,512]{1,0:T(1,128)} %bitcast.55, bf16[512,2048]{1,0:T(8,128)(2,1)} %bitcast.37, bf16[512,512]{1,0:T(8,128)(2,1)} %bitcast.44, bf16[512,512]{1,0:T(8,128)(2,1)} %bitcast.43, ...), custom_call_target="tpu_custom_call" | custom-call | tf_op jit(solution)/shard_map/pallas_call | solution.py:64
  147.1 2.4 copy.44
  149.5 5.7 %all-to-all-start.5 = ((bf16[4,128,512]{2,0,1:T(4,128)(2,1)}), bf16[4,128,512]{2,0,1:T(4,128)(2,1)}, u32[]{:S(2)}, u32[]{:S(2)}) async-start(bf16[4,128,512]{2,0,1:T(4,128)(2,1)} %copy.44), calls=%async_computation.5 | async-start | bytes 1048576 | tf_op jit(solution)/shard_map/all_to_all | solution.py:129
  155.3 2.2 copy.46
  157.5 11.1 %all-to-all-done.5 = bf16[4,128,512]{2,0,1:T(4,128)(2,1)} async-done(((bf16[4,128,512]{2,0,1:T(4,128)(2,1)}), bf16[4,128,512]{2,0,1:T(4,128)(2,1)}, u32[]{:S(2)}, u32[]{:S(2)}) %all-to-all-start.5) | async-done | bytes 524320 | tf_op jit(solution)/shard_map/all_to_all | solution.py:129
  168.6 5.7 %all-to-all-start.6 = ((bf16[4,128,512]{2,0,1:T(4,128)(2,1)}), bf16[4,128,512]{2,0,1:T(4,128)(2,1)}, u32[]{:S(2)}, u32[]{:S(2)}) async-start(bf16[4,128,512]{2,0,1:T(4,128)(2,1)} %copy.46), calls=%async_computation.6 | async-start | bytes 1048576 | tf_op jit(solution)/shard_map/all_to_all | solution.py:130
  174.3 0.0 copy-done.3
  174.3 3.0 %copy.42 = bf16[4,128,2048]{2,0,1:T(4,128)(2,1)} copy(bf16[4,128,2048]{2,1,0:T(8,128)(2,1)S(1)} %bitcast.45) | data formatting | bytes 4194304 | tf_op jit(solution)/shard_map/reshape | solution.py:106
  177.3 10.3 %all-to-all-done.6 = bf16[4,128,512]{2,0,1:T(4,128)(2,1)} async-done(((bf16[4,128,512]{2,0,1:T(4,128)(2,1)}), bf16[4,128,512]{2,0,1:T(4,128)(2,1)}, u32[]{:S(2)}, u32[]{:S(2)}) %all-to-all-start.6) | async-done | bytes 524320 | tf_op jit(solution)/shard_map/all_to_all | solution.py:130
  187.6 6.0 %all-to-all-start.4 = ((bf16[4,128,2048]{2,0,1:T(4,128)(2,1)}), bf16[4,128,2048]{2,0,1:T(4,128)(2,1)}, u32[]{:S(2)}, u32[]{:S(2)}) async-start(bf16[4,128,2048]{2,0,1:T(4,128)(2,1)} %copy.42), calls=%async_computation.4 | async-start | bytes 4194304 | tf_op jit(solution)/shard_map/all_to_all | solution.py:128
  193.6 3.3 %copy.48 = bf16[256,4096]{0,1:T(8,128)(2,1)S(1)} copy(bf16[256,4096]{1,0:T(8,128)(2,1)} %param.7) | data formatting | bytes 4194304 | tf_op args[0]
  196.9 1.5 constant_dynamic-slice_fusion
  198.4 0.0 collective-permute-start
  198.5 1.1 copy.47
  199.6 2.4 scatter_custom_fusion.2
  202.0 0.0 copy-start.5
  202.0 0.6 collective-permute-start.1
  202.6 0.0 collective-permute-done
  202.6 1.4 pad_maximum_fusion
  204.0 0.0 collective-permute-done.1
  204.0 0.0 copy-done.5
  204.0 3.2 %fusion = f32[64,32,512]{2,1,0:T(8,128)} fusion(bf16[64,32,512]{2,1,0:T(8,128)(2,1)S(1)} %bitcast.41, bf16[256,512]{1,0:T(8,128)(2,1)S(1)} %collective-permute-done.1, bf16[256,512]{1,0:T(8,128)(2,1)S(1)} %scatter_custom_fusion.2), kind=kOutput, calls=%fused_computation.12 | convolution fusion | flops 1074790400 | bytes 6815744 | tf_op jit(solution)/shard_map/td,tc->dc/dot_general | solution.py:143
  207.3 16.3 %all-to-all-done.4 = bf16[4,128,2048]{2,0,1:T(4,128)(2,1)} async-done(((bf16[4,128,2048]{2,0,1:T(4,128)(2,1)}), bf16[4,128,2048]{2,0,1:T(4,128)(2,1)}, u32[]{:S(2)}, u32[]{:S(2)}) %all-to-all-start.4) | async-done | bytes 2097184 | tf_op jit(solution)/shard_map/all_to_all | solution.py:128
  223.6 5.7 %all-to-all-start.7 = ((f32[64,32,512]{2,1,0:T(8,128)}), f32[64,32,512]{2,1,0:T(8,128)}, u32[]{:S(2)}, u32[]{:S(2)}) async-start(f32[64,32,512]{2,1,0:T(8,128)} %fusion), calls=%async_computation.7 | async-start | bytes 8388608 | tf_op jit(solution)/shard_map/all_to_all | solution.py:145
  229.2 1.1 copy.45
  230.4 3.0 %scatter_custom_fusion.1 = bf16[256,512]{1,0:T(8,128)(2,1)} fusion(s32[512]{0:T(512)S(1)} %bitcast.58, bf16[512,512]{1,0:T(8,128)(2,1)S(1)} %bitcast.53, bf16[]{:T(256)} %constant.9.clone.1), kind=kCustom, calls=%fused_computation.21 | custom fusion | bytes 262146 | tf_op jit(solution)/shard_map/scatter | solution.py:114
  233.4 2.7 copy.43
  236.1 4.5 %scatter_custom_fusion = bf16[256,2048]{1,0:T(8,128)(2,1)} fusion(s32[512]{0:T(512)S(1)} %bitcast.59, bf16[512,2048]{1,0:T(8,128)(2,1)S(1)} %bitcast.46, bf16[]{:T(256)} %constant.9.clone.1), kind=kCustom, calls=%fused_computation.17 | custom fusion | bytes 1048578 | tf_op jit(solution)/shard_map/scatter | solution.py:114
  240.7 39.7 %all-to-all-done.7 = f32[64,32,512]{2,1,0:T(8,128)} async-done(((f32[64,32,512]{2,1,0:T(8,128)}), f32[64,32,512]{2,1,0:T(8,128)}, u32[]{:S(2)}, u32[]{:S(2)}) %all-to-all-start.7) | async-done | bytes 4194336 | tf_op jit(solution)/shard_map/all_to_all | solution.py:145
  280.4 2.5 reduce_sum.9
  282.9 0.6 broadcast_multiply_fusion
  (4 shorter events, 0.0 us)
Async XLA Ops:
  0.6 19.7 %copy-start = (bf16[256,2048]{1,0:T(8,128)(2,1)S(1)}, bf16[256,2048]{1,0:T(8,128)(2,1)}, u32[]{:S(2)}) copy-start(bf16[256,2048]{1,0:T(8,128)(2,1)} %param.11) | copy-start | bytes 3145732
  2.3 3.0 %copy-start.2 = (bf16[256,512]{1,0:T(8,128)(2,1)S(1)}, bf16[256,512]{1,0:T(8,128)(2,1)}, u32[]{:S(2)}) copy-start(bf16[256,512]{1,0:T(8,128)(2,1)} %param.9) | copy-start | bytes 786436
  9.1 24.9 %all-to-all-start.2 = ((bf16[4,128,512]{2,0,1:T(4,128)(2,1)}), bf16[4,128,512]{2,0,1:T(4,128)(2,1)S(1)}, u32[]{:S(2)}, u32[]{:S(2)}) async-start(bf16[4,128,512]{2,0,1:T(4,128)(2,1)} %get-tuple-element.14), calls=%async_computation.2 | async-start | bytes 1048576 | tf_op jit(solution)/shard_map/all_to_all | solution.py:120
  20.3 3.3 %copy-start.1 = (bf16[256,2048]{1,0:T(8,128)(2,1)S(1)}, bf16[256,2048]{1,0:T(8,128)(2,1)}, u32[]{:S(2)}) copy-start(bf16[256,2048]{1,0:T(8,128)(2,1)} %param.8) | copy-start | bytes 3145732
  34.0 5.7 %copy-start.4 = (bf16[4,128,512]{2,0,1:T(4,128)(2,1)}, bf16[4,128,512]{2,0,1:T(4,128)(2,1)S(1)}, u32[]{:S(2)}) copy-start(bf16[4,128,512]{2,0,1:T(4,128)(2,1)S(1)} %all-to-all-done.2) | copy-start | bytes 1572868
  34.0 19.0 %all-to-all-start.1 = ((bf16[4,128,512]{2,0,1:T(4,128)(2,1)}), bf16[4,128,512]{2,0,1:T(4,128)(2,1)}, u32[]{:S(2)}, u32[]{:S(2)}) async-start(bf16[4,128,512]{2,0,1:T(4,128)(2,1)} %get-tuple-element.15), calls=%async_computation.1 | async-start | bytes 1048576 | tf_op jit(solution)/shard_map/all_to_all | solution.py:119
  88.3 5.0 %copy-start.7 = (s32[1,4]{1,0:T(1,128)S(1)}, s32[1,4]{1,0:T(1,128)}, u32[]{:S(2)}) copy-start(s32[1,4]{1,0:T(1,128)} %param.13) | copy-start | bytes 52
  88.3 35.4 %all-to-all-start = ((bf16[4,128,2048]{2,0,1:T(4,128)(2,1)}), bf16[4,128,2048]{2,0,1:T(4,128)(2,1)S(1)}, u32[]{:S(2)}, u32[]{:S(2)}) async-start(bf16[4,128,2048]{2,0,1:T(4,128)(2,1)} %get-tuple-element.13), calls=%async_computation | async-start | bytes 4194304 | tf_op jit(solution)/shard_map/all_to_all | solution.py:118
  93.4 8.8 %copy-start.6 = (s32[4,128]{1,0:T(4,128)}, s32[4,128]{1,0:T(4,128)S(1)}, u32[]{:S(2)}) copy-start(s32[4,128]{1,0:T(4,128)S(1)} %broadcast_in_dim.62) | copy-start | bytes 6148
  147.1 27.2 %copy-start.3 = (bf16[512,2048]{1,0:T(8,128)(2,1)S(1)}, bf16[512,2048]{1,0:T(8,128)(2,1)}, u32[]{:S(2)}) copy-start(bf16[512,2048]{1,0:T(8,128)(2,1)} %get-tuple-element.7) | copy-start | bytes 6291460
  149.5 19.0 %all-to-all-start.5 = ((bf16[4,128,512]{2,0,1:T(4,128)(2,1)}), bf16[4,128,512]{2,0,1:T(4,128)(2,1)}, u32[]{:S(2)}, u32[]{:S(2)}) async-start(bf16[4,128,512]{2,0,1:T(4,128)(2,1)} %copy.44), calls=%async_computation.5 | async-start | bytes 1048576 | tf_op jit(solution)/shard_map/all_to_all | solution.py:129
  168.6 19.1 %all-to-all-start.6 = ((bf16[4,128,512]{2,0,1:T(4,128)(2,1)}), bf16[4,128,512]{2,0,1:T(4,128)(2,1)}, u32[]{:S(2)}, u32[]{:S(2)}) async-start(bf16[4,128,512]{2,0,1:T(4,128)(2,1)} %copy.46), calls=%async_computation.6 | async-start | bytes 1048576 | tf_op jit(solution)/shard_map/all_to_all | solution.py:130
  187.6 35.9 %all-to-all-start.4 = ((bf16[4,128,2048]{2,0,1:T(4,128)(2,1)}), bf16[4,128,2048]{2,0,1:T(4,128)(2,1)}, u32[]{:S(2)}, u32[]{:S(2)}) async-start(bf16[4,128,2048]{2,0,1:T(4,128)(2,1)} %copy.42), calls=%async_computation.4 | async-start | bytes 4194304 | tf_op jit(solution)/shard_map/all_to_all | solution.py:128
  198.4 4.2 %collective-permute-start = (bf16[256,64,32]{0,2,1:T(8,128)(2,1)}, bf16[256,64,32]{0,2,1:T(8,128)(2,1)S(1)}, u32[]{:S(2)}, u32[]{:S(2)}) collective-permute-start(bf16[256,64,32]{0,2,1:T(8,128)(2,1)} %get-tuple-element.11), channel_id=1, source_target_pairs={{0,1},{1,0},{2,3},{3,2},{4,5},{5,4},{6,7},{7,6},{8,9},{9,8},{10,11... | collective-permute-start | bytes 3145736 | tf_op jit(solution)/shard_map/ppermute | solution.py:140
  202.0 2.0 copy-start.5
  202.0 2.0 collective-permute-start.1
  223.6 56.8 %all-to-all-start.7 = ((f32[64,32,512]{2,1,0:T(8,128)}), f32[64,32,512]{2,1,0:T(8,128)}, u32[]{:S(2)}, u32[]{:S(2)}) async-start(f32[64,32,512]{2,1,0:T(8,128)} %fusion), calls=%async_computation.7 | async-start | bytes 8388608 | tf_op jit(solution)/shard_map/all_to_all | solution.py:145
where the time goes:
time: 287 us; the launch traced here: 284 us
  waiting for transfers between devices  112 us (39%)
  local copies, waits for them, and re-layouts  50.5 us (18%)
  starting transfers between devices  45.6 us (16%)
  blocking collectives  35.2 us (12%)
  Pallas kernels  20.9 us (7%)
  other arithmetic  15.4 us (5%)
  matrix products  3.24 us (1%)
    all_to_all x1, waiting for transfers between devices, local(): lax.all_to_all(partial, CHIP, 0, 0, tiled=True).sum(0) * grad_scale  39.7 us
    all_to_all x1, blocking collectives, local(): lax.all_to_all(pack_rows(grad_attn), DP, split_axis=1, concat_axis=1, til...  35.2 us
    all_to_all x1, waiting for transfers between devices, local(): lax.all_to_all(pack_rows(queries), DP, split_axis=1, concat_axis=1, tiled...  21.6 us
    pallas_call x1, Pallas kernels, attend_rows(): pl.pallas_call(attend_kernel, grid=(HK,), in_specs=[pl.BlockSpec((row_cou...  20.9 us
    all_to_all x1, waiting for transfers between devices, local(): lax.all_to_all(unflatten(grad_q_rows), DP, split_axis=1, concat_axis=1, t...  16.3 us
    gather x4, local copies, waits for them, and re-layouts, pack_rows(): table[pick_rows]  11.6 us
    all_to_all x1, starting transfers between devices, local(): lax.all_to_all(pack_rows(values), DP, split_axis=1, concat_axis=1, tiled=...  11.2 us
    all_to_all x1, waiting for transfers between devices, local(): lax.all_to_all(unflatten(grad_k_rows), DP, split_axis=1, concat_axis=1, t...  11.1 us
  transfers between devices with their start and end apart: 9, of which 7 were waited for; matrix products, arithmetic and copies ran while one was open for 19% of the time, Pallas kernels for 0%

commit v1 on v0

v1 whole, which is shorter than its diff:
```python
import math

import jax
import jax.numpy as jnp
from jax import lax
from jax.sharding import Mesh, PartitionSpec as P
import numpy as np
from jax.experimental import pallas as pl
from jax.experimental.pallas import tpu as pltpu

HQ = 16
HK = 4
DH = 128
INTERPRET = False


NT = (((1,), (1,)), ((), ()))
TN = (((0,), (0,)), ((), ()))


def attend_kernel(seg_col_ref, seg_row_ref, key_col_ref, key_row_ref, rows_ref, out_ref):
    row_count = rows_ref.shape[0]
    group_size = HQ // HK
    q_w = group_size * DH
    score_scale = 1.0 / math.sqrt(DH)
    seg_col = seg_col_ref[...]
    live_rows = seg_col >= 0
    allowed = (
        (seg_col == seg_row_ref[...]) & (key_row_ref[...] <= key_col_ref[...]) & live_rows
    )
    k_group = rows_ref[:, q_w : q_w + DH]
    v_group = rows_ref[:, q_w + DH : q_w + 2 * DH]
    o_base = q_w + 2 * DH
    dk_acc = jnp.zeros((row_count, DH), jnp.float32)
    dv_acc = jnp.zeros((row_count, DH), jnp.float32)
    for head in range(group_size):
        q_head = rows_ref[:, head * DH : (head + 1) * DH]
        o_head = rows_ref[:, o_base + head * DH : o_base + (head + 1) * DH]
        scores = lax.dot_general(q_head, k_group, NT, preferred_element_type=jnp.float32)
        scores = jnp.where(allowed, scores * score_scale, jnp.float32(-1000000000.0))
        row_max = jnp.max(scores, axis=1, keepdims=True)
        weights = jnp.exp(scores - row_max)
        attn_probs = weights / jnp.sum(weights, axis=1, keepdims=True)
        attn_probs = jnp.where(live_rows, attn_probs, jnp.float32(0.0))
        probs_b = attn_probs.astype(jnp.bfloat16)
        dv_acc = dv_acc + lax.dot_general(probs_b, o_head, TN, preferred_element_type=jnp.float32)
        dprob = lax.dot_general(o_head, v_group, NT, preferred_element_type=jnp.float32)
        row_delta = jnp.sum(attn_probs * dprob, axis=1, keepdims=True)
        dscore = (attn_probs * (dprob - row_delta) * score_scale).astype(jnp.bfloat16)
        out_ref[:, head * DH : (head + 1) * DH] = jnp.dot(
            dscore, k_group, preferred_element_type=jnp.float32
        ).astype(out_ref.dtype)
        dk_acc = dk_acc + lax.dot_general(dscore, q_head, TN, preferred_element_type=jnp.float32)
    out_ref[:, q_w : q_w + DH] = dk_acc.astype(out_ref.dtype)
    out_ref[:, q_w + DH : q_w + 2 * DH] = dv_acc.astype(out_ref.dtype)


def attend_rows(rows_in, segment, order_key):
    row_count = rows_in.shape[0]
    q_w = (HQ // HK) * DH
    in_w, out_w = 2 * q_w + 2 * DH, q_w + 2 * DH
    whole = lambda g: (0, 0)
    col = pl.BlockSpec((row_count, 1), whole)
    row = pl.BlockSpec((1, row_count), whole)
    return pl.pallas_call(
        attend_kernel,
        grid=(HK,),
        in_specs=[col, row, col, row, pl.BlockSpec((row_count, in_w), lambda g: (0, g))],
        out_specs=pl.BlockSpec((row_count, out_w), lambda g: (0, g)),
        out_shape=jax.ShapeDtypeStruct((row_count, HK * out_w), jnp.bfloat16),
        compiler_params=pltpu.CompilerParams(dimension_semantics=("arbitrary",)),
        interpret=INTERPRET,
    )(
        segment.reshape(row_count, 1),
        segment.reshape(1, row_count),
        order_key.reshape(row_count, 1),
        order_key.reshape(1, row_count),
        rows_in,
    )


CHIP, CORE = "chip", "core"
DP = (CHIP, CORE)


def local(hidden_in, queries, keys, values, grad_attn, send_rows, slot_docs):
    chips, cores = lax.axis_size(CHIP), lax.axis_size(CORE)
    owners = chips * cores
    slot_count = send_rows.shape[0]
    tok_rows = queries.shape[0]
    group_size = HQ // HK
    q_w = group_size * DH
    live_send = (send_rows >= 0).T
    pick_rows = jnp.maximum(send_rows, 0).T
    grad_scale = 1.0 / math.sqrt(tok_rows * owners)
    pieces = []
    for head_kv in range(HK):
        pieces += [
            queries[:, head_kv * q_w : (head_kv + 1) * q_w],
            keys[:, head_kv * DH : (head_kv + 1) * DH],
            values[:, head_kv * DH : (head_kv + 1) * DH],
            grad_attn[:, head_kv * q_w : (head_kv + 1) * q_w],
        ]
    table = jnp.concatenate(pieces, axis=1)
    rows_in = lax.all_to_all(table[pick_rows], DP, 0, 0, tiled=True)
    rows_in = rows_in.reshape(owners * slot_count, table.shape[1])
    row_ids = jnp.arange(owners * slot_count, dtype=jnp.int32)
    order_key = (row_ids % slot_count) * owners + row_ids // slot_count
    segment = jnp.tile(slot_docs[0].astype(jnp.int32), owners)
    rows_out = attend_rows(rows_in, segment, order_key)
    back = lax.all_to_all(
        rows_out.reshape(owners, slot_count, rows_out.shape[1]), DP, 0, 0, tiled=True
    )
    targets = jnp.where(live_send, pick_rows, tok_rows).reshape(-1)
    home = (
        jnp.zeros((tok_rows, back.shape[2]), back.dtype)
        .at[targets]
        .set(back.reshape(owners * slot_count, back.shape[2]), mode="drop")
    )
    out_w = q_w + 2 * DH
    grad_queries = jnp.concatenate(
        [home[:, g * out_w : g * out_w + q_w] for g in range(HK)], axis=1
    )
    grad_keys = jnp.concatenate(
        [home[:, g * out_w + q_w : g * out_w + q_w + DH] for g in range(HK)], axis=1
    )
    grad_values = jnp.concatenate(
        [home[:, g * out_w + q_w + DH : (g + 1) * out_w] for g in range(HK)], axis=1
    )
    core = lax.axis_index(CORE)
    swap = [(0, 1), (1, 0)]
    blocks = hidden_in.reshape(tok_rows, chips, cores, -1)
    mine = lax.dynamic_index_in_dim(blocks, core, axis=2, keepdims=False)
    theirs = lax.dynamic_index_in_dim(blocks, 1 - core, axis=2, keepdims=False)
    from_partner = lax.ppermute(theirs, CORE, swap)
    hidden_pair = jnp.concatenate((mine, from_partner), axis=0).reshape(2 * tok_rows, -1)
    grad_pair = jnp.concatenate((grad_values, lax.ppermute(grad_values, CORE, swap)), axis=0)
    partial = jnp.einsum("td,tc->dc", hidden_pair, grad_pair, preferred_element_type=jnp.float32)
    partial = partial.reshape(chips, partial.shape[0] // chips, partial.shape[1])
    grad_wv = lax.all_to_all(partial, CHIP, 0, 0, tiled=True).sum(0) * grad_scale
    return (grad_queries, grad_keys, grad_values, grad_wv)


def solution(mesh):
    devices = np.asarray(mesh.devices).reshape(-1)
    pair_mesh = Mesh(devices.reshape(-1, 2), DP)
    rows = P(DP, None)
    placed = (rows, rows, rows, rows, rows, P(), rows)
    return jax.shard_map(
        local,
        mesh=pair_mesh,
        in_specs=placed,
        out_specs=(rows, rows, rows, rows),
        check_vma=False,
    )
```

time: 287 us -> 269 us (0.937)
  waiting for transfers between devices: 112 us -> 150 us
  blocking collectives: 35.2 us -> 0 us
  starting transfers between devices: 45.6 us -> 24.6 us
  other arithmetic: 15.4 us -> 8.68 us
  local copies, waits for them, and re-layouts: 50.5 us -> 55.3 us
    all_to_all x1 -> x0, blocking collectives: 35.2 us -> none  [local(): lax.all_to_all(pack_rows(grad_attn), DP, split_axis=1, concat_axis=1, til...]
    all_to_all x6 -> x2, waiting for transfers between devices: 72.1 us -> 95.6 us  [the longest x1 61.3 us: local(): rows_in = lax.all_to_all(table[pick_rows], DP, 0, 0, tiled=True)]
    all_to_all x6 -> x2, starting transfers between devices: 39.3 us -> 18.8 us  [the longest x1 11.6 us: local(): rows_in = lax.all_to_all(table[pick_rows], DP, 0, 0, tiled=True)]
    all_to_all x7 -> x0, local copies, waits for them, and re-layouts: 15.4 us -> none  [the longest x1 4.05 us: local(): lax.all_to_all(pack_rows(grad_attn), DP, split_axis=1, concat_axis=1, til...]
    all_to_all x1, waiting for transfers between devices: 39.7 us -> 53.8 us  [local(): lax.all_to_all(partial, CHIP, 0, 0, tiled=True).sum(0) * grad_scale]
    reshape x3 -> x4, local copies, waits for them, and re-layouts: 7.61 us -> 17.6 us  [the longest x1 8.91 us: local(): rows_in = rows_in.reshape(owners * slot_count, table.shape[1])]
    select_n x3 -> x2, other arithmetic: 9.38 us -> 0.98 us  [the longest x1 0.84 us: local(): rows_in = lax.all_to_all(table[pick_rows], DP, 0, 0, tiled=True)]
    unnamed x17 -> x30, local copies, waits for them, and re-layouts: 3.32 us -> 11.6 us
  transfers between devices with their start and end apart: 9 -> 5, of which waited for: 7 -> 4; matrix products, arithmetic and copies ran while one was open for 19% -> 9% of each run, Pallas kernels for 0% -> 0%
where the time goes in v1:
time: 269 us; the launch traced here: 265 us
  waiting for transfers between devices  150 us (56%)
  local copies, waits for them, and re-layouts  55.3 us (21%)
  starting transfers between devices  24.6 us (9%)
  Pallas kernels  22.3 us (8%)
  other arithmetic  8.68 us (3%)
  matrix products  3.28 us (1%)
    all_to_all x1, waiting for transfers between devices, local(): rows_in = lax.all_to_all(table[pick_rows], DP, 0, 0, tiled=True)  61.3 us
    all_to_all x1, waiting for transfers between devices, local(): lax.all_to_all(partial, CHIP, 0, 0, tiled=True).sum(0) * grad_scale  53.8 us
    all_to_all x1, waiting for transfers between devices, local(): lax.all_to_all(rows_out.reshape(owners, slot_count, rows_out.shape[1]), D...  34.3 us
    pallas_call x1, Pallas kernels, attend_rows(): pl.pallas_call(attend_kernel, grid=(HK,), in_specs=[col, row, col, row, p...  22.3 us
    gather x2, local copies, waits for them, and re-layouts, local(): rows_in = lax.all_to_all(table[pick_rows], DP, 0, 0, tiled=True)  14.4 us
    all_to_all x1, starting transfers between devices, local(): rows_in = lax.all_to_all(table[pick_rows], DP, 0, 0, tiled=True)  11.6 us
    unnamed x30, local copies, waits for them, and re-layouts  11.6 us
    reshape x1, local copies, waits for them, and re-layouts, local(): rows_in = rows_in.reshape(owners * slot_count, table.shape[1])  8.91 us
  transfers between devices with their start and end apart: 5, of which 4 were waited for; matrix products, arithmetic and copies ran while one was open for 9% of the time, Pallas kernels for 0%

profile of v1, /device:TPU:0, one launch (start us, length us, event | category | flops | bytes accessed | tf_op | source)
XLA Modules:
  0.0 264.7 jit_solution(7157844350305631006)
XLA Ops:
  0.6 0.0 copy-start.1
  0.6 0.0 copy-start.3
  0.7 0.0 copy-start.4
  0.7 0.0 copy-start.2
  0.7 0.8 compare_select_fusion.1
  1.5 1.0 slice_dynamic-update-slice_fusion.7
  2.5 0.9 slice_dynamic-update-slice_fusion.15
  3.4 0.9 slice_dynamic-update-slice_fusion.14
  4.2 1.0 slice_dynamic-update-slice_fusion.6
  5.2 1.0 slice_dynamic-update-slice_fusion.5
  6.2 0.9 slice_dynamic-update-slice_fusion.13
  7.0 0.9 slice_dynamic-update-slice_fusion.12
  7.9 1.0 slice_dynamic-update-slice_fusion.4
  8.9 0.0 copy-done.1
  8.9 0.0 copy-done.3
  9.0 0.0 copy-done.4
  9.0 0.0 copy-done.2
  9.2 0.1 copy.17
  9.3 0.1 reshape.176
  9.4 5.1 %gather_fusion = bf16[512,5120]{1,0:T(8,128)(2,1)} fusion(bf16[256,5120]{1,0:T(8,128)(2,1)S(1)} %slice_dynamic-update-slice_fusion, s32[1024]{0:T(1024)S(1)} %pad_clamp_fusion), kind=kCustom, calls=%fused_computation | custom fusion | bytes 10487808 | tf_op jit(solution)/shard_map/gather | solution.py:105
  14.5 9.3 %reshape.175 = bf16[128,4,5120]{2,1,0:T(4,128)(2,1)} reshape(bf16[512,5120]{1,0:T(8,128)(2,1)} %gather_fusion) | data formatting | bytes 10485760 | tf_op jit(solution)/shard_map/gather | solution.py:105
  23.8 0.0 copy-start.6
  23.8 11.6 %all-to-all-start = ((bf16[128,4,5120]{2,1,0:T(4,128)(2,1)}), bf16[128,4,5120]{2,1,0:T(4,128)(2,1)}, u32[]{:S(2)}, u32[]{:S(2)}) async-start(bf16[128,4,5120]{2,1,0:T(4,128)(2,1)} %reshape.175), calls=%async_computation | async-start | bytes 10485760 | tf_op jit(solution)/shard_map/all_to_all | solution.py:105
  35.5 0.0 copy-done.6
  35.5 0.8 reshape_tile.8.seg_col_ref
  36.3 0.7 reshape_tile.7.seg_row_ref
  37.0 0.6 fusion.22.key_row_ref
  37.6 0.8 fusion.17.key_col_ref
  38.3 61.3 %all-to-all-done = bf16[128,4,5120]{2,1,0:T(4,128)(2,1)} async-done(((bf16[128,4,5120]{2,1,0:T(4,128)(2,1)}), bf16[128,4,5120]{2,1,0:T(4,128)(2,1)}, u32[]{:S(2)}, u32[]{:S(2)}) %all-to-all-start) | async-done | bytes 5242912 | tf_op jit(solution)/shard_map/all_to_all | solution.py:105
  99.7 8.9 %reshape.170.rows_ref = bf16[512,5120]{1,0:T(8,128)(2,1)} reshape(bf16[128,4,5120]{2,1,0:T(4,128)(2,1)} %all-to-all-done) | data formatting | bytes 10485760 | tf_op jit(solution)/shard_map/reshape | solution.py:106
  108.6 22.3 %shard_map.102 = bf16[512,3072]{1,0:T(8,128)(2,1)} custom-call(s32[512,1]{1,0:T(8,128)} %reshape_tile.8.seg_col_ref, s32[1,512]{1,0:T(1,128)} %reshape_tile.7.seg_row_ref, s32[512,1]{1,0:T(8,128)} %fusion.17.key_col_ref, s32[1,512]{1,0:T(1,128)} %fusion.22.key_row_ref, bf16[512,5120]{1,0:T(8,128)(2,1)} %reshape.170.rows_ref), custom_call_target="tpu_custom_call" | custom-call | tf_op jit(solution)/shard_map/pallas_call | solution.py:65
  130.9 6.1 %reshape.171 = bf16[128,4,3072]{2,1,0:T(4,128)(2,1)} reshape(bf16[512,3072]{1,0:T(8,128)(2,1)} %shard_map.102) | data formatting | bytes 6291456 | tf_op jit(solution)/shard_map/reshape | solution.py:112
  137.1 7.2 %all-to-all-start.1 = ((bf16[128,4,3072]{2,1,0:T(4,128)(2,1)}), bf16[128,4,3072]{2,1,0:T(4,128)(2,1)S(1)}, u32[]{:S(2)}, u32[]{:S(2)}) async-start(bf16[128,4,3072]{2,1,0:T(4,128)(2,1)} %reshape.171), calls=%async_computation.1 | async-start | bytes 6291456 | tf_op jit(solution)/shard_map/all_to_all | solution.py:111
  144.3 4.1 %copy.19 = bf16[256,4096]{0,1:T(8,128)(2,1)} copy(bf16[256,4096]{1,0:T(8,128)(2,1)} %param.7) | data formatting | bytes 4194304 | tf_op args[0]
  148.4 3.1 %constant_dynamic-slice_fusion = (bf16[256,64,1,32]{0,3,2,1:T(8,128)(2,1)}, bf16[256,64,32]{0,2,1:T(8,128)(2,1)}) fusion(bf16[256,64,2,32]{0,3,2,1:T(8,128)(2,1)} %bitcast.18, s32[]{:T(128)S(6)} %select_n.75, s32[]{:T(128)S(6)} %select_n.76), kind=kLoop, calls=%fused_computation.61 | loop fusion | bytes 4194312 | tf_op jit(solution)/shard_map/jit(dynamic_index_in_dim)/dynamic_slice | solution.py:133
  151.4 0.0 collective-permute-start
  151.4 0.1 copy.13
  151.6 0.1 reshape.193
  151.7 0.1 fusion.20
  151.8 34.3 %all-to-all-done.1 = bf16[128,4,3072]{2,1,0:T(4,128)(2,1)S(1)} async-done(((bf16[128,4,3072]{2,1,0:T(4,128)(2,1)}), bf16[128,4,3072]{2,1,0:T(4,128)(2,1)S(1)}, u32[]{:S(2)}, u32[]{:S(2)}) %all-to-all-start.1) | async-done | bytes 3145760 | tf_op jit(solution)/shard_map/all_to_all | solution.py:111
  186.1 2.4 reshape.186
  188.5 0.0 copy-start
  188.5 6.6 %scatter_custom_fusion = bf16[256,3072]{1,0:T(8,128)(2,1)S(1)} fusion(s32[512]{0:T(512)S(1)} %fusion.20, bf16[512,3072]{1,0:T(8,128)(2,1)} %reshape.186, bf16[]{:T(256)} %constant.51.clone.1), kind=kCustom, calls=%fused_computation.5 | custom fusion | bytes 1573376 | tf_op jit(solution)/shard_map/scatter | solution.py:118
  195.1 0.1 fusion.24
  195.2 0.0 copy-start.5
  195.3 0.1 collective-permute-start.1
  195.4 0.0 collective-permute-done
  195.4 0.0 copy-done
  195.4 1.4 pad_maximum_fusion
  196.8 0.1 collective-permute-done.1
  196.9 3.3 %fusion.2 = f32[64,32,512]{2,1,0:T(8,128)} fusion(bf16[64,32,512]{2,1,0:T(8,128)(2,1)S(1)} %bitcast.19, bf16[256,512]{1,0:T(8,128)(2,1)S(1)} %collective-permute-done.1, bf16[256,128]{1,0:T(8,128)(2,1)S(1)} %get-tuple-element.7, bf16[256,128]{1,0:T(8,128)(2,1)S(1)} %get-tuple-element.8, bf16[256,128]{1,0:T(8,128)(2,1)S(1)} %get-tuple-element.9, ...), kind=kOutput, calls=%fused_computation.9 | convolution fusion | flops 1076363264 | bytes 6815744 | tf_op jit(solution)/shard_map/td,tc->dc/dot_general | solution.py:138
  200.2 0.0 copy-done.5
  200.2 5.7 %all-to-all-start.2 = ((f32[64,32,512]{2,1,0:T(8,128)}), f32[64,32,512]{2,1,0:T(8,128)}, u32[]{:S(2)}, u32[]{:S(2)}) async-start(f32[64,32,512]{2,1,0:T(8,128)} %fusion.2), calls=%async_computation.2 | async-start | bytes 8388608 | tf_op jit(solution)/shard_map/all_to_all | solution.py:140
  205.8 0.7 pad_maximum_fusion.2
  206.6 0.1 fusion.25
  206.7 1.1 pad_maximum_fusion.1
  207.7 53.8 %all-to-all-done.2 = f32[64,32,512]{2,1,0:T(8,128)} async-done(((f32[64,32,512]{2,1,0:T(8,128)}), f32[64,32,512]{2,1,0:T(8,128)}, u32[]{:S(2)}, u32[]{:S(2)}) %all-to-all-start.2) | async-done | bytes 4194336 | tf_op jit(solution)/shard_map/all_to_all | solution.py:140
  261.6 2.5 reduce_sum.9
  264.1 0.6 broadcast_multiply_fusion
  (11 shorter events, 0.2 us)
Async XLA Ops:
  0.6 8.3 %copy-start.1 = (bf16[256,2048]{1,0:T(8,128)(2,1)S(1)}, bf16[256,2048]{1,0:T(8,128)(2,1)}, u32[]{:S(2)}) copy-start(bf16[256,2048]{1,0:T(8,128)(2,1)} %param.8) | copy-start | bytes 3145732
  0.6 8.3 %copy-start.3 = (bf16[256,512]{1,0:T(8,128)(2,1)S(1)}, bf16[256,512]{1,0:T(8,128)(2,1)}, u32[]{:S(2)}) copy-start(bf16[256,512]{1,0:T(8,128)(2,1)} %param.9) | copy-start | bytes 786436
  0.7 8.3 %copy-start.4 = (bf16[256,512]{1,0:T(8,128)(2,1)S(1)}, bf16[256,512]{1,0:T(8,128)(2,1)}, u32[]{:S(2)}) copy-start(bf16[256,512]{1,0:T(8,128)(2,1)} %param.10) | copy-start | bytes 786436
  0.7 8.3 %copy-start.2 = (bf16[256,2048]{1,0:T(8,128)(2,1)S(1)}, bf16[256,2048]{1,0:T(8,128)(2,1)}, u32[]{:S(2)}) copy-start(bf16[256,2048]{1,0:T(8,128)(2,1)} %param.11) | copy-start | bytes 3145732
  23.8 11.7 %copy-start.6 = (s32[1,4]{1,0:T(1,128)S(1)}, s32[1,4]{1,0:T(1,128)}, u32[]{:S(2)}) copy-start(s32[1,4]{1,0:T(1,128)} %param.13) | copy-start | bytes 52
  23.8 75.9 %all-to-all-start = ((bf16[128,4,5120]{2,1,0:T(4,128)(2,1)}), bf16[128,4,5120]{2,1,0:T(4,128)(2,1)}, u32[]{:S(2)}, u32[]{:S(2)}) async-start(bf16[128,4,5120]{2,1,0:T(4,128)(2,1)} %reshape.175), calls=%async_computation | async-start | bytes 10485760 | tf_op jit(solution)/shard_map/all_to_all | solution.py:105
  137.1 49.0 %all-to-all-start.1 = ((bf16[128,4,3072]{2,1,0:T(4,128)(2,1)}), bf16[128,4,3072]{2,1,0:T(4,128)(2,1)S(1)}, u32[]{:S(2)}, u32[]{:S(2)}) async-start(bf16[128,4,3072]{2,1,0:T(4,128)(2,1)} %reshape.171), calls=%async_computation.1 | async-start | bytes 6291456 | tf_op jit(solution)/shard_map/all_to_all | solution.py:111
  151.4 43.9 %collective-permute-start = (bf16[256,64,32]{0,2,1:T(8,128)(2,1)}, bf16[256,64,32]{0,2,1:T(8,128)(2,1)}, u32[]{:S(2)}, u32[]{:S(2)}) collective-permute-start(bf16[256,64,32]{0,2,1:T(8,128)(2,1)} %get-tuple-element.5), channel_id=1, source_target_pairs={{0,1},{1,0},{2,3},{3,2},{4,5},{5,4},{6,7},{7,6},{8,9},{9,8},{10,11... | collective-permute-start | bytes 3145736 | tf_op jit(solution)/shard_map/ppermute | solution.py:135
  188.5 6.9 %copy-start = (bf16[256,64,1,32]{0,3,2,1:T(8,128)(2,1)S(1)}, bf16[256,64,1,32]{0,3,2,1:T(8,128)(2,1)}, u32[]{:S(2)}) copy-start(bf16[256,64,1,32]{0,3,2,1:T(8,128)(2,1)} %get-tuple-element.4) | copy-start | bytes 3145732
  195.2 4.9 %copy-start.5 = (bf16[256,512]{1,0:T(8,128)(2,1)}, bf16[256,512]{1,0:T(8,128)(2,1)S(1)}, u32[]{:S(2)}) copy-start(bf16[256,512]{1,0:T(8,128)(2,1)S(1)} %pad_maximum_fusion.3) | copy-start | bytes 786436
  195.3 1.6 collective-permute-start.1
  200.2 61.4 %all-to-all-start.2 = ((f32[64,32,512]{2,1,0:T(8,128)}), f32[64,32,512]{2,1,0:T(8,128)}, u32[]{:S(2)}, u32[]{:S(2)}) async-start(f32[64,32,512]{2,1,0:T(8,128)} %fusion.2), calls=%async_computation.2 | async-start | bytes 8388608 | tf_op jit(solution)/shard_map/all_to_all | solution.py:140

commit v2 on v1

--- a/solution.py
+++ b/solution.py
@@ -18,8 +18,10 @@
 TN = (((0,), (0,)), ((), ()))
 
 
-def attend_kernel(seg_col_ref, seg_row_ref, key_col_ref, key_row_ref, rows_ref, out_ref):
-    row_count = rows_ref.shape[0]
+def attend_kernel(
+    seg_col_ref, seg_row_ref, key_col_ref, key_row_ref, q_ref, k_ref, v_ref, o_ref, out_ref
+):
+    row_count = q_ref.shape[0]
     group_size = HQ // HK
     q_w = group_size * DH
     score_scale = 1.0 / math.sqrt(DH)
@@ -28,19 +30,18 @@
     allowed = (
         (seg_col == seg_row_ref[...]) & (key_row_ref[...] <= key_col_ref[...]) & live_rows
     )
-    k_group = rows_ref[:, q_w : q_w + DH]
-    v_group = rows_ref[:, q_w + DH : q_w + 2 * DH]
-    o_base = q_w + 2 * DH
+    k_group = k_ref[...]
+    v_group = v_ref[...]
     dk_acc = jnp.zeros((row_count, DH), jnp.float32)
     dv_acc = jnp.zeros((row_count, DH), jnp.float32)
     for head in range(group_size):
-        q_head = rows_ref[:, head * DH : (head + 1) * DH]
-        o_head = rows_ref[:, o_base + head * DH : o_base + (head + 1) * DH]
+        q_head = q_ref[:, head * DH : (head + 1) * DH]
+        o_head = o_ref[:, head * DH : (head + 1) * DH]
         scores = lax.dot_general(q_head, k_group, NT, preferred_element_type=jnp.float32)
         scores = jnp.where(allowed, scores * score_scale, jnp.float32(-1000000000.0))
         row_max = jnp.max(scores, axis=1, keepdims=True)
         weights = jnp.exp(scores - row_max)
-        attn_probs = weights / jnp.sum(weights, axis=1, keepdims=True)
+        attn_probs = weights * (1.0 / jnp.sum(weights, axis=1, keepdims=True))
         attn_probs = jnp.where(live_rows, attn_probs, jnp.float32(0.0))
         probs_b = attn_probs.astype(jnp.bfloat16)
         dv_acc = dv_acc + lax.dot_general(probs_b, o_head, TN, preferred_element_type=jnp.float32)
@@ -58,14 +59,24 @@
 def attend_rows(rows_in, segment, order_key):
     row_count = rows_in.shape[0]
     q_w = (HQ // HK) * DH
-    in_w, out_w = 2 * q_w + 2 * DH, q_w + 2 * DH
+    out_w = q_w + 2 * DH
+    k_at, v_at, o_at = HK * q_w // DH, HK * q_w // DH + HK, (HK * q_w + 2 * HK * DH) // q_w
     whole = lambda g: (0, 0)
     col = pl.BlockSpec((row_count, 1), whole)
     row = pl.BlockSpec((1, row_count), whole)
     return pl.pallas_call(
         attend_kernel,
         grid=(HK,),
-        in_specs=[col, row, col, row, pl.BlockSpec((row_count, in_w), lambda g: (0, g))],
+        in_specs=[
+            col,
+            row,
+            col,
+            row,
+            pl.BlockSpec((row_count, q_w), lambda g: (0, g)),
+            pl.BlockSpec((row_count, DH), lambda g: (0, k_at + g)),
+            pl.BlockSpec((row_count, DH), lambda g: (0, v_at + g)),
+            pl.BlockSpec((row_count, q_w), lambda g: (0, o_at + g)),
+        ],
         out_specs=pl.BlockSpec((row_count, out_w), lambda g: (0, g)),
         out_shape=jax.ShapeDtypeStruct((row_count, HK * out_w), jnp.bfloat16),
         compiler_params=pltpu.CompilerParams(dimension_semantics=("arbitrary",)),
@@ -75,6 +86,9 @@
         segment.reshape(1, row_count),
         order_key.reshape(row_count, 1),
         order_key.reshape(1, row_count),
+        rows_in,
+        rows_in,
+        rows_in,
         rows_in,
     )
 
@@ -93,15 +107,7 @@
     live_send = (send_rows >= 0).T
     pick_rows = jnp.maximum(send_rows, 0).T
     grad_scale = 1.0 / math.sqrt(tok_rows * owners)
-    pieces = []
-    for head_kv in range(HK):
-        pieces += [
-            queries[:, head_kv * q_w : (head_kv + 1) * q_w],
-            keys[:, head_kv * DH : (head_kv + 1) * DH],
-            values[:, head_kv * DH : (head_kv + 1) * DH],
-            grad_attn[:, head_kv * q_w : (head_kv + 1) * q_w],
-        ]
-    table = jnp.concatenate(pieces, axis=1)
+    table = jnp.concatenate((queries, keys, values, grad_attn), axis=1)
     rows_in = lax.all_to_all(table[pick_rows], DP, 0, 0, tiled=True)
     rows_in = rows_in.reshape(owners * slot_count, table.shape[1])
     row_ids = jnp.arange(owners * slot_count, dtype=jnp.int32)

time: 269 us -> 262 us (0.974)
  local copies, waits for them, and re-layouts: 55.3 us -> 47.7 us
    unnamed x30 -> x7, local copies, waits for them, and re-layouts: 11.6 us -> 4.09 us
where the time goes in v2:
time: 262 us; the launch traced here: 259 us
  waiting for transfers between devices  150 us (57%)
  local copies, waits for them, and re-layouts  47.7 us (18%)
  starting transfers between devices  24.6 us (9%)
  Pallas kernels  22.5 us (9%)
  other arithmetic  10.4 us (4%)
  matrix products  3.3 us (1%)
    all_to_all x1, waiting for transfers between devices, local(): rows_in = lax.all_to_all(table[pick_rows], DP, 0, 0, tiled=True)  61.3 us
    all_to_all x1, waiting for transfers between devices, local(): lax.all_to_all(partial, CHIP, 0, 0, tiled=True).sum(0) * grad_scale  53.8 us
    all_to_all x1, waiting for transfers between devices, local(): lax.all_to_all(rows_out.reshape(owners, slot_count, rows_out.shape[1]), D...  34.3 us
    pallas_call x1, Pallas kernels, attend_rows(): pl.pallas_call(attend_kernel, grid=(HK,), in_specs=[col, row, col, row, p...  22.5 us
    gather x2, local copies, waits for them, and re-layouts, local(): rows_in = lax.all_to_all(table[pick_rows], DP, 0, 0, tiled=True)  14.4 us
    all_to_all x1, starting transfers between devices, local(): rows_in = lax.all_to_all(table[pick_rows], DP, 0, 0, tiled=True)  11.6 us
    reshape x1, local copies, waits for them, and re-layouts, local(): rows_in = rows_in.reshape(owners * slot_count, table.shape[1])  8.91 us
    all_to_all x1, starting transfers between devices, local(): lax.all_to_all(rows_out.reshape(owners, slot_count, rows_out.shape[1]), D...  7.22 us
  transfers between devices with their start and end apart: 5, of which 4 were waited for; matrix products, arithmetic and copies ran while one was open for 9% of the time, Pallas kernels for 0%

profile of v2, /device:TPU:0, one launch (start us, length us, event | category | flops | bytes accessed | tf_op | source)
XLA Modules:
  0.0 258.8 jit_solution(15442406168437071381)
XLA Ops:
  0.6 0.7 compare_select_fusion.1
  1.3 0.1 copy.17
  1.4 0.1 reshape.176
  1.6 1.8 pad_maximum_fusion
  3.4 5.1 %gather_fusion = bf16[512,5120]{1,0:T(8,128)(2,1)} fusion(bf16[256,5120]{1,0:T(8,128)(2,1)S(1)} %pad_maximum_fusion, s32[1024]{0:T(1024)S(1)} %pad_clamp_fusion), kind=kCustom, calls=%fused_computation | custom fusion | bytes 10487808 | tf_op jit(solution)/shard_map/gather | solution.py:111
  8.5 9.3 %reshape.175 = bf16[128,4,5120]{2,1,0:T(4,128)(2,1)} reshape(bf16[512,5120]{1,0:T(8,128)(2,1)} %gather_fusion) | data formatting | bytes 10485760 | tf_op jit(solution)/shard_map/gather | solution.py:111
  17.8 0.0 copy-start.2
  17.8 11.6 %all-to-all-start = ((bf16[128,4,5120]{2,1,0:T(4,128)(2,1)}), bf16[128,4,5120]{2,1,0:T(4,128)(2,1)}, u32[]{:S(2)}, u32[]{:S(2)}) async-start(bf16[128,4,5120]{2,1,0:T(4,128)(2,1)} %reshape.175), calls=%async_computation | async-start | bytes 10485760 | tf_op jit(solution)/shard_map/all_to_all | solution.py:111
  29.4 0.0 copy-done.2
  29.5 0.8 reshape_tile.8.seg_col_ref
  30.3 0.7 reshape_tile.7.seg_row_ref
  31.0 0.6 fusion.22.key_row_ref
  31.6 0.8 fusion.17.key_col_ref
  32.3 61.3 %all-to-all-done = bf16[128,4,5120]{2,1,0:T(4,128)(2,1)} async-done(((bf16[128,4,5120]{2,1,0:T(4,128)(2,1)}), bf16[128,4,5120]{2,1,0:T(4,128)(2,1)}, u32[]{:S(2)}, u32[]{:S(2)}) %all-to-all-start) | async-done | bytes 5242912 | tf_op jit(solution)/shard_map/all_to_all | solution.py:111
  93.7 8.9 %reshape.170.q_ref.k_ref.v_ref.o_ref = bf16[512,5120]{1,0:T(8,128)(2,1)} reshape(bf16[128,4,5120]{2,1,0:T(4,128)(2,1)} %all-to-all-done) | data formatting | bytes 10485760 | tf_op jit(solution)/shard_map/reshape | solution.py:112
  102.6 22.5 %shard_map.102 = bf16[512,3072]{1,0:T(8,128)(2,1)} custom-call(s32[512,1]{1,0:T(8,128)} %reshape_tile.8.seg_col_ref, s32[1,512]{1,0:T(1,128)} %reshape_tile.7.seg_row_ref, s32[512,1]{1,0:T(8,128)} %fusion.17.key_col_ref, s32[1,512]{1,0:T(1,128)} %fusion.22.key_row_ref, bf16[512,5120]{1,0:T(8,128)(2,1)} %reshape.170.q_ref.k_ref.v_ref.o_ref, ...), custom_call_target="tpu_custom_call" | custom-call | tf_op jit(solution)/shard_map/pallas_call | solution.py:67
  125.0 6.1 %reshape.171 = bf16[128,4,3072]{2,1,0:T(4,128)(2,1)} reshape(bf16[512,3072]{1,0:T(8,128)(2,1)} %shard_map.102) | data formatting | bytes 6291456 | tf_op jit(solution)/shard_map/reshape | solution.py:118
  131.2 7.2 %all-to-all-start.1 = ((bf16[128,4,3072]{2,1,0:T(4,128)(2,1)}), bf16[128,4,3072]{2,1,0:T(4,128)(2,1)S(1)}, u32[]{:S(2)}, u32[]{:S(2)}) async-start(bf16[128,4,3072]{2,1,0:T(4,128)(2,1)} %reshape.171), calls=%async_computation.1 | async-start | bytes 6291456 | tf_op jit(solution)/shard_map/all_to_all | solution.py:117
  138.4 4.1 %copy.19 = bf16[256,4096]{0,1:T(8,128)(2,1)} copy(bf16[256,4096]{1,0:T(8,128)(2,1)} %param.7) | data formatting | bytes 4194304 | tf_op args[0]
  142.5 3.1 %constant_dynamic-slice_fusion = (bf16[256,64,1,32]{0,3,2,1:T(8,128)(2,1)}, bf16[256,64,32]{0,2,1:T(8,128)(2,1)}) fusion(bf16[256,64,2,32]{0,3,2,1:T(8,128)(2,1)} %bitcast.18, s32[]{:T(128)S(6)} %select_n.75, s32[]{:T(128)S(6)} %select_n.76), kind=kLoop, calls=%fused_computation.46 | loop fusion | bytes 4194312 | tf_op jit(solution)/shard_map/jit(dynamic_index_in_dim)/dynamic_slice | solution.py:139
  145.6 0.0 collective-permute-start
  145.6 0.1 copy.13
  145.7 0.1 reshape.193
  145.8 0.1 fusion.20
  145.9 34.3 %all-to-all-done.1 = bf16[128,4,3072]{2,1,0:T(4,128)(2,1)S(1)} async-done(((bf16[128,4,3072]{2,1,0:T(4,128)(2,1)}), bf16[128,4,3072]{2,1,0:T(4,128)(2,1)S(1)}, u32[]{:S(2)}, u32[]{:S(2)}) %all-to-all-start.1) | async-done | bytes 3145760 | tf_op jit(solution)/shard_map/all_to_all | solution.py:117
  180.2 2.4 reshape.186
  182.6 0.0 copy-start
  182.6 6.6 %scatter_custom_fusion = bf16[256,3072]{1,0:T(8,128)(2,1)S(1)} fusion(s32[512]{0:T(512)S(1)} %fusion.20, bf16[512,3072]{1,0:T(8,128)(2,1)} %reshape.186, bf16[]{:T(256)} %constant.51.clone.1), kind=kCustom, calls=%fused_computation.6 | custom fusion | bytes 1573376 | tf_op jit(solution)/shard_map/scatter | solution.py:124
  189.2 0.1 fusion.24
  189.4 0.0 copy-start.1
  189.4 0.1 collective-permute-start.1
  189.5 0.0 collective-permute-done
  189.5 0.0 copy-done
  189.5 1.4 pad_maximum_fusion.1
  190.9 0.1 collective-permute-done.1
  191.0 3.3 %fusion.2 = f32[64,32,512]{2,1,0:T(8,128)} fusion(bf16[64,32,512]{2,1,0:T(8,128)(2,1)S(1)} %bitcast.19, bf16[256,512]{1,0:T(8,128)(2,1)S(1)} %collective-permute-done.1, bf16[256,128]{1,0:T(8,128)(2,1)S(1)} %get-tuple-element.7, bf16[256,128]{1,0:T(8,128)(2,1)S(1)} %get-tuple-element.8, bf16[256,128]{1,0:T(8,128)(2,1)S(1)} %get-tuple-element.9, ...), kind=kOutput, calls=%fused_computation.10 | convolution fusion | flops 1076363264 | bytes 6815744 | tf_op jit(solution)/shard_map/td,tc->dc/dot_general | solution.py:144
  194.3 0.0 copy-done.1
  194.3 5.7 %all-to-all-start.2 = ((f32[64,32,512]{2,1,0:T(8,128)}), f32[64,32,512]{2,1,0:T(8,128)}, u32[]{:S(2)}, u32[]{:S(2)}) async-start(f32[64,32,512]{2,1,0:T(8,128)} %fusion.2), calls=%async_computation.2 | async-start | bytes 8388608 | tf_op jit(solution)/shard_map/all_to_all | solution.py:146
  200.0 0.7 pad_maximum_fusion.3
  200.7 0.1 fusion.25
  200.8 1.1 pad_maximum_fusion.2
  201.9 53.8 %all-to-all-done.2 = f32[64,32,512]{2,1,0:T(8,128)} async-done(((f32[64,32,512]{2,1,0:T(8,128)}), f32[64,32,512]{2,1,0:T(8,128)}, u32[]{:S(2)}, u32[]{:S(2)}) %all-to-all-start.2) | async-done | bytes 4194336 | tf_op jit(solution)/shard_map/all_to_all | solution.py:146
  255.7 2.5 reduce_sum.9
  258.2 0.6 broadcast_multiply_fusion
  (3 shorter events, 0.0 us)
Async XLA Ops:
  17.8 11.7 %copy-start.2 = (s32[1,4]{1,0:T(1,128)S(1)}, s32[1,4]{1,0:T(1,128)}, u32[]{:S(2)}) copy-start(s32[1,4]{1,0:T(1,128)} %param.13) | copy-start | bytes 52
  17.8 75.9 %all-to-all-start = ((bf16[128,4,5120]{2,1,0:T(4,128)(2,1)}), bf16[128,4,5120]{2,1,0:T(4,128)(2,1)}, u32[]{:S(2)}, u32[]{:S(2)}) async-start(bf16[128,4,5120]{2,1,0:T(4,128)(2,1)} %reshape.175), calls=%async_computation | async-start | bytes 10485760 | tf_op jit(solution)/shard_map/all_to_all | solution.py:111
  131.2 49.0 %all-to-all-start.1 = ((bf16[128,4,3072]{2,1,0:T(4,128)(2,1)}), bf16[128,4,3072]{2,1,0:T(4,128)(2,1)S(1)}, u32[]{:S(2)}, u32[]{:S(2)}) async-start(bf16[128,4,3072]{2,1,0:T(4,128)(2,1)} %reshape.171), calls=%async_computation.1 | async-start | bytes 6291456 | tf_op jit(solution)/shard_map/all_to_all | solution.py:117
  145.6 43.9 %collective-permute-start = (bf16[256,64,32]{0,2,1:T(8,128)(2,1)}, bf16[256,64,32]{0,2,1:T(8,128)(2,1)}, u32[]{:S(2)}, u32[]{:S(2)}) collective-permute-start(bf16[256,64,32]{0,2,1:T(8,128)(2,1)} %get-tuple-element.5), channel_id=1, source_target_pairs={{0,1},{1,0},{2,3},{3,2},{4,5},{5,4},{6,7},{7,6},{8,9},{9,8},{10,11... | collective-permute-start | bytes 3145736 | tf_op jit(solution)/shard_map/ppermute | solution.py:141
  182.6 6.9 %copy-start = (bf16[256,64,1,32]{0,3,2,1:T(8,128)(2,1)S(1)}, bf16[256,64,1,32]{0,3,2,1:T(8,128)(2,1)}, u32[]{:S(2)}) copy-start(bf16[256,64,1,32]{0,3,2,1:T(8,128)(2,1)} %get-tuple-element.4) | copy-start | bytes 3145732
  189.4 4.9 %copy-start.1 = (bf16[256,512]{1,0:T(8,128)(2,1)}, bf16[256,512]{1,0:T(8,128)(2,1)S(1)}, u32[]{:S(2)}) copy-start(bf16[256,512]{1,0:T(8,128)(2,1)S(1)} %pad_maximum_fusion.4) | copy-start | bytes 786436
  189.4 1.6 collective-permute-start.1
  194.3 61.4 %all-to-all-start.2 = ((f32[64,32,512]{2,1,0:T(8,128)}), f32[64,32,512]{2,1,0:T(8,128)}, u32[]{:S(2)}, u32[]{:S(2)}) async-start(f32[64,32,512]{2,1,0:T(8,128)} %fusion.2), calls=%async_computation.2 | async-start | bytes 8388608 | tf_op jit(solution)/shard_map/all_to_all | solution.py:146

commit v3 on v2

--- a/solution.py
+++ b/solution.py
@@ -93,13 +93,14 @@
     )
 
 
-CHIP, CORE = "chip", "core"
-DP = (CHIP, CORE)
+OUTER, INNER = "outer", "inner"
+DP = (OUTER, INNER)
+GROUP = 8
 
 
 def local(hidden_in, queries, keys, values, grad_attn, send_rows, slot_docs):
-    chips, cores = lax.axis_size(CHIP), lax.axis_size(CORE)
-    owners = chips * cores
+    outers, groups = lax.axis_size(OUTER), lax.axis_size(INNER)
+    owners = outers * groups
     slot_count = send_rows.shape[0]
     tok_rows = queries.shape[0]
     group_size = HQ // HK
@@ -133,23 +134,30 @@
     grad_values = jnp.concatenate(
         [home[:, g * out_w + q_w + DH : (g + 1) * out_w] for g in range(HK)], axis=1
     )
-    core = lax.axis_index(CORE)
-    swap = [(0, 1), (1, 0)]
-    blocks = hidden_in.reshape(tok_rows, chips, cores, -1)
-    mine = lax.dynamic_index_in_dim(blocks, core, axis=2, keepdims=False)
-    theirs = lax.dynamic_index_in_dim(blocks, 1 - core, axis=2, keepdims=False)
-    from_partner = lax.ppermute(theirs, CORE, swap)
-    hidden_pair = jnp.concatenate((mine, from_partner), axis=0).reshape(2 * tok_rows, -1)
-    grad_pair = jnp.concatenate((grad_values, lax.ppermute(grad_values, CORE, swap)), axis=0)
-    partial = jnp.einsum("td,tc->dc", hidden_pair, grad_pair, preferred_element_type=jnp.float32)
-    partial = partial.reshape(chips, partial.shape[0] // chips, partial.shape[1])
-    grad_wv = lax.all_to_all(partial, CHIP, 0, 0, tiled=True).sum(0) * grad_scale
+    me = lax.axis_index(INNER)
+    shifts = range(1, groups)
+    blocks = hidden_in.reshape(tok_rows, outers, groups, -1)
+    hidden_grp = [lax.dynamic_index_in_dim(blocks, me, axis=2, keepdims=False)]
+    for shift in shifts:
+        ring = [(i, (i + shift) % groups) for i in range(groups)]
+        theirs = lax.dynamic_index_in_dim(blocks, (me + shift) % groups, axis=2, keepdims=False)
+        hidden_grp.append(lax.ppermute(theirs, INNER, ring))
+    grad_grp = [grad_values]
+    for shift in shifts:
+        ring = [(i, (i + shift) % groups) for i in range(groups)]
+        grad_grp.append(lax.ppermute(grad_values, INNER, ring))
+    hidden_grp = jnp.concatenate(hidden_grp, axis=0).reshape(groups * tok_rows, -1)
+    grad_grp = jnp.concatenate(grad_grp, axis=0)
+    partial = jnp.einsum("td,tc->dc", hidden_grp, grad_grp, preferred_element_type=jnp.float32)
+    partial = partial.reshape(outers, partial.shape[0] // outers, partial.shape[1])
+    grad_wv = lax.all_to_all(partial, OUTER, 0, 0, tiled=True).sum(0) * grad_scale
     return (grad_queries, grad_keys, grad_values, grad_wv)
 
 
 def solution(mesh):
     devices = np.asarray(mesh.devices).reshape(-1)
-    pair_mesh = Mesh(devices.reshape(-1, 2), DP)
+    group = GROUP if devices.size % GROUP == 0 else 1
+    pair_mesh = Mesh(devices.reshape(-1, group), DP)
     rows = P(DP, None)
     placed = (rows, rows, rows, rows, rows, P(), rows)
     return jax.shard_map(

time: 262 us -> 271 us (1.034)
  waiting for transfers between devices: 150 us -> 126 us
  starting transfers between devices: 24.6 us -> 47.5 us
  local copies, waits for them, and re-layouts: 47.7 us -> 61.6 us
  other arithmetic: 10.4 us -> 7.53 us
    ppermute x2 -> x14, waiting for transfers between devices: 0.12 us -> 47.4 us  [the longest x7 29.3 us: local(): hidden_grp.append(lax.ppermute(theirs, INNER, ring))]
    all_to_all x1, waiting for transfers between devices: 53.8 us -> 17.2 us  [local(): lax.all_to_all(partial, OUTER, 0, 0, tiled=True).sum(0) * grad_scale]
    all_to_all x1, waiting for transfers between devices: 34.3 us -> 0.01 us  [local(): lax.all_to_all(rows_out.reshape(owners, slot_count, rows_out.shape[1]), D...]
    ppermute x2 -> x14, starting transfers between devices: 0.09 us -> 22.5 us  [the longest x7 12.3 us: local(): hidden_grp.append(lax.ppermute(theirs, INNER, ring))]
    unnamed x7 -> x22, local copies, waits for them, and re-layouts: 4.09 us -> 15.2 us
    dynamic_slice x1 -> x0, local copies, waits for them, and re-layouts: 3.08 us -> none  [local(): mine = lax.dynamic_index_in_dim(blocks, core, axis=2, keepdims=False)]
    squeeze x0 -> x1, local copies, waits for them, and re-layouts: none -> 2.74 us  [local(): lax.dynamic_index_in_dim(blocks, (me + shift) % groups, axis=2, keepdims=...]
  transfers between devices with their start and end apart: 5 -> 17, of which waited for: 4 -> 10; matrix products, arithmetic and copies ran while one was open for 9% -> 13% of each run, Pallas kernels for 0% -> 0%
where the time goes in v3:
time: 271 us; the launch traced here: 270 us
  waiting for transfers between devices  126 us (46%)
  local copies, waits for them, and re-layouts  61.6 us (23%)
  starting transfers between devices  47.5 us (18%)
  Pallas kernels  22.5 us (8%)
  other arithmetic  7.53 us (3%)
  matrix products  3.83 us (1%)
    all_to_all x1, waiting for transfers between devices, local(): rows_in = lax.all_to_all(table[pick_rows], DP, 0, 0, tiled=True)  61.3 us
    ppermute x7, waiting for transfers between devices, local(): hidden_grp.append(lax.ppermute(theirs, INNER, ring))  29.3 us
    pallas_call x1, Pallas kernels, attend_rows(): pl.pallas_call(attend_kernel, grid=(HK,), in_specs=[col, row, col, row, p...  22.5 us
    ppermute x7, waiting for transfers between devices, local(): grad_grp.append(lax.ppermute(grad_values, INNER, ring))  18.2 us
    all_to_all x1, waiting for transfers between devices, local(): lax.all_to_all(partial, OUTER, 0, 0, tiled=True).sum(0) * grad_scale  17.2 us
    unnamed x22, local copies, waits for them, and re-layouts  15.2 us
    gather x2, local copies, waits for them, and re-layouts, local(): rows_in = lax.all_to_all(table[pick_rows], DP, 0, 0, tiled=True)  14.5 us
    ppermute x7, starting transfers between devices, local(): hidden_grp.append(lax.ppermute(theirs, INNER, ring))  12.3 us
  transfers between devices with their start and end apart: 17, of which 10 were waited for; matrix products, arithmetic and copies ran while one was open for 13% of the time, Pallas kernels for 0%

profile of v3, /device:TPU:0, one launch (start us, length us, event | category | flops | bytes accessed | tf_op | source)
XLA Modules:
  0.0 269.8 jit_solution(11103517785243680819)
XLA Ops:
  0.6 0.7 compare_select_fusion.1
  1.3 0.1 copy.17
  1.4 0.1 reshape.182
  1.6 1.8 pad_maximum_fusion
  3.4 5.1 %gather_fusion = bf16[512,5120]{1,0:T(8,128)(2,1)} fusion(bf16[256,5120]{1,0:T(8,128)(2,1)S(1)} %pad_maximum_fusion, s32[1024]{0:T(1024)S(1)} %pad_clamp_fusion), kind=kCustom, calls=%fused_computation | custom fusion | bytes 10487808 | tf_op jit(solution)/shard_map/gather | solution.py:112
  8.5 9.3 %reshape.181 = bf16[128,4,5120]{2,1,0:T(4,128)(2,1)} reshape(bf16[512,5120]{1,0:T(8,128)(2,1)} %gather_fusion) | data formatting | bytes 10485760 | tf_op jit(solution)/shard_map/gather | solution.py:112
  17.9 11.6 %all-to-all-start = ((bf16[128,4,5120]{2,1,0:T(4,128)(2,1)}), bf16[128,4,5120]{2,1,0:T(4,128)(2,1)}, u32[]{:S(2)}, u32[]{:S(2)}) async-start(bf16[128,4,5120]{2,1,0:T(4,128)(2,1)} %reshape.181), calls=%async_computation | async-start | bytes 10485760 | tf_op jit(solution)/shard_map/all_to_all | solution.py:112
  29.5 0.8 reshape_tile.8.seg_col_ref
  30.3 0.7 reshape_tile.7.seg_row_ref
  31.0 0.6 fusion.15.key_row_ref
  31.6 0.8 fusion.10.key_col_ref
  32.4 61.3 %all-to-all-done = bf16[128,4,5120]{2,1,0:T(4,128)(2,1)} async-done(((bf16[128,4,5120]{2,1,0:T(4,128)(2,1)}), bf16[128,4,5120]{2,1,0:T(4,128)(2,1)}, u32[]{:S(2)}, u32[]{:S(2)}) %all-to-all-start) | async-done | bytes 5242912 | tf_op jit(solution)/shard_map/all_to_all | solution.py:112
  93.7 8.9 %reshape.176.q_ref.k_ref.v_ref.o_ref = bf16[512,5120]{1,0:T(8,128)(2,1)} reshape(bf16[128,4,5120]{2,1,0:T(4,128)(2,1)} %all-to-all-done) | data formatting | bytes 10485760 | tf_op jit(solution)/shard_map/reshape | solution.py:113
  102.7 22.5 %shard_map.102 = bf16[512,3072]{1,0:T(8,128)(2,1)} custom-call(s32[512,1]{1,0:T(8,128)} %reshape_tile.8.seg_col_ref, s32[1,512]{1,0:T(1,128)} %reshape_tile.7.seg_row_ref, s32[512,1]{1,0:T(8,128)} %fusion.10.key_col_ref, s32[1,512]{1,0:T(1,128)} %fusion.15.key_row_ref, bf16[512,5120]{1,0:T(8,128)(2,1)} %reshape.176.q_ref.k_ref.v_ref.o_ref, ...), custom_call_target="tpu_custom_call" | custom-call | tf_op jit(solution)/shard_map/pallas_call | solution.py:67
  125.2 6.1 %reshape.177 = bf16[128,4,3072]{2,1,0:T(4,128)(2,1)} reshape(bf16[512,3072]{1,0:T(8,128)(2,1)} %shard_map.102) | data formatting | bytes 6291456 | tf_op jit(solution)/shard_map/reshape | solution.py:119
  131.3 7.2 %all-to-all-start.1 = ((bf16[128,4,3072]{2,1,0:T(4,128)(2,1)}), bf16[128,4,3072]{2,1,0:T(4,128)(2,1)S(1)}, u32[]{:S(2)}, u32[]{:S(2)}) async-start(bf16[128,4,3072]{2,1,0:T(4,128)(2,1)} %reshape.177), calls=%async_computation.1 | async-start | bytes 6291456 | tf_op jit(solution)/shard_map/all_to_all | solution.py:118
  138.6 4.1 %copy.19 = bf16[256,4096]{0,1:T(8,128)(2,1)} copy(bf16[256,4096]{1,0:T(8,128)(2,1)} %param.7) | data formatting | bytes 4194304 | tf_op args[0]
  142.7 2.7 %dynamic-slice_bitcast_fusion = (bf16[256,16,32]{0,2,1:T(8,128)(2,1)}, bf16[256,16,32]{0,2,1:T(8,128)(2,1)}, bf16[256,16,32]{0,2,1:T(8,128)(2,1)}, bf16[256,16,3...) fusion(bf16[256,16,8,32]{0,3,2,1:T(8,128)(2,1)} %bitcast.36, ...), kind=kLoop, calls=%fused_computation.25 | loop fusion | bytes 4194336 | tf_op jit(solution)/shard_map/jit(dynamic_index_in_dim)/squeeze | solution.py:143
  145.4 0.0 collective-permute-start
  145.4 1.2 collective-permute-start.1
  146.6 2.5 collective-permute-start.2
  149.1 1.5 collective-permute-start.3
  150.7 2.2 collective-permute-start.4
  152.8 0.1 copy.13
  152.9 0.8 reshape.199
  153.8 1.1 fusion.13
  154.9 0.8 constant_dynamic-update-slice_fusion.7
  155.6 25.6 %collective-permute-done = bf16[256,16,32]{0,2,1:T(8,128)(2,1)} collective-permute-done((bf16[256,16,32]{0,2,1:T(8,128)(2,1)}, bf16[256,16,32]{0,2,1:T(8,128)(2,1)}, u32[]{:S(2)}, u32[]{:S(2)}) %collective-permute-start) | collective-permute-done | bytes 262176 | tf_op jit(solution)/shard_map/ppermute | solution.py:144
  181.2 1.3 collective-permute-start.5
  182.5 1.7 constant_dynamic-update-slice_fusion.6
  184.2 0.0 collective-permute-done.1
  184.2 3.6 %collective-permute-start.6 = (bf16[256,16,32]{0,2,1:T(8,128)(2,1)}, bf16[256,16,32]{0,2,1:T(8,128)(2,1)}, u32[]{:S(2)}, u32[]{:S(2)}) collective-permute-start(bf16[256,16,32]{0,2,1:T(8,128)(2,1)} %get-tuple-element.6), channel_id=1, source_target_pairs={{0,7},{1,0},{2,1},{3,2},{4,3},{5,4},{6,5},{7,6},{8,15},{9,8},{10,9... | collective-permute-start | bytes 786440 | tf_op jit(solution)/shard_map/ppermute | solution.py:144
  187.8 1.7 constant_dynamic-update-slice_fusion.5
  189.5 3.6 %collective-permute-done.2 = bf16[256,16,32]{0,2,1:T(8,128)(2,1)} collective-permute-done((bf16[256,16,32]{0,2,1:T(8,128)(2,1)}, bf16[256,16,32]{0,2,1:T(8,128)(2,1)}, u32[]{:S(2)}, u32[]{:S(2)}) %collective-permute-start.2) | collective-permute-done | bytes 262176 | tf_op jit(solution)/shard_map/ppermute | solution.py:144
  193.2 1.7 constant_dynamic-update-slice_fusion.4
  194.9 0.0 collective-permute-done.3
  194.9 1.7 constant_dynamic-update-slice_fusion.3
  196.6 2.4 reshape.192
  199.0 6.5 %scatter_custom_fusion = bf16[256,3072]{1,0:T(8,128)(2,1)S(1)} fusion(s32[512]{0:T(512)S(1)} %fusion.13, bf16[512,3072]{1,0:T(8,128)(2,1)} %reshape.192, bf16[]{:T(256)} %constant.101.clone.1), kind=kCustom, calls=%fused_computation.6 | custom fusion | bytes 1573376 | tf_op jit(solution)/shard_map/scatter | solution.py:125
  205.5 0.7 fusion.16
  206.3 0.0 copy-start
  206.3 3.7 %collective-permute-start.7 = (bf16[256,512]{1,0:T(8,128)(2,1)S(1)}, bf16[256,512]{1,0:T(8,128)(2,1)S(1)}, u32[]{:S(2)}, u32[]{:S(2)}) collective-permute-start(bf16[256,512]{1,0:T(8,128)(2,1)S(1)} %get-tuple-element.5), channel_id=1, source_target_pairs={{0,1},{1,2},{2,3},{3,4},{4,5},{5,6},{6,7},{7,0},{8,9},{9,10},{10,1... | collective-permute-start | bytes 786440 | tf_op jit(solution)/shard_map/ppermute | solution.py:148
  210.1 0.0 collective-permute-done.4
  210.1 1.7 constant_dynamic-update-slice_fusion.2
  211.8 0.0 collective-permute-start.8
  211.8 1.7 constant_dynamic-update-slice_fusion.1
  213.5 0.1 collective-permute-start.9
  213.5 1.7 constant_dynamic-update-slice_fusion
  215.2 4.0 %collective-permute-start.10 = (bf16[256,512]{1,0:T(8,128)(2,1)S(1)}, bf16[256,512]{1,0:T(8,128)(2,1)S(1)}, u32[]{:S(2)}, u32[]{:S(2)}) collective-permute-start(bf16[256,512]{1,0:T(8,128)(2,1)S(1)} %get-tuple-element.5), channel_id=1, source_target_pairs={{0,4},{1,5},{2,6},{3,7},{4,0},{5,1},{6,2},{7,3},{8,12},{9,13},{10,... | collective-permute-start | bytes 786440 | tf_op jit(solution)/shard_map/ppermute | solution.py:148
  219.3 2.4 collective-permute-start.12
  221.7 0.4 collective-permute-done.8
  222.1 4.1 %collective-permute-done.9 = bf16[256,512]{1,0:T(8,128)(2,1)S(1)} collective-permute-done((bf16[256,512]{1,0:T(8,128)(2,1)S(1)}, bf16[256,512]{1,0:T(8,128)(2,1)S(1)}, u32[]{:S(2)}, u32[]{:S(2)}) %collective-permute-start.9) | collective-permute-done | bytes 262176 | tf_op jit(solution)/shard_map/ppermute | solution.py:148
  226.2 4.8 %collective-permute-done.10 = bf16[256,512]{1,0:T(8,128)(2,1)S(1)} collective-permute-done((bf16[256,512]{1,0:T(8,128)(2,1)S(1)}, bf16[256,512]{1,0:T(8,128)(2,1)S(1)}, u32[]{:S(2)}, u32[]{:S(2)}) %collective-permute-start.10) | collective-permute-done | bytes 262176 | tf_op jit(solution)/shard_map/ppermute | solution.py:148
  231.0 2.1 collective-permute-done.11
  233.2 4.5 %collective-permute-done.12 = bf16[256,512]{1,0:T(8,128)(2,1)S(1)} collective-permute-done((bf16[256,512]{1,0:T(8,128)(2,1)S(1)}, bf16[256,512]{1,0:T(8,128)(2,1)S(1)}, u32[]{:S(2)}, u32[]{:S(2)}) %collective-permute-start.12) | collective-permute-done | bytes 262176 | tf_op jit(solution)/shard_map/ppermute | solution.py:148
  237.7 2.3 collective-permute-done.13
  240.0 3.8 %fusion = f32[16,32,512]{2,1,0:T(8,128)} fusion(bf16[16,32,2048]{2,1,0:T(8,128)(2,1)} %bitcast.20, bf16[2048,512]{1,0:T(8,128)(2,1)S(1)} %constant_dynamic-update-slice_fusion.8), kind=kOutput, calls=%fused_computation.3 | convolution fusion | flops 1073741824 | bytes 5242880 | tf_op jit(solution)/shard_map/td,tc->dc/dot_general | solution.py:151
  243.8 6.1 %all-to-all-start.2 = ((f32[16,32,512]{2,1,0:T(8,128)}), f32[16,32,512]{2,1,0:T(8,128)S(1)}, u32[]{:S(2)}, u32[]{:S(2)}) async-start(f32[16,32,512]{2,1,0:T(8,128)} %fusion), calls=%async_computation.2 | async-start | bytes 2097152 | tf_op jit(solution)/shard_map/all_to_all | solution.py:153
  249.9 0.7 pad_maximum_fusion.2
  250.7 0.1 fusion.17
  250.8 1.1 pad_maximum_fusion.1
  251.9 17.2 %all-to-all-done.2 = f32[16,32,512]{2,1,0:T(8,128)S(1)} async-done(((f32[16,32,512]{2,1,0:T(8,128)}), f32[16,32,512]{2,1,0:T(8,128)S(1)}, u32[]{:S(2)}, u32[]{:S(2)}) %all-to-all-start.2) | async-done | bytes 1048608 | tf_op jit(solution)/shard_map/all_to_all | solution.py:153
  269.0 0.1 reduce_sum.9
  269.1 0.6 broadcast_multiply_fusion
  (23 shorter events, 0.2 us)
Async XLA Ops:
  17.9 11.7 %copy-start.3 = (s32[1,4]{1,0:T(1,128)S(1)}, s32[1,4]{1,0:T(1,128)}, u32[]{:S(2)}) copy-start(s32[1,4]{1,0:T(1,128)} %param.13) | copy-start | bytes 52
  17.9 75.9 %all-to-all-start = ((bf16[128,4,5120]{2,1,0:T(4,128)(2,1)}), bf16[128,4,5120]{2,1,0:T(4,128)(2,1)}, u32[]{:S(2)}, u32[]{:S(2)}) async-start(bf16[128,4,5120]{2,1,0:T(4,128)(2,1)} %reshape.181), calls=%async_computation | async-start | bytes 10485760 | tf_op jit(solution)/shard_map/all_to_all | solution.py:112
  131.3 65.3 %all-to-all-start.1 = ((bf16[128,4,3072]{2,1,0:T(4,128)(2,1)}), bf16[128,4,3072]{2,1,0:T(4,128)(2,1)S(1)}, u32[]{:S(2)}, u32[]{:S(2)}) async-start(bf16[128,4,3072]{2,1,0:T(4,128)(2,1)} %reshape.177), calls=%async_computation.1 | async-start | bytes 6291456 | tf_op jit(solution)/shard_map/all_to_all | solution.py:118
  145.4 35.8 %collective-permute-start = (bf16[256,16,32]{0,2,1:T(8,128)(2,1)}, bf16[256,16,32]{0,2,1:T(8,128)(2,1)}, u32[]{:S(2)}, u32[]{:S(2)}) collective-permute-start(bf16[256,16,32]{0,2,1:T(8,128)(2,1)} %get-tuple-element.12), channel_id=1, source_target_pairs={{0,1},{1,2},{2,3},{3,4},{4,5},{5,6},{6,7},{7,0},{8,9},{9,10},{10,1... | collective-permute-start | bytes 786440 | tf_op jit(solution)/shard_map/ppermute | solution.py:144
  145.4 38.7 %collective-permute-start.1 = (bf16[256,16,32]{0,2,1:T(8,128)(2,1)}, bf16[256,16,32]{0,2,1:T(8,128)(2,1)}, u32[]{:S(2)}, u32[]{:S(2)}) collective-permute-start(bf16[256,16,32]{0,2,1:T(8,128)(2,1)} %get-tuple-element.11), channel_id=1, source_target_pairs={{0,2},{1,3},{2,4},{3,5},{4,6},{5,7},{6,0},{7,1},{8,10},{9,11},{10,... | collective-permute-start | bytes 786440 | tf_op jit(solution)/shard_map/ppermute | solution.py:144
  146.6 46.5 %collective-permute-start.2 = (bf16[256,16,32]{0,2,1:T(8,128)(2,1)}, bf16[256,16,32]{0,2,1:T(8,128)(2,1)}, u32[]{:S(2)}, u32[]{:S(2)}) collective-permute-start(bf16[256,16,32]{0,2,1:T(8,128)(2,1)} %get-tuple-element.10), channel_id=1, source_target_pairs={{0,3},{1,4},{2,5},{3,6},{4,7},{5,0},{6,1},{7,2},{8,11},{9,12},{10,... | collective-permute-start | bytes 786440 | tf_op jit(solution)/shard_map/ppermute | solution.py:144
  149.1 45.7 %collective-permute-start.3 = (bf16[256,16,32]{0,2,1:T(8,128)(2,1)}, bf16[256,16,32]{0,2,1:T(8,128)(2,1)}, u32[]{:S(2)}, u32[]{:S(2)}) collective-permute-start(bf16[256,16,32]{0,2,1:T(8,128)(2,1)} %get-tuple-element.9), channel_id=1, source_target_pairs={{0,4},{1,5},{2,6},{3,7},{4,0},{5,1},{6,2},{7,3},{8,12},{9,13},{10,... | collective-permute-start | bytes 786440 | tf_op jit(solution)/shard_map/ppermute | solution.py:144
  150.7 59.4 %collective-permute-start.4 = (bf16[256,16,32]{0,2,1:T(8,128)(2,1)}, bf16[256,16,32]{0,2,1:T(8,128)(2,1)}, u32[]{:S(2)}, u32[]{:S(2)}) collective-permute-start(bf16[256,16,32]{0,2,1:T(8,128)(2,1)} %get-tuple-element.8), channel_id=1, source_target_pairs={{0,5},{1,6},{2,7},{3,0},{4,1},{5,2},{6,3},{7,4},{8,13},{9,14},{10,... | collective-permute-start | bytes 786440 | tf_op jit(solution)/shard_map/ppermute | solution.py:144
  181.2 30.5 %collective-permute-start.5 = (bf16[256,16,32]{0,2,1:T(8,128)(2,1)}, bf16[256,16,32]{0,2,1:T(8,128)(2,1)}, u32[]{:S(2)}, u32[]{:S(2)}) collective-permute-start(bf16[256,16,32]{0,2,1:T(8,128)(2,1)} %get-tuple-element.7), channel_id=1, source_target_pairs={{0,6},{1,7},{2,0},{3,1},{4,2},{5,3},{6,4},{7,5},{8,14},{9,15},{10,... | collective-permute-start | bytes 786440 | tf_op jit(solution)/shard_map/ppermute | solution.py:144
  184.2 29.4 %collective-permute-start.6 = (bf16[256,16,32]{0,2,1:T(8,128)(2,1)}, bf16[256,16,32]{0,2,1:T(8,128)(2,1)}, u32[]{:S(2)}, u32[]{:S(2)}) collective-permute-start(bf16[256,16,32]{0,2,1:T(8,128)(2,1)} %get-tuple-element.6), channel_id=1, source_target_pairs={{0,7},{1,0},{2,1},{3,2},{4,3},{5,4},{6,5},{7,6},{8,15},{9,8},{10,9... | collective-permute-start | bytes 786440 | tf_op jit(solution)/shard_map/ppermute | solution.py:144
  206.3 26.8 %copy-start = (bf16[256,512]{1,0:T(8,128)(2,1)}, bf16[256,512]{1,0:T(8,128)(2,1)S(1)}, u32[]{:S(2)}) copy-start(bf16[256,512]{1,0:T(8,128)(2,1)S(1)} %get-tuple-element.5) | copy-start | bytes 786436
  206.3 13.0 %collective-permute-start.7 = (bf16[256,512]{1,0:T(8,128)(2,1)S(1)}, bf16[256,512]{1,0:T(8,128)(2,1)S(1)}, u32[]{:S(2)}, u32[]{:S(2)}) collective-permute-start(bf16[256,512]{1,0:T(8,128)(2,1)S(1)} %get-tuple-element.5), channel_id=1, source_target_pairs={{0,1},{1,2},{2,3},{3,4},{4,5},{5,6},{6,7},{7,0},{8,9},{9,10},{10,1... | collective-permute-start | bytes 786440 | tf_op jit(solution)/shard_map/ppermute | solution.py:148
  211.8 10.3 %collective-permute-start.8 = (bf16[256,512]{1,0:T(8,128)(2,1)S(1)}, bf16[256,512]{1,0:T(8,128)(2,1)S(1)}, u32[]{:S(2)}, u32[]{:S(2)}) collective-permute-start(bf16[256,512]{1,0:T(8,128)(2,1)S(1)} %get-tuple-element.5), channel_id=1, source_target_pairs={{0,2},{1,3},{2,4},{3,5},{4,6},{5,7},{6,0},{7,1},{8,10},{9,11},{10,... | collective-permute-start | bytes 786440 | tf_op jit(solution)/shard_map/ppermute | solution.py:148
  213.5 12.7 %collective-permute-start.9 = (bf16[256,512]{1,0:T(8,128)(2,1)S(1)}, bf16[256,512]{1,0:T(8,128)(2,1)S(1)}, u32[]{:S(2)}, u32[]{:S(2)}) collective-permute-start(bf16[256,512]{1,0:T(8,128)(2,1)S(1)} %get-tuple-element.5), channel_id=1, source_target_pairs={{0,3},{1,4},{2,5},{3,6},{4,7},{5,0},{6,1},{7,2},{8,11},{9,12},{10,... | collective-permute-start | bytes 786440 | tf_op jit(solution)/shard_map/ppermute | solution.py:148
  215.2 15.7 %collective-permute-start.10 = (bf16[256,512]{1,0:T(8,128)(2,1)S(1)}, bf16[256,512]{1,0:T(8,128)(2,1)S(1)}, u32[]{:S(2)}, u32[]{:S(2)}) collective-permute-start(bf16[256,512]{1,0:T(8,128)(2,1)S(1)} %get-tuple-element.5), channel_id=1, source_target_pairs={{0,4},{1,5},{2,6},{3,7},{4,0},{5,1},{6,2},{7,3},{8,12},{9,13},{10,... | collective-permute-start | bytes 786440 | tf_op jit(solution)/shard_map/ppermute | solution.py:148
  219.3 13.8 %collective-permute-start.11 = (bf16[256,512]{1,0:T(8,128)(2,1)S(1)}, bf16[256,512]{1,0:T(8,128)(2,1)S(1)}, u32[]{:S(2)}, u32[]{:S(2)}) collective-permute-start(bf16[256,512]{1,0:T(8,128)(2,1)S(1)} %get-tuple-element.5), channel_id=1, source_target_pairs={{0,5},{1,6},{2,7},{3,0},{4,1},{5,2},{6,3},{7,4},{8,13},{9,14},{10,... | collective-permute-start | bytes 786440 | tf_op jit(solution)/shard_map/ppermute | solution.py:148
  219.3 18.4 %collective-permute-start.12 = (bf16[256,512]{1,0:T(8,128)(2,1)S(1)}, bf16[256,512]{1,0:T(8,128)(2,1)S(1)}, u32[]{:S(2)}, u32[]{:S(2)}) collective-permute-start(bf16[256,512]{1,0:T(8,128)(2,1)S(1)} %get-tuple-element.5), channel_id=1, source_target_pairs={{0,6},{1,7},{2,0},{3,1},{4,2},{5,3},{6,4},{7,5},{8,14},{9,15},{10,... | collective-permute-start | bytes 786440 | tf_op jit(solution)/shard_map/ppermute | solution.py:148
  222.1 17.9 %collective-permute-start.13 = (bf16[256,512]{1,0:T(8,128)(2,1)S(1)}, bf16[256,512]{1,0:T(8,128)(2,1)S(1)}, u32[]{:S(2)}, u32[]{:S(2)}) collective-permute-start(bf16[256,512]{1,0:T(8,128)(2,1)S(1)} %get-tuple-element.5), channel_id=1, source_target_pairs={{0,7},{1,0},{2,1},{3,2},{4,3},{5,4},{6,5},{7,6},{8,15},{9,8},{10,9... | collective-permute-start | bytes 786440 | tf_op jit(solution)/shard_map/ppermute | solution.py:148
  243.8 6.1 %copy-start.1 = (bf16[256,128]{1,0:T(8,128)(2,1)S(1)}, bf16[256,128]{1,0:T(8,128)(2,1)}, u32[]{:S(2)}) copy-start(bf16[256,128]{1,0:T(8,128)(2,1)} %get-tuple-element.20) | copy-start | bytes 196612
  243.8 6.1 %copy-start.2 = (bf16[256,128]{1,0:T(8,128)(2,1)S(1)}, bf16[256,128]{1,0:T(8,128)(2,1)}, u32[]{:S(2)}) copy-start(bf16[256,128]{1,0:T(8,128)(2,1)} %get-tuple-element.21) | copy-start | bytes 196612
  243.8 25.2 %all-to-all-start.2 = ((f32[16,32,512]{2,1,0:T(8,128)}), f32[16,32,512]{2,1,0:T(8,128)S(1)}, u32[]{:S(2)}, u32[]{:S(2)}) async-start(f32[16,32,512]{2,1,0:T(8,128)} %fusion), calls=%async_computation.2 | async-start | bytes 2097152 | tf_op jit(solution)/shard_map/all_to_all | solution.py:153

commit v4 on v3

--- a/solution.py
+++ b/solution.py
@@ -142,12 +142,11 @@
         ring = [(i, (i + shift) % groups) for i in range(groups)]
         theirs = lax.dynamic_index_in_dim(blocks, (me + shift) % groups, axis=2, keepdims=False)
         hidden_grp.append(lax.ppermute(theirs, INNER, ring))
-    grad_grp = [grad_values]
-    for shift in shifts:
-        ring = [(i, (i + shift) % groups) for i in range(groups)]
-        grad_grp.append(lax.ppermute(grad_values, INNER, ring))
     hidden_grp = jnp.concatenate(hidden_grp, axis=0).reshape(groups * tok_rows, -1)
-    grad_grp = jnp.concatenate(grad_grp, axis=0)
+    spread = jnp.broadcast_to(grad_values[None], (groups,) + grad_values.shape)
+    gathered = lax.all_to_all(spread, INNER, 0, 0, tiled=True)
+    order = (me - jnp.arange(groups, dtype=jnp.int32)) % groups
+    grad_grp = jnp.take(gathered, order, axis=0).reshape(groups * tok_rows, -1)
     partial = jnp.einsum("td,tc->dc", hidden_grp, grad_grp, preferred_element_type=jnp.float32)
     partial = partial.reshape(outers, partial.shape[0] // outers, partial.shape[1])
     grad_wv = lax.all_to_all(partial, OUTER, 0, 0, tiled=True).sum(0) * grad_scale

time: 271 us -> 275 us (1.015); the launches traced: 270 us -> 270 us
  waiting for transfers between devices: 126 us -> 142 us
  local copies, waits for them, and re-layouts: 61.6 us -> 54.1 us
  starting transfers between devices: 47.5 us -> 40 us
    all_to_all x1, waiting for transfers between devices: 0.01 us -> 41.3 us  [local(): lax.all_to_all(rows_out.reshape(owners, slot_count, rows_out.shape[1]), D...]
    ppermute x7 -> x0, waiting for transfers between devices: 18.2 us -> none  [local(): grad_grp.append(lax.ppermute(grad_values, INNER, ring))]
    ppermute x7 -> x0, starting transfers between devices: 10.2 us -> none  [local(): grad_grp.append(lax.ppermute(grad_values, INNER, ring))]
    unnamed x22 -> x16, local copies, waits for them, and re-layouts: 15.2 us -> 8.59 us
    all_to_all x0 -> x1, starting transfers between devices: none -> 4.35 us  [local(): gathered = lax.all_to_all(spread, INNER, 0, 0, tiled=True)]
    ppermute x7, waiting for transfers between devices: 29.3 us -> 25.6 us  [local(): hidden_grp.append(lax.ppermute(theirs, INNER, ring))]
    all_to_all x1, waiting for transfers between devices: 17.2 us -> 14 us  [local(): lax.all_to_all(partial, OUTER, 0, 0, tiled=True).sum(0) * grad_scale]
  transfers between devices with their start and end apart: 17 -> 11, of which waited for: 10 -> 7; matrix products, arithmetic and copies ran while one was open for 13% -> 5% of each run, Pallas kernels for 0% -> 0%
where the time goes in v4:
time: 275 us; the launch traced here: 270 us
  waiting for transfers between devices  142 us (52%)
  local copies, waits for them, and re-layouts  54.1 us (20%)
  starting transfers between devices  40 us (15%)
  Pallas kernels  22.5 us (8%)
  other arithmetic  6.88 us (3%)
  matrix products  3.82 us (1%)
    all_to_all x1, waiting for transfers between devices, local(): rows_in = lax.all_to_all(table[pick_rows], DP, 0, 0, tiled=True)  61.3 us
    all_to_all x1, waiting for transfers between devices, local(): lax.all_to_all(rows_out.reshape(owners, slot_count, rows_out.shape[1]), D...  41.3 us
    ppermute x7, waiting for transfers between devices, local(): hidden_grp.append(lax.ppermute(theirs, INNER, ring))  25.6 us
    pallas_call x1, Pallas kernels, attend_rows(): pl.pallas_call(attend_kernel, grid=(HK,), in_specs=[col, row, col, row, p...  22.5 us
    gather x2, local copies, waits for them, and re-layouts, local(): rows_in = lax.all_to_all(table[pick_rows], DP, 0, 0, tiled=True)  14.4 us
    all_to_all x1, waiting for transfers between devices, local(): lax.all_to_all(partial, OUTER, 0, 0, tiled=True).sum(0) * grad_scale  14 us
    ppermute x7, starting transfers between devices, local(): hidden_grp.append(lax.ppermute(theirs, INNER, ring))  12.9 us
    all_to_all x1, starting transfers between devices, local(): rows_in = lax.all_to_all(table[pick_rows], DP, 0, 0, tiled=True)  11.6 us
  transfers between devices with their start and end apart: 11, of which 7 were waited for; matrix products, arithmetic and copies ran while one was open for 5% of the time, Pallas kernels for 0%

profile of v4, /device:TPU:0, one launch (start us, length us, event | category | flops | bytes accessed | tf_op | source)
XLA Modules:
  0.0 270.5 jit_solution(4435815940778239611)
XLA Ops:
  0.6 0.7 compare_select_fusion.1
  1.3 0.1 copy.17
  1.4 0.1 reshape.270
  1.6 1.8 pad_maximum_fusion
  3.4 5.1 %gather_fusion = bf16[512,5120]{1,0:T(8,128)(2,1)} fusion(bf16[256,5120]{1,0:T(8,128)(2,1)S(1)} %pad_maximum_fusion, s32[1024]{0:T(1024)S(1)} %pad_clamp_fusion.1), kind=kCustom, calls=%fused_computation | custom fusion | bytes 10487808 | tf_op jit(solution)/shard_map/gather | solution.py:112
  8.5 9.3 %reshape.269 = bf16[128,4,5120]{2,1,0:T(4,128)(2,1)} reshape(bf16[512,5120]{1,0:T(8,128)(2,1)} %gather_fusion) | data formatting | bytes 10485760 | tf_op jit(solution)/shard_map/gather | solution.py:112
  17.8 11.6 %all-to-all-start = ((bf16[128,4,5120]{2,1,0:T(4,128)(2,1)}), bf16[128,4,5120]{2,1,0:T(4,128)(2,1)}, u32[]{:S(2)}, u32[]{:S(2)}) async-start(bf16[128,4,5120]{2,1,0:T(4,128)(2,1)} %reshape.269), calls=%async_computation | async-start | bytes 10485760 | tf_op jit(solution)/shard_map/all_to_all | solution.py:112
  29.5 0.0 copy-done.3
  29.5 0.8 reshape_tile.8.seg_col_ref
  30.3 0.7 reshape_tile.7.seg_row_ref
  31.0 0.6 fusion.13.key_row_ref
  31.6 0.8 fusion.8.key_col_ref
  32.4 61.3 %all-to-all-done = bf16[128,4,5120]{2,1,0:T(4,128)(2,1)} async-done(((bf16[128,4,5120]{2,1,0:T(4,128)(2,1)}), bf16[128,4,5120]{2,1,0:T(4,128)(2,1)}, u32[]{:S(2)}, u32[]{:S(2)}) %all-to-all-start) | async-done | bytes 5242912 | tf_op jit(solution)/shard_map/all_to_all | solution.py:112
  93.7 8.9 %reshape.264.q_ref.k_ref.v_ref.o_ref = bf16[512,5120]{1,0:T(8,128)(2,1)} reshape(bf16[128,4,5120]{2,1,0:T(4,128)(2,1)} %all-to-all-done) | data formatting | bytes 10485760 | tf_op jit(solution)/shard_map/reshape | solution.py:113
  102.6 22.5 %shard_map.102 = bf16[512,3072]{1,0:T(8,128)(2,1)} custom-call(s32[512,1]{1,0:T(8,128)} %reshape_tile.8.seg_col_ref, s32[1,512]{1,0:T(1,128)} %reshape_tile.7.seg_row_ref, s32[512,1]{1,0:T(8,128)} %fusion.8.key_col_ref, s32[1,512]{1,0:T(1,128)} %fusion.13.key_row_ref, bf16[512,5120]{1,0:T(8,128)(2,1)} %reshape.264.q_ref.k_ref.v_ref.o_ref, ...), custom_call_target="tpu_custom_call" | custom-call | tf_op jit(solution)/shard_map/pallas_call | solution.py:67
  125.1 6.1 %reshape.265 = bf16[128,4,3072]{2,1,0:T(4,128)(2,1)} reshape(bf16[512,3072]{1,0:T(8,128)(2,1)} %shard_map.102) | data formatting | bytes 6291456 | tf_op jit(solution)/shard_map/reshape | solution.py:119
  131.3 7.4 %all-to-all-start.1 = ((bf16[128,4,3072]{2,1,0:T(4,128)(2,1)}), bf16[128,4,3072]{2,1,0:T(4,128)(2,1)S(1)}, u32[]{:S(2)}, u32[]{:S(2)}) async-start(bf16[128,4,3072]{2,1,0:T(4,128)(2,1)} %reshape.265), calls=%async_computation.1 | async-start | bytes 6291456 | tf_op jit(solution)/shard_map/all_to_all | solution.py:118
  138.7 0.1 copy.13
  138.8 0.1 reshape.295
  138.9 0.1 fusion.11
  139.1 41.3 %all-to-all-done.1 = bf16[128,4,3072]{2,1,0:T(4,128)(2,1)S(1)} async-done(((bf16[128,4,3072]{2,1,0:T(4,128)(2,1)}), bf16[128,4,3072]{2,1,0:T(4,128)(2,1)S(1)}, u32[]{:S(2)}, u32[]{:S(2)}) %all-to-all-start.1) | async-done | bytes 3145760 | tf_op jit(solution)/shard_map/all_to_all | solution.py:118
  180.3 2.4 reshape.288
  182.7 6.5 %scatter_custom_fusion = bf16[256,3072]{1,0:T(8,128)(2,1)S(1)} fusion(s32[512]{0:T(512)S(1)} %fusion.11, bf16[512,3072]{1,0:T(8,128)(2,1)} %reshape.288, bf16[]{:T(256)} %constant.123.clone.1), kind=kCustom, calls=%fused_computation.6 | custom fusion | bytes 1573376 | tf_op jit(solution)/shard_map/scatter | solution.py:125
  189.2 0.0 copy-start
  189.2 0.1 fusion.17
  189.4 0.0 copy-start.2
  189.4 1.8 broadcast_in_dim.31
  191.2 0.0 copy-done
  191.2 4.3 %all-to-all-start.2 = ((bf16[8,256,512]{2,1,0:T(8,128)(2,1)}), bf16[8,256,512]{2,1,0:T(8,128)(2,1)}, u32[]{:S(2)}, u32[]{:S(2)}) async-start(bf16[8,256,512]{2,1,0:T(8,128)(2,1)} %broadcast_in_dim.31), calls=%async_computation.2 | async-start | bytes 4194304 | tf_op jit(solution)/shard_map/all_to_all | solution.py:147
  195.6 3.3 %copy.19 = bf16[256,4096]{0,1:T(8,128)(2,1)S(1)} copy(bf16[256,4096]{1,0:T(8,128)(2,1)} %param.7) | data formatting | bytes 4194304 | tf_op args[0]
  198.9 0.2 dynamic-slice_bitcast_fusion
  199.2 0.3 collective-permute-start
  199.4 1.6 collective-permute-start.1
  201.1 2.0 collective-permute-start.2
  203.1 2.0 collective-permute-start.3
  205.1 1.7 collective-permute-start.4
  206.8 0.8 constant_dynamic-update-slice_fusion.7
  207.6 20.0 %collective-permute-done = bf16[256,16,32]{0,2,1:T(8,128)(2,1)S(1)} collective-permute-done((bf16[256,16,32]{0,2,1:T(8,128)(2,1)S(1)}, bf16[256,16,32]{0,2,1:T(8,128)(2,1)S(1)}, u32[]{:S(2)}, u32[]{:S(2)}) %collective-permute-start) | collective-permute-done | bytes 262176 | tf_op jit(solution)/shard_map/ppermute | solution.py:144
  227.5 0.7 collective-permute-start.5
  228.2 0.8 constant_dynamic-update-slice_fusion.6
  229.0 0.0 collective-permute-done.1
  229.0 4.6 %collective-permute-start.6 = (bf16[256,16,32]{0,2,1:T(8,128)(2,1)S(1)}, bf16[256,16,32]{0,2,1:T(8,128)(2,1)S(1)}, u32[]{:S(2)}, u32[]{:S(2)}) collective-permute-start(bf16[256,16,32]{0,2,1:T(8,128)(2,1)S(1)} %get-tuple-element.4), channel_id=1, source_target_pairs={{0,7},{1,0},{2,1},{3,2},{4,3},{5,4},{6,5},{7,6},{8,15},{9,8},{10,9... | collective-permute-start | bytes 786440 | tf_op jit(solution)/shard_map/ppermute | solution.py:144
  233.6 0.8 constant_dynamic-update-slice_fusion.5
  234.3 4.6 %collective-permute-done.2 = bf16[256,16,32]{0,2,1:T(8,128)(2,1)S(1)} collective-permute-done((bf16[256,16,32]{0,2,1:T(8,128)(2,1)S(1)}, bf16[256,16,32]{0,2,1:T(8,128)(2,1)S(1)}, u32[]{:S(2)}, u32[]{:S(2)}) %collective-permute-start.2) | collective-permute-done | bytes 262176 | tf_op jit(solution)/shard_map/ppermute | solution.py:144
  238.9 0.8 constant_dynamic-update-slice_fusion.4
  239.7 0.4 collective-permute-done.3
  240.0 0.8 constant_dynamic-update-slice_fusion.3
  240.8 0.7 collective-permute-done.4
  241.5 0.7 constant_dynamic-update-slice_fusion.2
  242.2 0.0 collective-permute-done.5
  242.2 0.7 constant_dynamic-update-slice_fusion.1
  243.0 0.0 collective-permute-done.6
  243.0 0.7 constant_dynamic-update-slice_fusion
  243.7 0.0 all-to-all-done.2
  243.7 2.3 gather_fusion.1
  246.0 0.3 broadcast_select_fusion
  246.3 3.8 %fusion.19 = f32[16,32,512]{2,1,0:T(8,128)} fusion(bf16[16,32,2048]{2,1,0:T(8,128)(2,1)} %bitcast.20, bf16[2048,512,1]{1,0,2:T(8,128)(2,1)S(1)} %bitcast.40), kind=kOutput, calls=%fused_computation.67 | convolution fusion | flops 1073741824 | bytes 5242880 | tf_op jit(solution)/shard_map/td,tc->dc/dot_general | solution.py:150
  250.1 3.8 %all-to-all-start.3 = ((f32[16,32,512]{2,1,0:T(8,128)}), f32[16,32,512]{2,1,0:T(8,128)S(1)}, u32[]{:S(2)}, u32[]{:S(2)}) async-start(f32[16,32,512]{2,1,0:T(8,128)} %fusion.19), calls=%async_computation.3 | async-start | bytes 2097152 | tf_op jit(solution)/shard_map/all_to_all | solution.py:152
  253.9 0.7 pad_maximum_fusion.2
  254.6 0.1 fusion.18
  254.7 1.1 pad_maximum_fusion.1
  255.8 14.0 %all-to-all-done.3 = f32[16,32,512]{2,1,0:T(8,128)S(1)} async-done(((f32[16,32,512]{2,1,0:T(8,128)}), f32[16,32,512]{2,1,0:T(8,128)S(1)}, u32[]{:S(2)}, u32[]{:S(2)}) %all-to-all-start.3) | async-done | bytes 1048608 | tf_op jit(solution)/shard_map/all_to_all | solution.py:152
  269.8 0.1 reduce_sum.9
  269.8 0.6 broadcast_multiply_fusion
  (10 shorter events, 0.1 us)
Async XLA Ops:
  17.8 11.7 %copy-start.3 = (s32[1,4]{1,0:T(1,128)S(1)}, s32[1,4]{1,0:T(1,128)}, u32[]{:S(2)}) copy-start(s32[1,4]{1,0:T(1,128)} %param.13) | copy-start | bytes 52
  17.8 75.9 %all-to-all-start = ((bf16[128,4,5120]{2,1,0:T(4,128)(2,1)}), bf16[128,4,5120]{2,1,0:T(4,128)(2,1)}, u32[]{:S(2)}, u32[]{:S(2)}) async-start(bf16[128,4,5120]{2,1,0:T(4,128)(2,1)} %reshape.269), calls=%async_computation | async-start | bytes 10485760 | tf_op jit(solution)/shard_map/all_to_all | solution.py:112
  131.3 49.0 %all-to-all-start.1 = ((bf16[128,4,3072]{2,1,0:T(4,128)(2,1)}), bf16[128,4,3072]{2,1,0:T(4,128)(2,1)S(1)}, u32[]{:S(2)}, u32[]{:S(2)}) async-start(bf16[128,4,3072]{2,1,0:T(4,128)(2,1)} %reshape.265), calls=%async_computation.1 | async-start | bytes 6291456 | tf_op jit(solution)/shard_map/all_to_all | solution.py:118
  189.2 1.9 copy-start
  189.4 1.8 copy-start.2
  191.2 52.6 %all-to-all-start.2 = ((bf16[8,256,512]{2,1,0:T(8,128)(2,1)}), bf16[8,256,512]{2,1,0:T(8,128)(2,1)}, u32[]{:S(2)}, u32[]{:S(2)}) async-start(bf16[8,256,512]{2,1,0:T(8,128)(2,1)} %broadcast_in_dim.31), calls=%async_computation.2 | async-start | bytes 4194304 | tf_op jit(solution)/shard_map/all_to_all | solution.py:147
  199.2 28.4 %collective-permute-start = (bf16[256,16,32]{0,2,1:T(8,128)(2,1)S(1)}, bf16[256,16,32]{0,2,1:T(8,128)(2,1)S(1)}, u32[]{:S(2)}, u32[]{:S(2)}) collective-permute-start(bf16[256,16,32]{0,2,1:T(8,128)(2,1)S(1)} %get-tuple-element.10), channel_id=1, source_target_pairs={{0,1},{1,2},{2,3},{3,4},{4,5},{5,6},{6,7},{7,0},{8,9},{9,10},{10,1... | collective-permute-start | bytes 786440 | tf_op jit(solution)/shard_map/ppermute | solution.py:144
  199.4 29.6 %collective-permute-start.1 = (bf16[256,16,32]{0,2,1:T(8,128)(2,1)S(1)}, bf16[256,16,32]{0,2,1:T(8,128)(2,1)S(1)}, u32[]{:S(2)}, u32[]{:S(2)}) collective-permute-start(bf16[256,16,32]{0,2,1:T(8,128)(2,1)S(1)} %get-tuple-element.9), channel_id=1, source_target_pairs={{0,2},{1,3},{2,4},{3,5},{4,6},{5,7},{6,0},{7,1},{8,10},{9,11},{10,... | collective-permute-start | bytes 786440 | tf_op jit(solution)/shard_map/ppermute | solution.py:144
  201.1 37.8 %collective-permute-start.2 = (bf16[256,16,32]{0,2,1:T(8,128)(2,1)S(1)}, bf16[256,16,32]{0,2,1:T(8,128)(2,1)S(1)}, u32[]{:S(2)}, u32[]{:S(2)}) collective-permute-start(bf16[256,16,32]{0,2,1:T(8,128)(2,1)S(1)} %get-tuple-element.8), channel_id=1, source_target_pairs={{0,3},{1,4},{2,5},{3,6},{4,7},{5,0},{6,1},{7,2},{8,11},{9,12},{10,... | collective-permute-start | bytes 786440 | tf_op jit(solution)/shard_map/ppermute | solution.py:144
  203.1 37.0 %collective-permute-start.3 = (bf16[256,16,32]{0,2,1:T(8,128)(2,1)S(1)}, bf16[256,16,32]{0,2,1:T(8,128)(2,1)S(1)}, u32[]{:S(2)}, u32[]{:S(2)}) collective-permute-start(bf16[256,16,32]{0,2,1:T(8,128)(2,1)S(1)} %get-tuple-element.7), channel_id=1, source_target_pairs={{0,4},{1,5},{2,6},{3,7},{4,0},{5,1},{6,2},{7,3},{8,12},{9,13},{10,... | collective-permute-start | bytes 786440 | tf_op jit(solution)/shard_map/ppermute | solution.py:144
  205.1 36.4 %collective-permute-start.4 = (bf16[256,16,32]{0,2,1:T(8,128)(2,1)S(1)}, bf16[256,16,32]{0,2,1:T(8,128)(2,1)S(1)}, u32[]{:S(2)}, u32[]{:S(2)}) collective-permute-start(bf16[256,16,32]{0,2,1:T(8,128)(2,1)S(1)} %get-tuple-element.6), channel_id=1, source_target_pairs={{0,5},{1,6},{2,7},{3,0},{4,1},{5,2},{6,3},{7,4},{8,13},{9,14},{10,... | collective-permute-start | bytes 786440 | tf_op jit(solution)/shard_map/ppermute | solution.py:144
  227.5 14.7 %collective-permute-start.5 = (bf16[256,16,32]{0,2,1:T(8,128)(2,1)S(1)}, bf16[256,16,32]{0,2,1:T(8,128)(2,1)S(1)}, u32[]{:S(2)}, u32[]{:S(2)}) collective-permute-start(bf16[256,16,32]{0,2,1:T(8,128)(2,1)S(1)} %get-tuple-element.5), channel_id=1, source_target_pairs={{0,6},{1,7},{2,0},{3,1},{4,2},{5,3},{6,4},{7,5},{8,14},{9,15},{10,... | collective-permute-start | bytes 786440 | tf_op jit(solution)/shard_map/ppermute | solution.py:144
  229.0 14.0 %collective-permute-start.6 = (bf16[256,16,32]{0,2,1:T(8,128)(2,1)S(1)}, bf16[256,16,32]{0,2,1:T(8,128)(2,1)S(1)}, u32[]{:S(2)}, u32[]{:S(2)}) collective-permute-start(bf16[256,16,32]{0,2,1:T(8,128)(2,1)S(1)} %get-tuple-element.4), channel_id=1, source_target_pairs={{0,7},{1,0},{2,1},{3,2},{4,3},{5,4},{6,5},{7,6},{8,15},{9,8},{10,9... | collective-permute-start | bytes 786440 | tf_op jit(solution)/shard_map/ppermute | solution.py:144
  250.1 4.5 %copy-start.1 = (bf16[256,3072]{1,0:T(8,128)(2,1)S(1)}, bf16[256,3072]{1,0:T(8,128)(2,1)}, u32[]{:S(2)}) copy-start(bf16[256,3072]{1,0:T(8,128)(2,1)} %copy-done) | copy-start | bytes 4718596
  250.1 19.7 %all-to-all-start.3 = ((f32[16,32,512]{2,1,0:T(8,128)}), f32[16,32,512]{2,1,0:T(8,128)S(1)}, u32[]{:S(2)}, u32[]{:S(2)}) async-start(f32[16,32,512]{2,1,0:T(8,128)} %fusion.19), calls=%async_computation.3 | async-start | bytes 2097152 | tf_op jit(solution)/shard_map/all_to_all | solution.py:152

commit v5 on v4

--- a/solution.py
+++ b/solution.py
@@ -109,11 +109,21 @@
     pick_rows = jnp.maximum(send_rows, 0).T
     grad_scale = 1.0 / math.sqrt(tok_rows * owners)
     table = jnp.concatenate((queries, keys, values, grad_attn), axis=1)
+    me = lax.axis_index(INNER)
+    shifts = range(1, groups)
+    blocks = hidden_in.reshape(tok_rows, outers, groups, -1)
+    hidden_grp = [lax.dynamic_index_in_dim(blocks, me, axis=2, keepdims=False)]
+    for shift in shifts:
+        ring = [(i, (i + shift) % groups) for i in range(groups)]
+        theirs = lax.dynamic_index_in_dim(blocks, (me + shift) % groups, axis=2, keepdims=False)
+        hidden_grp.append(lax.ppermute(theirs, INNER, ring))
+    hidden_grp = jnp.concatenate(hidden_grp, axis=0).reshape(groups * tok_rows, -1)
     rows_in = lax.all_to_all(table[pick_rows], DP, 0, 0, tiled=True)
     rows_in = rows_in.reshape(owners * slot_count, table.shape[1])
     row_ids = jnp.arange(owners * slot_count, dtype=jnp.int32)
     order_key = (row_ids % slot_count) * owners + row_ids // slot_count
     segment = jnp.tile(slot_docs[0].astype(jnp.int32), owners)
+    hidden_grp, rows_in = lax.optimization_barrier((hidden_grp, rows_in))
     rows_out = attend_rows(rows_in, segment, order_key)
     back = lax.all_to_all(
         rows_out.reshape(owners, slot_count, rows_out.shape[1]), DP, 0, 0, tiled=True
@@ -134,15 +144,6 @@
     grad_values = jnp.concatenate(
         [home[:, g * out_w + q_w + DH : (g + 1) * out_w] for g in range(HK)], axis=1
     )
-    me = lax.axis_index(INNER)
-    shifts = range(1, groups)
-    blocks = hidden_in.reshape(tok_rows, outers, groups, -1)
-    hidden_grp = [lax.dynamic_index_in_dim(blocks, me, axis=2, keepdims=False)]
-    for shift in shifts:
-        ring = [(i, (i + shift) % groups) for i in range(groups)]
-        theirs = lax.dynamic_index_in_dim(blocks, (me + shift) % groups, axis=2, keepdims=False)
-        hidden_grp.append(lax.ppermute(theirs, INNER, ring))
-    hidden_grp = jnp.concatenate(hidden_grp, axis=0).reshape(groups * tok_rows, -1)
     spread = jnp.broadcast_to(grad_values[None], (groups,) + grad_values.shape)
     gathered = lax.all_to_all(spread, INNER, 0, 0, tiled=True)
     order = (me - jnp.arange(groups, dtype=jnp.int32)) % groups

time: 275 us -> 274 us (level); the launches traced: 270 us -> 273 us
  starting transfers between devices: 40 us -> 43.5 us
    all_to_all x1, waiting for transfers between devices: 61.3 us -> 0.01 us  [local(): rows_in = lax.all_to_all(table[pick_rows], DP, 0, 0, tiled=True)]
    ppermute x7, waiting for transfers between devices: 25.6 us -> 55.5 us  [local(): hidden_grp.append(lax.ppermute(theirs, INNER, ring))]
    all_to_all x1, waiting for transfers between devices: 0.01 us -> 27 us  [local(): gathered = lax.all_to_all(spread, INNER, 0, 0, tiled=True)]
    all_to_all x1, starting transfers between devices: 7.39 us -> 12.4 us  [local(): lax.all_to_all(rows_out.reshape(owners, slot_count, rows_out.shape[1]), D...]
    unnamed x16 -> x18, local copies, waits for them, and re-layouts: 8.59 us -> 8.73 us
  transfers between devices with their start and end apart: 11 -> 11, of which waited for: 7 -> 8; matrix products, arithmetic and copies ran while one was open for 5% -> 6% of each run, Pallas kernels for 0% -> 0%
where the time goes in v5:
time: 274 us; the launch traced here: 273 us
  waiting for transfers between devices  140 us (51%)
  local copies, waits for them, and re-layouts  55.1 us (20%)
  starting transfers between devices  43.5 us (16%)
  Pallas kernels  22.5 us (8%)
  other arithmetic  8.63 us (3%)
    ppermute x7, waiting for transfers between devices, local(): hidden_grp.append(lax.ppermute(theirs, INNER, ring))  55.5 us
    all_to_all x1, waiting for transfers between devices, local(): lax.all_to_all(rows_out.reshape(owners, slot_count, rows_out.shape[1]), D...  41.4 us
    all_to_all x1, waiting for transfers between devices, local(): gathered = lax.all_to_all(spread, INNER, 0, 0, tiled=True)  27 us
    pallas_call x1, Pallas kernels, attend_rows(): pl.pallas_call(attend_kernel, grid=(HK,), in_specs=[col, row, col, row, p...  22.5 us
    all_to_all x1, waiting for transfers between devices, local(): lax.all_to_all(partial, OUTER, 0, 0, tiled=True).sum(0) * grad_scale  15.8 us
    gather x2, local copies, waits for them, and re-layouts, local(): rows_in = lax.all_to_all(table[pick_rows], DP, 0, 0, tiled=True)  14.5 us
    all_to_all x1, starting transfers between devices, local(): lax.all_to_all(rows_out.reshape(owners, slot_count, rows_out.shape[1]), D...  12.4 us
    ppermute x7, starting transfers between devices, local(): hidden_grp.append(lax.ppermute(theirs, INNER, ring))  12.1 us
  transfers between devices with their start and end apart: 11, of which 8 were waited for; matrix products, arithmetic and copies ran while one was open for 6% of the time, Pallas kernels for 0%

profile of v5, /device:TPU:0, one launch (start us, length us, event | category | flops | bytes accessed | tf_op | source)
XLA Modules:
  0.0 272.7 jit_solution(7798654026972789277)
XLA Ops:
  0.6 0.7 compare_select_fusion.1
  1.3 0.1 copy.17
  1.4 0.1 reshape.270
  1.6 1.8 pad_maximum_fusion
  3.4 5.1 %gather_fusion = bf16[512,5120]{1,0:T(8,128)(2,1)} fusion(bf16[256,5120]{1,0:T(8,128)(2,1)S(1)} %pad_maximum_fusion, s32[1024]{0:T(1024)S(1)} %pad_clamp_fusion.1), kind=kCustom, calls=%fused_computation | custom fusion | bytes 10487808 | tf_op jit(solution)/shard_map/gather | solution.py:121
  8.5 9.3 %reshape.269 = bf16[128,4,5120]{2,1,0:T(4,128)(2,1)} reshape(bf16[512,5120]{1,0:T(8,128)(2,1)} %gather_fusion) | data formatting | bytes 10485760 | tf_op jit(solution)/shard_map/gather | solution.py:121
  17.8 11.6 %all-to-all-start = ((bf16[128,4,5120]{2,1,0:T(4,128)(2,1)}), bf16[128,4,5120]{2,1,0:T(4,128)(2,1)}, u32[]{:S(2)}, u32[]{:S(2)}) async-start(bf16[128,4,5120]{2,1,0:T(4,128)(2,1)} %reshape.269), calls=%async_computation | async-start | bytes 10485760 | tf_op jit(solution)/shard_map/all_to_all | solution.py:121
  29.6 3.3 %copy.16 = bf16[256,4096]{0,1:T(8,128)(2,1)S(1)} copy(bf16[256,4096]{1,0:T(8,128)(2,1)} %param.7) | data formatting | bytes 4194304 | tf_op args[0]
  32.9 0.0 copy-start.4
  32.9 1.0 dynamic-slice_bitcast_fusion
  34.0 0.0 collective-permute-start
  34.0 1.1 collective-permute-start.1
  35.1 2.5 collective-permute-start.2
  37.6 1.5 collective-permute-start.3
  39.1 2.2 collective-permute-start.4
  41.3 0.8 fusion.8.key_col_ref
  42.0 0.7 constant_dynamic-update-slice_fusion.7
  42.8 0.6 fusion.13.key_row_ref
  43.4 0.0 copy-done.4
  43.4 0.8 reshape_tile.8.seg_col_ref
  44.2 0.7 reshape_tile.7.seg_row_ref
  44.9 48.8 %collective-permute-done = bf16[256,16,32]{0,2,1:T(8,128)(2,1)S(1)} collective-permute-done((bf16[256,16,32]{0,2,1:T(8,128)(2,1)}, bf16[256,16,32]{0,2,1:T(8,128)(2,1)S(1)}, u32[]{:S(2)}, u32[]{:S(2)}) %collective-permute-start) | collective-permute-done | bytes 262176 | tf_op jit(solution)/shard_map/ppermute | solution.py:119
  93.7 0.5 collective-permute-start.5
  94.2 0.8 constant_dynamic-update-slice_fusion.6
  95.0 0.0 collective-permute-done.1
  95.0 4.3 %collective-permute-start.6 = (bf16[256,16,32]{0,2,1:T(8,128)(2,1)S(1)}, bf16[256,16,32]{0,2,1:T(8,128)(2,1)S(1)}, u32[]{:S(2)}, u32[]{:S(2)}) collective-permute-start(bf16[256,16,32]{0,2,1:T(8,128)(2,1)S(1)} %get-tuple-element.8), channel_id=1, source_target_pairs={{0,7},{1,0},{2,1},{3,2},{4,3},{5,4},{6,5},{7,6},{8,15},{9,8},{10,9... | collective-permute-start | bytes 786440 | tf_op jit(solution)/shard_map/ppermute | solution.py:119
  99.3 0.7 constant_dynamic-update-slice_fusion.5
  100.0 4.9 %collective-permute-done.2 = bf16[256,16,32]{0,2,1:T(8,128)(2,1)S(1)} collective-permute-done((bf16[256,16,32]{0,2,1:T(8,128)(2,1)S(1)}, bf16[256,16,32]{0,2,1:T(8,128)(2,1)S(1)}, u32[]{:S(2)}, u32[]{:S(2)}) %collective-permute-start.2) | collective-permute-done | bytes 262176 | tf_op jit(solution)/shard_map/ppermute | solution.py:119
  104.9 0.7 constant_dynamic-update-slice_fusion.4
  105.7 0.6 collective-permute-done.3
  106.3 0.8 constant_dynamic-update-slice_fusion.3
  107.0 0.9 collective-permute-done.4
  108.0 0.7 constant_dynamic-update-slice_fusion.2
  108.7 0.0 collective-permute-done.5
  108.7 0.7 constant_dynamic-update-slice_fusion.1
  109.4 0.3 collective-permute-done.6
  109.7 0.7 constant_dynamic-update-slice_fusion
  110.5 0.0 all-to-all-done
  110.5 8.9 %reshape.265.q_ref.k_ref.v_ref.o_ref = bf16[512,5120]{1,0:T(8,128)(2,1)} reshape(bf16[128,4,5120]{2,1,0:T(4,128)(2,1)} %all-to-all-done) | data formatting | bytes 10485760 | tf_op jit(solution)/shard_map/reshape | solution.py:122
  119.4 22.5 %shard_map.102 = bf16[512,3072]{1,0:T(8,128)(2,1)} custom-call(s32[512,1]{1,0:T(8,128)} %reshape_tile.8.seg_col_ref, s32[1,512]{1,0:T(1,128)} %reshape_tile.7.seg_row_ref, s32[512,1]{1,0:T(8,128)} %fusion.8.key_col_ref, s32[1,512]{1,0:T(1,128)} %fusion.13.key_row_ref, bf16[512,5120]{1,0:T(8,128)(2,1)} %reshape.265.q_ref.k_ref.v_ref.o_ref, ...), custom_call_target="tpu_custom_call" | custom-call | tf_op jit(solution)/shard_map/pallas_call | solution.py:67
  141.9 6.1 %reshape.266 = bf16[128,4,3072]{2,1,0:T(4,128)(2,1)} reshape(bf16[512,3072]{1,0:T(8,128)(2,1)} %shard_map.102) | data formatting | bytes 6291456 | tf_op jit(solution)/shard_map/reshape | solution.py:129
  148.1 12.4 %all-to-all-start.1 = ((bf16[128,4,3072]{2,1,0:T(4,128)(2,1)}), bf16[128,4,3072]{2,1,0:T(4,128)(2,1)S(1)}, u32[]{:S(2)}, u32[]{:S(2)}) async-start(bf16[128,4,3072]{2,1,0:T(4,128)(2,1)} %reshape.266), calls=%async_computation.1 | async-start | bytes 6291456 | tf_op jit(solution)/shard_map/all_to_all | solution.py:128
  160.4 0.1 copy.12
  160.5 0.1 reshape.295
  160.7 0.1 fusion.11
  160.8 41.4 %all-to-all-done.1 = bf16[128,4,3072]{2,1,0:T(4,128)(2,1)S(1)} async-done(((bf16[128,4,3072]{2,1,0:T(4,128)(2,1)}), bf16[128,4,3072]{2,1,0:T(4,128)(2,1)S(1)}, u32[]{:S(2)}, u32[]{:S(2)}) %all-to-all-start.1) | async-done | bytes 3145760 | tf_op jit(solution)/shard_map/all_to_all | solution.py:128
  202.3 2.4 reshape.288
  204.7 6.7 %scatter_custom_fusion = bf16[256,3072]{1,0:T(8,128)(2,1)S(1)} fusion(s32[512]{0:T(512)S(1)} %fusion.11, bf16[512,3072]{1,0:T(8,128)(2,1)} %reshape.288, bf16[]{:T(256)} %constant.123.clone.1), kind=kCustom, calls=%fused_computation.6 | custom fusion | bytes 1573376 | tf_op jit(solution)/shard_map/scatter | solution.py:135
  211.4 0.1 fusion.17
  211.6 0.0 copy-start.2
  211.6 1.8 broadcast_in_dim.31
  213.3 3.6 %all-to-all-start.2 = ((bf16[8,256,512]{2,1,0:T(8,128)(2,1)}), bf16[8,256,512]{2,1,0:T(8,128)(2,1)S(1)}, u32[]{:S(2)}, u32[]{:S(2)}) async-start(bf16[8,256,512]{2,1,0:T(8,128)(2,1)} %broadcast_in_dim.31), calls=%async_computation.2 | async-start | bytes 4194304 | tf_op jit(solution)/shard_map/all_to_all | solution.py:148
  217.0 27.0 %all-to-all-done.2 = bf16[8,256,512]{2,1,0:T(8,128)(2,1)S(1)} async-done(((bf16[8,256,512]{2,1,0:T(8,128)(2,1)}), bf16[8,256,512]{2,1,0:T(8,128)(2,1)S(1)}, u32[]{:S(2)}, u32[]{:S(2)}) %all-to-all-start.2) | async-done | bytes 2097184 | tf_op jit(solution)/shard_map/all_to_all | solution.py:148
  244.0 2.0 gather_fusion.1
  246.1 2.0 broadcast_select_fusion
  248.1 0.2 copy-done.3
  248.3 2.2 fusion.19
  250.5 3.8 %all-to-all-start.3 = ((f32[16,32,512]{2,1,0:T(8,128)}), f32[16,32,512]{2,1,0:T(8,128)S(1)}, u32[]{:S(2)}, u32[]{:S(2)}) async-start(f32[16,32,512]{2,1,0:T(8,128)} %fusion.19), calls=%async_computation.3 | async-start | bytes 2097152 | tf_op jit(solution)/shard_map/all_to_all | solution.py:153
  254.3 0.7 pad_maximum_fusion.2
  255.0 0.1 fusion.18
  255.1 1.1 pad_maximum_fusion.1
  256.2 15.8 %all-to-all-done.3 = f32[16,32,512]{2,1,0:T(8,128)S(1)} async-done(((f32[16,32,512]{2,1,0:T(8,128)}), f32[16,32,512]{2,1,0:T(8,128)S(1)}, u32[]{:S(2)}, u32[]{:S(2)}) %all-to-all-start.3) | async-done | bytes 1048608 | tf_op jit(solution)/shard_map/all_to_all | solution.py:153
  272.0 0.1 reduce_sum.9
  272.1 0.6 broadcast_multiply_fusion
  (12 shorter events, 0.1 us)
Async XLA Ops:
  17.8 92.6 %all-to-all-start = ((bf16[128,4,5120]{2,1,0:T(4,128)(2,1)}), bf16[128,4,5120]{2,1,0:T(4,128)(2,1)}, u32[]{:S(2)}, u32[]{:S(2)}) async-start(bf16[128,4,5120]{2,1,0:T(4,128)(2,1)} %reshape.269), calls=%async_computation | async-start | bytes 10485760 | tf_op jit(solution)/shard_map/all_to_all | solution.py:121
  32.9 10.5 %copy-start.4 = (s32[1,4]{1,0:T(1,128)S(1)}, s32[1,4]{1,0:T(1,128)}, u32[]{:S(2)}) copy-start(s32[1,4]{1,0:T(1,128)} %param.13) | copy-start | bytes 52
  34.0 59.7 %collective-permute-start = (bf16[256,16,32]{0,2,1:T(8,128)(2,1)}, bf16[256,16,32]{0,2,1:T(8,128)(2,1)S(1)}, u32[]{:S(2)}, u32[]{:S(2)}) collective-permute-start(bf16[256,16,32]{0,2,1:T(8,128)(2,1)} %get-tuple-element.14), channel_id=1, source_target_pairs={{0,1},{1,2},{2,3},{3,4},{4,5},{5,6},{6,7},{7,0},{8,9},{9,10},{10,1... | collective-permute-start | bytes 786440 | tf_op jit(solution)/shard_map/ppermute | solution.py:119
  34.0 61.0 %collective-permute-start.1 = (bf16[256,16,32]{0,2,1:T(8,128)(2,1)}, bf16[256,16,32]{0,2,1:T(8,128)(2,1)S(1)}, u32[]{:S(2)}, u32[]{:S(2)}) collective-permute-start(bf16[256,16,32]{0,2,1:T(8,128)(2,1)} %get-tuple-element.13), channel_id=1, source_target_pairs={{0,2},{1,3},{2,4},{3,5},{4,6},{5,7},{6,0},{7,1},{8,10},{9,11},{10,... | collective-permute-start | bytes 786440 | tf_op jit(solution)/shard_map/ppermute | solution.py:119
  35.1 69.8 %collective-permute-start.2 = (bf16[256,16,32]{0,2,1:T(8,128)(2,1)S(1)}, bf16[256,16,32]{0,2,1:T(8,128)(2,1)S(1)}, u32[]{:S(2)}, u32[]{:S(2)}) collective-permute-start(bf16[256,16,32]{0,2,1:T(8,128)(2,1)S(1)} %get-tuple-element.12), channel_id=1, source_target_pairs={{0,3},{1,4},{2,5},{3,6},{4,7},{5,0},{6,1},{7,2},{8,11},{9,12},{10,... | collective-permute-start | bytes 786440 | tf_op jit(solution)/shard_map/ppermute | solution.py:119
  37.6 68.7 %collective-permute-start.3 = (bf16[256,16,32]{0,2,1:T(8,128)(2,1)S(1)}, bf16[256,16,32]{0,2,1:T(8,128)(2,1)S(1)}, u32[]{:S(2)}, u32[]{:S(2)}) collective-permute-start(bf16[256,16,32]{0,2,1:T(8,128)(2,1)S(1)} %get-tuple-element.11), channel_id=1, source_target_pairs={{0,4},{1,5},{2,6},{3,7},{4,0},{5,1},{6,2},{7,3},{8,12},{9,13},{10,... | collective-permute-start | bytes 786440 | tf_op jit(solution)/shard_map/ppermute | solution.py:119
  39.1 68.8 %collective-permute-start.4 = (bf16[256,16,32]{0,2,1:T(8,128)(2,1)S(1)}, bf16[256,16,32]{0,2,1:T(8,128)(2,1)S(1)}, u32[]{:S(2)}, u32[]{:S(2)}) collective-permute-start(bf16[256,16,32]{0,2,1:T(8,128)(2,1)S(1)} %get-tuple-element.10), channel_id=1, source_target_pairs={{0,5},{1,6},{2,7},{3,0},{4,1},{5,2},{6,3},{7,4},{8,13},{9,14},{10,... | collective-permute-start | bytes 786440 | tf_op jit(solution)/shard_map/ppermute | solution.py:119
  93.7 15.0 %collective-permute-start.5 = (bf16[256,16,32]{0,2,1:T(8,128)(2,1)S(1)}, bf16[256,16,32]{0,2,1:T(8,128)(2,1)S(1)}, u32[]{:S(2)}, u32[]{:S(2)}) collective-permute-start(bf16[256,16,32]{0,2,1:T(8,128)(2,1)S(1)} %get-tuple-element.9), channel_id=1, source_target_pairs={{0,6},{1,7},{2,0},{3,1},{4,2},{5,3},{6,4},{7,5},{8,14},{9,15},{10,... | collective-permute-start | bytes 786440 | tf_op jit(solution)/shard_map/ppermute | solution.py:119
  95.0 14.7 %collective-permute-start.6 = (bf16[256,16,32]{0,2,1:T(8,128)(2,1)S(1)}, bf16[256,16,32]{0,2,1:T(8,128)(2,1)S(1)}, u32[]{:S(2)}, u32[]{:S(2)}) collective-permute-start(bf16[256,16,32]{0,2,1:T(8,128)(2,1)S(1)} %get-tuple-element.8), channel_id=1, source_target_pairs={{0,7},{1,0},{2,1},{3,2},{4,3},{5,4},{6,5},{7,6},{8,15},{9,8},{10,9... | collective-permute-start | bytes 786440 | tf_op jit(solution)/shard_map/ppermute | solution.py:119
  148.1 54.2 %all-to-all-start.1 = ((bf16[128,4,3072]{2,1,0:T(4,128)(2,1)}), bf16[128,4,3072]{2,1,0:T(4,128)(2,1)S(1)}, u32[]{:S(2)}, u32[]{:S(2)}) async-start(bf16[128,4,3072]{2,1,0:T(4,128)(2,1)} %reshape.266), calls=%async_computation.1 | async-start | bytes 6291456 | tf_op jit(solution)/shard_map/all_to_all | solution.py:128
  211.4 1.9 copy-start
  211.6 1.8 copy-start.2
  213.3 30.7 %all-to-all-start.2 = ((bf16[8,256,512]{2,1,0:T(8,128)(2,1)}), bf16[8,256,512]{2,1,0:T(8,128)(2,1)S(1)}, u32[]{:S(2)}, u32[]{:S(2)}) async-start(bf16[8,256,512]{2,1,0:T(8,128)(2,1)} %broadcast_in_dim.31), calls=%async_computation.2 | async-start | bytes 4194304 | tf_op jit(solution)/shard_map/all_to_all | solution.py:148
  246.1 2.2 copy-start.3
  250.5 4.5 %copy-start.1 = (bf16[256,3072]{1,0:T(8,128)(2,1)S(1)}, bf16[256,3072]{1,0:T(8,128)(2,1)}, u32[]{:S(2)}) copy-start(bf16[256,3072]{1,0:T(8,128)(2,1)} %copy-done) | copy-start | bytes 4718596
  250.5 21.5 %all-to-all-start.3 = ((f32[16,32,512]{2,1,0:T(8,128)}), f32[16,32,512]{2,1,0:T(8,128)S(1)}, u32[]{:S(2)}, u32[]{:S(2)}) async-start(f32[16,32,512]{2,1,0:T(8,128)} %fusion.19), calls=%async_computation.3 | async-start | bytes 2097152 | tf_op jit(solution)/shard_map/all_to_all | solution.py:153

commit v6 on v2

--- a/solution.py
+++ b/solution.py
@@ -25,10 +25,10 @@
     group_size = HQ // HK
     q_w = group_size * DH
     score_scale = 1.0 / math.sqrt(DH)
-    seg_col = seg_col_ref[...]
-    live_rows = seg_col >= 0
+    seg_row = seg_row_ref[...]
+    live_queries = seg_row >= 0
     allowed = (
-        (seg_col == seg_row_ref[...]) & (key_row_ref[...] <= key_col_ref[...]) & live_rows
+        (seg_col_ref[...] == seg_row) & (key_col_ref[...] <= key_row_ref[...]) & live_queries
     )
     k_group = k_ref[...]
     v_group = v_ref[...]
@@ -37,21 +37,24 @@
     for head in range(group_size):
         q_head = q_ref[:, head * DH : (head + 1) * DH]
         o_head = o_ref[:, head * DH : (head + 1) * DH]
-        scores = lax.dot_general(q_head, k_group, NT, preferred_element_type=jnp.float32)
+        scores = lax.dot_general(k_group, q_head, NT, preferred_element_type=jnp.float32)
         scores = jnp.where(allowed, scores * score_scale, jnp.float32(-1000000000.0))
-        row_max = jnp.max(scores, axis=1, keepdims=True)
-        weights = jnp.exp(scores - row_max)
-        attn_probs = weights * (1.0 / jnp.sum(weights, axis=1, keepdims=True))
-        attn_probs = jnp.where(live_rows, attn_probs, jnp.float32(0.0))
-        probs_b = attn_probs.astype(jnp.bfloat16)
-        dv_acc = dv_acc + lax.dot_general(probs_b, o_head, TN, preferred_element_type=jnp.float32)
-        dprob = lax.dot_general(o_head, v_group, NT, preferred_element_type=jnp.float32)
-        row_delta = jnp.sum(attn_probs * dprob, axis=1, keepdims=True)
+        col_max = jnp.max(scores, axis=0, keepdims=True)
+        weights = jnp.exp(scores - col_max)
+        scale_of = jnp.where(
+            live_queries, 1.0 / jnp.sum(weights, axis=0, keepdims=True), jnp.float32(0.0)
+        )
+        attn_probs = weights * scale_of
+        dv_acc = dv_acc + jnp.dot(
+            attn_probs.astype(jnp.bfloat16), o_head, preferred_element_type=jnp.float32
+        )
+        dprob = lax.dot_general(v_group, o_head, NT, preferred_element_type=jnp.float32)
+        row_delta = jnp.sum(attn_probs * dprob, axis=0, keepdims=True)
         dscore = (attn_probs * (dprob - row_delta) * score_scale).astype(jnp.bfloat16)
-        out_ref[:, head * DH : (head + 1) * DH] = jnp.dot(
-            dscore, k_group, preferred_element_type=jnp.float32
+        out_ref[:, head * DH : (head + 1) * DH] = lax.dot_general(
+            dscore, k_group, TN, preferred_element_type=jnp.float32
         ).astype(out_ref.dtype)
-        dk_acc = dk_acc + lax.dot_general(dscore, q_head, TN, preferred_element_type=jnp.float32)
+        dk_acc = dk_acc + jnp.dot(dscore, q_head, preferred_element_type=jnp.float32)
     out_ref[:, q_w : q_w + DH] = dk_acc.astype(out_ref.dtype)
     out_ref[:, q_w + DH : q_w + 2 * DH] = dv_acc.astype(out_ref.dtype)
 

time: 262 us -> 263 us (level)
  no operation moved by 1% of the time
where the time goes in v6:
time: 263 us; the launch traced here: 259 us
  waiting for transfers between devices  150 us (57%)
  local copies, waits for them, and re-layouts  47.7 us (18%)
  starting transfers between devices  24.6 us (9%)
  Pallas kernels  22.2 us (8%)
  other arithmetic  10.4 us (4%)
  matrix products  3.3 us (1%)
    all_to_all x1, waiting for transfers between devices, local(): rows_in = lax.all_to_all(table[pick_rows], DP, 0, 0, tiled=True)  61.3 us
    all_to_all x1, waiting for transfers between devices, local(): lax.all_to_all(partial, CHIP, 0, 0, tiled=True).sum(0) * grad_scale  53.8 us
    all_to_all x1, waiting for transfers between devices, local(): lax.all_to_all(rows_out.reshape(owners, slot_count, rows_out.shape[1]), D...  34.3 us
    pallas_call x1, Pallas kernels, attend_rows(): pl.pallas_call(attend_kernel, grid=(HK,), in_specs=[col, row, col, row, p...  22.2 us
    gather x2, local copies, waits for them, and re-layouts, local(): rows_in = lax.all_to_all(table[pick_rows], DP, 0, 0, tiled=True)  14.4 us
    all_to_all x1, starting transfers between devices, local(): rows_in = lax.all_to_all(table[pick_rows], DP, 0, 0, tiled=True)  11.6 us
    reshape x1, local copies, waits for them, and re-layouts, local(): rows_in = rows_in.reshape(owners * slot_count, table.shape[1])  8.91 us
    all_to_all x1, starting transfers between devices, local(): lax.all_to_all(rows_out.reshape(owners, slot_count, rows_out.shape[1]), D...  7.21 us
  transfers between devices with their start and end apart: 5, of which 4 were waited for; matrix products, arithmetic and copies ran while one was open for 9% of the time, Pallas kernels for 0%

profile of v6, /device:TPU:0, one launch (start us, length us, event | category | flops | bytes accessed | tf_op | source)
XLA Modules:
  0.0 258.5 jit_solution(1952279963154233425)
XLA Ops:
  0.6 0.7 compare_select_fusion.1
  1.3 0.1 copy.17
  1.4 0.1 reshape.176
  1.6 1.8 pad_maximum_fusion
  3.4 5.1 %gather_fusion = bf16[512,5120]{1,0:T(8,128)(2,1)} fusion(bf16[256,5120]{1,0:T(8,128)(2,1)S(1)} %pad_maximum_fusion, s32[1024]{0:T(1024)S(1)} %pad_clamp_fusion), kind=kCustom, calls=%fused_computation | custom fusion | bytes 10487808 | tf_op jit(solution)/shard_map/gather | solution.py:114
  8.5 9.3 %reshape.175 = bf16[128,4,5120]{2,1,0:T(4,128)(2,1)} reshape(bf16[512,5120]{1,0:T(8,128)(2,1)} %gather_fusion) | data formatting | bytes 10485760 | tf_op jit(solution)/shard_map/gather | solution.py:114
  17.8 0.0 copy-start.2
  17.8 11.6 %all-to-all-start = ((bf16[128,4,5120]{2,1,0:T(4,128)(2,1)}), bf16[128,4,5120]{2,1,0:T(4,128)(2,1)}, u32[]{:S(2)}, u32[]{:S(2)}) async-start(bf16[128,4,5120]{2,1,0:T(4,128)(2,1)} %reshape.175), calls=%async_computation | async-start | bytes 10485760 | tf_op jit(solution)/shard_map/all_to_all | solution.py:114
  29.4 0.0 copy-done.2
  29.5 0.8 reshape_tile.8.seg_col_ref
  30.3 0.7 reshape_tile.7.seg_row_ref
  31.0 0.6 fusion.22.key_row_ref
  31.6 0.8 fusion.17.key_col_ref
  32.3 61.3 %all-to-all-done = bf16[128,4,5120]{2,1,0:T(4,128)(2,1)} async-done(((bf16[128,4,5120]{2,1,0:T(4,128)(2,1)}), bf16[128,4,5120]{2,1,0:T(4,128)(2,1)}, u32[]{:S(2)}, u32[]{:S(2)}) %all-to-all-start) | async-done | bytes 5242912 | tf_op jit(solution)/shard_map/all_to_all | solution.py:114
  93.7 8.9 %reshape.170.q_ref.k_ref.v_ref.o_ref = bf16[512,5120]{1,0:T(8,128)(2,1)} reshape(bf16[128,4,5120]{2,1,0:T(4,128)(2,1)} %all-to-all-done) | data formatting | bytes 10485760 | tf_op jit(solution)/shard_map/reshape | solution.py:115
  102.6 22.2 %shard_map.102 = bf16[512,3072]{1,0:T(8,128)(2,1)} custom-call(s32[512,1]{1,0:T(8,128)} %reshape_tile.8.seg_col_ref, s32[1,512]{1,0:T(1,128)} %reshape_tile.7.seg_row_ref, s32[512,1]{1,0:T(8,128)} %fusion.17.key_col_ref, s32[1,512]{1,0:T(1,128)} %fusion.22.key_row_ref, bf16[512,5120]{1,0:T(8,128)(2,1)} %reshape.170.q_ref.k_ref.v_ref.o_ref, ...), custom_call_target="tpu_custom_call" | custom-call | tf_op jit(solution)/shard_map/pallas_call | solution.py:70
  124.8 6.1 %reshape.171 = bf16[128,4,3072]{2,1,0:T(4,128)(2,1)} reshape(bf16[512,3072]{1,0:T(8,128)(2,1)} %shard_map.102) | data formatting | bytes 6291456 | tf_op jit(solution)/shard_map/reshape | solution.py:121
  130.9 7.2 %all-to-all-start.1 = ((bf16[128,4,3072]{2,1,0:T(4,128)(2,1)}), bf16[128,4,3072]{2,1,0:T(4,128)(2,1)S(1)}, u32[]{:S(2)}, u32[]{:S(2)}) async-start(bf16[128,4,3072]{2,1,0:T(4,128)(2,1)} %reshape.171), calls=%async_computation.1 | async-start | bytes 6291456 | tf_op jit(solution)/shard_map/all_to_all | solution.py:120
  138.1 4.1 %copy.19 = bf16[256,4096]{0,1:T(8,128)(2,1)} copy(bf16[256,4096]{1,0:T(8,128)(2,1)} %param.7) | data formatting | bytes 4194304 | tf_op args[0]
  142.2 3.1 %constant_dynamic-slice_fusion = (bf16[256,64,1,32]{0,3,2,1:T(8,128)(2,1)}, bf16[256,64,32]{0,2,1:T(8,128)(2,1)}) fusion(bf16[256,64,2,32]{0,3,2,1:T(8,128)(2,1)} %bitcast.18, s32[]{:T(128)S(6)} %select_n.75, s32[]{:T(128)S(6)} %select_n.76), kind=kLoop, calls=%fused_computation.46 | loop fusion | bytes 4194312 | tf_op jit(solution)/shard_map/jit(dynamic_index_in_dim)/dynamic_slice | solution.py:142
  145.3 0.0 collective-permute-start
  145.3 0.1 copy.13
  145.4 0.1 reshape.193
  145.5 0.1 fusion.20
  145.7 34.3 %all-to-all-done.1 = bf16[128,4,3072]{2,1,0:T(4,128)(2,1)S(1)} async-done(((bf16[128,4,3072]{2,1,0:T(4,128)(2,1)}), bf16[128,4,3072]{2,1,0:T(4,128)(2,1)S(1)}, u32[]{:S(2)}, u32[]{:S(2)}) %all-to-all-start.1) | async-done | bytes 3145760 | tf_op jit(solution)/shard_map/all_to_all | solution.py:120
  179.9 2.4 reshape.186
  182.3 0.0 copy-start
  182.3 6.6 %scatter_custom_fusion = bf16[256,3072]{1,0:T(8,128)(2,1)S(1)} fusion(s32[512]{0:T(512)S(1)} %fusion.20, bf16[512,3072]{1,0:T(8,128)(2,1)} %reshape.186, bf16[]{:T(256)} %constant.51.clone.1), kind=kCustom, calls=%fused_computation.6 | custom fusion | bytes 1573376 | tf_op jit(solution)/shard_map/scatter | solution.py:127
  188.9 0.1 fusion.24
  189.1 0.0 copy-start.1
  189.1 0.1 collective-permute-start.1
  189.2 0.0 collective-permute-done
  189.2 0.0 copy-done
  189.2 1.4 pad_maximum_fusion.1
  190.6 0.1 collective-permute-done.1
  190.7 3.3 %fusion.2 = f32[64,32,512]{2,1,0:T(8,128)} fusion(bf16[64,32,512]{2,1,0:T(8,128)(2,1)S(1)} %bitcast.19, bf16[256,512]{1,0:T(8,128)(2,1)S(1)} %collective-permute-done.1, bf16[256,128]{1,0:T(8,128)(2,1)S(1)} %get-tuple-element.7, bf16[256,128]{1,0:T(8,128)(2,1)S(1)} %get-tuple-element.8, bf16[256,128]{1,0:T(8,128)(2,1)S(1)} %get-tuple-element.9, ...), kind=kOutput, calls=%fused_computation.10 | convolution fusion | flops 1076363264 | bytes 6815744 | tf_op jit(solution)/shard_map/td,tc->dc/dot_general | solution.py:147
  194.0 0.0 copy-done.1
  194.0 5.7 %all-to-all-start.2 = ((f32[64,32,512]{2,1,0:T(8,128)}), f32[64,32,512]{2,1,0:T(8,128)}, u32[]{:S(2)}, u32[]{:S(2)}) async-start(f32[64,32,512]{2,1,0:T(8,128)} %fusion.2), calls=%async_computation.2 | async-start | bytes 8388608 | tf_op jit(solution)/shard_map/all_to_all | solution.py:149
  199.7 0.7 pad_maximum_fusion.3
  200.4 0.1 fusion.25
  200.5 1.1 pad_maximum_fusion.2
  201.6 53.8 %all-to-all-done.2 = f32[64,32,512]{2,1,0:T(8,128)} async-done(((f32[64,32,512]{2,1,0:T(8,128)}), f32[64,32,512]{2,1,0:T(8,128)}, u32[]{:S(2)}, u32[]{:S(2)}) %all-to-all-start.2) | async-done | bytes 4194336 | tf_op jit(solution)/shard_map/all_to_all | solution.py:149
  255.4 2.5 reduce_sum.9
  257.9 0.6 broadcast_multiply_fusion
  (3 shorter events, 0.0 us)
Async XLA Ops:
  17.8 11.7 %copy-start.2 = (s32[1,4]{1,0:T(1,128)S(1)}, s32[1,4]{1,0:T(1,128)}, u32[]{:S(2)}) copy-start(s32[1,4]{1,0:T(1,128)} %param.13) | copy-start | bytes 52
  17.8 75.9 %all-to-all-start = ((bf16[128,4,5120]{2,1,0:T(4,128)(2,1)}), bf16[128,4,5120]{2,1,0:T(4,128)(2,1)}, u32[]{:S(2)}, u32[]{:S(2)}) async-start(bf16[128,4,5120]{2,1,0:T(4,128)(2,1)} %reshape.175), calls=%async_computation | async-start | bytes 10485760 | tf_op jit(solution)/shard_map/all_to_all | solution.py:114
  130.9 49.0 %all-to-all-start.1 = ((bf16[128,4,3072]{2,1,0:T(4,128)(2,1)}), bf16[128,4,3072]{2,1,0:T(4,128)(2,1)S(1)}, u32[]{:S(2)}, u32[]{:S(2)}) async-start(bf16[128,4,3072]{2,1,0:T(4,128)(2,1)} %reshape.171), calls=%async_computation.1 | async-start | bytes 6291456 | tf_op jit(solution)/shard_map/all_to_all | solution.py:120
  145.3 43.9 %collective-permute-start = (bf16[256,64,32]{0,2,1:T(8,128)(2,1)}, bf16[256,64,32]{0,2,1:T(8,128)(2,1)}, u32[]{:S(2)}, u32[]{:S(2)}) collective-permute-start(bf16[256,64,32]{0,2,1:T(8,128)(2,1)} %get-tuple-element.5), channel_id=1, source_target_pairs={{0,1},{1,0},{2,3},{3,2},{4,5},{5,4},{6,7},{7,6},{8,9},{9,8},{10,11... | collective-permute-start | bytes 3145736 | tf_op jit(solution)/shard_map/ppermute | solution.py:144
  182.3 6.9 %copy-start = (bf16[256,64,1,32]{0,3,2,1:T(8,128)(2,1)S(1)}, bf16[256,64,1,32]{0,3,2,1:T(8,128)(2,1)}, u32[]{:S(2)}) copy-start(bf16[256,64,1,32]{0,3,2,1:T(8,128)(2,1)} %get-tuple-element.4) | copy-start | bytes 3145732
  189.1 4.9 %copy-start.1 = (bf16[256,512]{1,0:T(8,128)(2,1)}, bf16[256,512]{1,0:T(8,128)(2,1)S(1)}, u32[]{:S(2)}) copy-start(bf16[256,512]{1,0:T(8,128)(2,1)S(1)} %pad_maximum_fusion.4) | copy-start | bytes 786436
  189.1 1.6 collective-permute-start.1
  194.0 61.4 %all-to-all-start.2 = ((f32[64,32,512]{2,1,0:T(8,128)}), f32[64,32,512]{2,1,0:T(8,128)}, u32[]{:S(2)}, u32[]{:S(2)}) async-start(f32[64,32,512]{2,1,0:T(8,128)} %fusion.2), calls=%async_computation.2 | async-start | bytes 8388608 | tf_op jit(solution)/shard_map/all_to_all | solution.py:149

commit v7 on v6

--- a/solution.py
+++ b/solution.py
@@ -121,11 +121,12 @@
         rows_out.reshape(owners, slot_count, rows_out.shape[1]), DP, 0, 0, tiled=True
     )
     targets = jnp.where(live_send, pick_rows, tok_rows).reshape(-1)
-    home = (
-        jnp.zeros((tok_rows, back.shape[2]), back.dtype)
+    slot_of_row = (
+        jnp.zeros((tok_rows,), jnp.int32)
         .at[targets]
-        .set(back.reshape(owners * slot_count, back.shape[2]), mode="drop")
+        .set(jnp.arange(owners * slot_count, dtype=jnp.int32), mode="drop")
     )
+    home = back.reshape(owners * slot_count, back.shape[2])[slot_of_row]
     out_w = q_w + 2 * DH
     grad_queries = jnp.concatenate(
         [home[:, g * out_w : g * out_w + q_w] for g in range(HK)], axis=1

time: 263 us -> 263 us (level)
    scatter x1, local copies, waits for them, and re-layouts: 6.6 us -> 2.62 us  [local(): slot_of_row = jnp.zeros((tok_rows,), jnp.int32).at[targets].set(jnp.arang...]
    gather x0 -> x1, local copies, waits for them, and re-layouts: none -> 2.77 us  [local(): home = back.reshape(owners * slot_count, back.shape[2])[slot_of_row]]
  transfers between devices with their start and end apart: 5 -> 5, of which waited for: 4 -> 3; matrix products, arithmetic and copies ran while one was open for 9% -> 9% of each run, Pallas kernels for 0% -> 0%
where the time goes in v7:
time: 263 us; the launch traced here: 261 us
  waiting for transfers between devices  151 us (57%)
  local copies, waits for them, and re-layouts  47.3 us (18%)
  starting transfers between devices  25.2 us (10%)
  Pallas kernels  22.2 us (8%)
  other arithmetic  10.7 us (4%)
  matrix products  3.3 us (1%)
    all_to_all x1, waiting for transfers between devices, local(): rows_in = lax.all_to_all(table[pick_rows], DP, 0, 0, tiled=True)  61.3 us
    all_to_all x1, waiting for transfers between devices, local(): lax.all_to_all(partial, CHIP, 0, 0, tiled=True).sum(0) * grad_scale  56.1 us
    all_to_all x1, waiting for transfers between devices, local(): lax.all_to_all(rows_out.reshape(owners, slot_count, rows_out.shape[1]), D...  33.6 us
    pallas_call x1, Pallas kernels, attend_rows(): pl.pallas_call(attend_kernel, grid=(HK,), in_specs=[col, row, col, row, p...  22.2 us
    gather x2, local copies, waits for them, and re-layouts, local(): rows_in = lax.all_to_all(table[pick_rows], DP, 0, 0, tiled=True)  14.4 us
    all_to_all x1, starting transfers between devices, local(): rows_in = lax.all_to_all(table[pick_rows], DP, 0, 0, tiled=True)  11.6 us
    reshape x1, local copies, waits for them, and re-layouts, local(): rows_in = rows_in.reshape(owners * slot_count, table.shape[1])  8.91 us
    all_to_all x1, starting transfers between devices, local(): lax.all_to_all(rows_out.reshape(owners, slot_count, rows_out.shape[1]), D...  7.68 us
  transfers between devices with their start and end apart: 5, of which 3 were waited for; matrix products, arithmetic and copies ran while one was open for 9% of the time, Pallas kernels for 0%

profile of v7, /device:TPU:0, one launch (start us, length us, event | category | flops | bytes accessed | tf_op | source)
XLA Modules:
  0.0 260.6 jit_solution(924338341630203246)
XLA Ops:
  0.6 0.7 bitcast_select_fusion
  1.3 0.1 copy.13
  1.4 0.1 reshape.176
  1.6 1.8 pad_maximum_fusion
  3.4 5.1 %gather_fusion = bf16[512,5120]{1,0:T(8,128)(2,1)} fusion(bf16[256,5120]{1,0:T(8,128)(2,1)S(1)} %pad_maximum_fusion, s32[1024]{0:T(1024)S(1)} %pad_clamp_fusion.1), kind=kCustom, calls=%fused_computation | custom fusion | bytes 10487808 | tf_op jit(solution)/shard_map/gather | solution.py:114
  8.5 9.3 %reshape.175 = bf16[128,4,5120]{2,1,0:T(4,128)(2,1)} reshape(bf16[512,5120]{1,0:T(8,128)(2,1)} %gather_fusion) | data formatting | bytes 10485760 | tf_op jit(solution)/shard_map/gather | solution.py:114
  17.8 0.0 copy-start.2
  17.8 11.6 %all-to-all-start = ((bf16[128,4,5120]{2,1,0:T(4,128)(2,1)}), bf16[128,4,5120]{2,1,0:T(4,128)(2,1)}, u32[]{:S(2)}, u32[]{:S(2)}) async-start(bf16[128,4,5120]{2,1,0:T(4,128)(2,1)} %reshape.175), calls=%async_computation | async-start | bytes 10485760 | tf_op jit(solution)/shard_map/all_to_all | solution.py:114
  29.4 0.0 copy-done.2
  29.5 0.8 reshape_tile.8.seg_col_ref
  30.3 0.7 reshape_tile.7.seg_row_ref
  31.0 0.6 fusion.20.key_row_ref
  31.6 0.8 fusion.15.key_col_ref
  32.3 61.3 %all-to-all-done = bf16[128,4,5120]{2,1,0:T(4,128)(2,1)} async-done(((bf16[128,4,5120]{2,1,0:T(4,128)(2,1)}), bf16[128,4,5120]{2,1,0:T(4,128)(2,1)}, u32[]{:S(2)}, u32[]{:S(2)}) %all-to-all-start) | async-done | bytes 5242912 | tf_op jit(solution)/shard_map/all_to_all | solution.py:114
  93.7 8.9 %reshape.169.q_ref.k_ref.v_ref.o_ref = bf16[512,5120]{1,0:T(8,128)(2,1)} reshape(bf16[128,4,5120]{2,1,0:T(4,128)(2,1)} %all-to-all-done) | data formatting | bytes 10485760 | tf_op jit(solution)/shard_map/reshape | solution.py:115
  102.6 22.2 %shard_map.102 = bf16[512,3072]{1,0:T(8,128)(2,1)} custom-call(s32[512,1]{1,0:T(8,128)} %reshape_tile.8.seg_col_ref, s32[1,512]{1,0:T(1,128)} %reshape_tile.7.seg_row_ref, s32[512,1]{1,0:T(8,128)} %fusion.15.key_col_ref, s32[1,512]{1,0:T(1,128)} %fusion.20.key_row_ref, bf16[512,5120]{1,0:T(8,128)(2,1)} %reshape.169.q_ref.k_ref.v_ref.o_ref, ...), custom_call_target="tpu_custom_call" | custom-call | tf_op jit(solution)/shard_map/pallas_call | solution.py:70
  124.8 6.1 %reshape.170 = bf16[128,4,3072]{2,1,0:T(4,128)(2,1)} reshape(bf16[512,3072]{1,0:T(8,128)(2,1)} %shard_map.102) | data formatting | bytes 6291456 | tf_op jit(solution)/shard_map/reshape | solution.py:121
  130.9 7.7 %all-to-all-start.1 = ((bf16[128,4,3072]{2,1,0:T(4,128)(2,1)}), bf16[128,4,3072]{2,1,0:T(4,128)(2,1)}, u32[]{:S(2)}, u32[]{:S(2)}) async-start(bf16[128,4,3072]{2,1,0:T(4,128)(2,1)} %reshape.170), calls=%async_computation.1 | async-start | bytes 6291456 | tf_op jit(solution)/shard_map/all_to_all | solution.py:120
  138.6 3.3 %copy.19 = bf16[256,4096]{0,1:T(8,128)(2,1)S(1)} copy(bf16[256,4096]{1,0:T(8,128)(2,1)} %param.7) | data formatting | bytes 4194304 | tf_op args[0]
  141.9 1.6 constant_dynamic-slice_fusion
  143.4 0.0 collective-permute-start
  143.4 0.1 copy.15
  143.5 0.1 reshape.202
  143.7 0.1 fusion.18
  143.8 2.6 %scatter_custom_fusion = s32[256]{0:T(256)S(1)} fusion(s32[512]{0:T(512)S(1)} %fusion.18, s32[512]{0:T(512)S(1)} %iota.12, s32[]{:T(128)} %constant.53.clone.1), kind=kCustom, calls=%fused_computation.47 | custom fusion | bytes 1028 | tf_op jit(solution)/shard_map/scatter | solution.py:127
  146.5 33.6 %all-to-all-done.1 = bf16[128,4,3072]{2,1,0:T(4,128)(2,1)} async-done(((bf16[128,4,3072]{2,1,0:T(4,128)(2,1)}), bf16[128,4,3072]{2,1,0:T(4,128)(2,1)}, u32[]{:S(2)}, u32[]{:S(2)}) %all-to-all-start.1) | async-done | bytes 3145760 | tf_op jit(solution)/shard_map/all_to_all | solution.py:120
  180.0 4.5 %reshape.171 = bf16[512,3072]{1,0:T(8,128)(2,1)S(1)} reshape(bf16[128,4,3072]{2,1,0:T(4,128)(2,1)} %all-to-all-done.1) | data formatting | bytes 6291456 | tf_op jit(solution)/shard_map/reshape | solution.py:129
  184.5 2.8 %gather_fusion.1 = bf16[256,3072]{1,0:T(8,128)(2,1)} fusion(bf16[512,3072]{1,0:T(8,128)(2,1)S(1)} %reshape.171, s32[1024]{0:T(1024)S(1)} %pad_clamp_fusion), kind=kCustom, calls=%fused_computation.1 | custom fusion | bytes 3146752 | tf_op jit(solution)/shard_map/gather | solution.py:129
  187.3 1.1 fusion.24
  188.5 0.0 copy-start.1
  188.5 0.1 collective-permute-start.1
  188.6 0.0 collective-permute-done
  188.6 1.7 pad_maximum_fusion.1
  190.3 0.0 collective-permute-done.1
  190.3 3.3 %fusion = f32[64,32,512]{2,1,0:T(8,128)} fusion(bf16[64,32,512]{2,1,0:T(8,128)(2,1)S(1)} %bitcast.19, bf16[256,512]{1,0:T(8,128)(2,1)S(1)} %collective-permute-done.1, bf16[256,128]{1,0:T(8,128)(2,1)S(1)} %get-tuple-element.13, bf16[256,128]{1,0:T(8,128)(2,1)S(1)} %get-tuple-element.7, bf16[256,128]{1,0:T(8,128)(2,1)S(1)} %get-tuple-element.8, ...), kind=kOutput, calls=%fused_computation.9 | convolution fusion | flops 1076363264 | bytes 6815744 | tf_op jit(solution)/shard_map/td,tc->dc/dot_general | solution.py:148
  193.6 0.0 copy-done.1
  193.6 0.0 copy-start
  193.6 5.8 %all-to-all-start.2 = ((f32[64,32,512]{2,1,0:T(8,128)}), f32[64,32,512]{2,1,0:T(8,128)}, u32[]{:S(2)}, u32[]{:S(2)}) async-start(f32[64,32,512]{2,1,0:T(8,128)} %fusion), calls=%async_computation.2 | async-start | bytes 8388608 | tf_op jit(solution)/shard_map/all_to_all | solution.py:150
  199.4 0.7 pad_maximum_fusion.3
  200.1 0.0 copy-done
  200.1 0.1 fusion.25
  200.2 1.1 pad_maximum_fusion.2
  201.3 56.1 %all-to-all-done.2 = f32[64,32,512]{2,1,0:T(8,128)} async-done(((f32[64,32,512]{2,1,0:T(8,128)}), f32[64,32,512]{2,1,0:T(8,128)}, u32[]{:S(2)}, u32[]{:S(2)}) %all-to-all-start.2) | async-done | bytes 4194336 | tf_op jit(solution)/shard_map/all_to_all | solution.py:150
  257.5 2.5 reduce_sum.9
  259.9 0.6 broadcast_multiply_fusion
  (6 shorter events, 0.1 us)
Async XLA Ops:
  17.8 11.7 %copy-start.2 = (s32[1,4]{1,0:T(1,128)S(1)}, s32[1,4]{1,0:T(1,128)}, u32[]{:S(2)}) copy-start(s32[1,4]{1,0:T(1,128)} %param.13) | copy-start | bytes 52
  17.8 75.9 %all-to-all-start = ((bf16[128,4,5120]{2,1,0:T(4,128)(2,1)}), bf16[128,4,5120]{2,1,0:T(4,128)(2,1)}, u32[]{:S(2)}, u32[]{:S(2)}) async-start(bf16[128,4,5120]{2,1,0:T(4,128)(2,1)} %reshape.175), calls=%async_computation | async-start | bytes 10485760 | tf_op jit(solution)/shard_map/all_to_all | solution.py:114
  130.9 49.1 %all-to-all-start.1 = ((bf16[128,4,3072]{2,1,0:T(4,128)(2,1)}), bf16[128,4,3072]{2,1,0:T(4,128)(2,1)}, u32[]{:S(2)}, u32[]{:S(2)}) async-start(bf16[128,4,3072]{2,1,0:T(4,128)(2,1)} %reshape.170), calls=%async_computation.1 | async-start | bytes 6291456 | tf_op jit(solution)/shard_map/all_to_all | solution.py:120
  143.4 45.1 %collective-permute-start = (bf16[256,64,32]{0,2,1:T(8,128)(2,1)}, bf16[256,64,32]{0,2,1:T(8,128)(2,1)}, u32[]{:S(2)}, u32[]{:S(2)}) collective-permute-start(bf16[256,64,32]{0,2,1:T(8,128)(2,1)} %get-tuple-element.5), channel_id=1, source_target_pairs={{0,1},{1,0},{2,3},{3,2},{4,5},{5,4},{6,7},{7,6},{8,9},{9,8},{10,11... | collective-permute-start | bytes 3145736 | tf_op jit(solution)/shard_map/ppermute | solution.py:145
  188.5 5.1 %copy-start.1 = (bf16[256,512]{1,0:T(8,128)(2,1)}, bf16[256,512]{1,0:T(8,128)(2,1)S(1)}, u32[]{:S(2)}) copy-start(bf16[256,512]{1,0:T(8,128)(2,1)S(1)} %pad_maximum_fusion.4) | copy-start | bytes 786436
  188.5 1.8 collective-permute-start.1
  193.6 6.5 %copy-start = (bf16[256,3072]{1,0:T(8,128)(2,1)S(1)}, bf16[256,3072]{1,0:T(8,128)(2,1)}, u32[]{:S(2)}) copy-start(bf16[256,3072]{1,0:T(8,128)(2,1)} %gather_fusion.1) | copy-start | bytes 4718596
  193.6 63.9 %all-to-all-start.2 = ((f32[64,32,512]{2,1,0:T(8,128)}), f32[64,32,512]{2,1,0:T(8,128)}, u32[]{:S(2)}, u32[]{:S(2)}) async-start(f32[64,32,512]{2,1,0:T(8,128)} %fusion), calls=%async_computation.2 | async-start | bytes 8388608 | tf_op jit(solution)/shard_map/all_to_all | solution.py:150

commit v8 on v6

--- a/solution.py
+++ b/solution.py
@@ -59,17 +59,17 @@
     out_ref[:, q_w + DH : q_w + 2 * DH] = dv_acc.astype(out_ref.dtype)
 
 
-def attend_rows(rows_in, segment, order_key):
+def attend_rows(rows_in, segment, order_key, n_kv):
     row_count = rows_in.shape[0]
     q_w = (HQ // HK) * DH
     out_w = q_w + 2 * DH
-    k_at, v_at, o_at = HK * q_w // DH, HK * q_w // DH + HK, (HK * q_w + 2 * HK * DH) // q_w
+    k_at, v_at, o_at = n_kv * q_w // DH, n_kv * q_w // DH + n_kv, (n_kv + 2 * n_kv * DH // q_w)
     whole = lambda g: (0, 0)
     col = pl.BlockSpec((row_count, 1), whole)
     row = pl.BlockSpec((1, row_count), whole)
     return pl.pallas_call(
         attend_kernel,
-        grid=(HK,),
+        grid=(n_kv,),
         in_specs=[
             col,
             row,
@@ -81,7 +81,7 @@
             pl.BlockSpec((row_count, q_w), lambda g: (0, o_at + g)),
         ],
         out_specs=pl.BlockSpec((row_count, out_w), lambda g: (0, g)),
-        out_shape=jax.ShapeDtypeStruct((row_count, HK * out_w), jnp.bfloat16),
+        out_shape=jax.ShapeDtypeStruct((row_count, n_kv * out_w), jnp.bfloat16),
         compiler_params=pltpu.CompilerParams(dimension_semantics=("arbitrary",)),
         interpret=INTERPRET,
     )(
@@ -98,6 +98,7 @@
 
 CHIP, CORE = "chip", "core"
 DP = (CHIP, CORE)
+PARTS = 2
 
 
 def local(hidden_in, queries, keys, values, grad_attn, send_rows, slot_docs):
@@ -110,32 +111,11 @@
     live_send = (send_rows >= 0).T
     pick_rows = jnp.maximum(send_rows, 0).T
     grad_scale = 1.0 / math.sqrt(tok_rows * owners)
-    table = jnp.concatenate((queries, keys, values, grad_attn), axis=1)
-    rows_in = lax.all_to_all(table[pick_rows], DP, 0, 0, tiled=True)
-    rows_in = rows_in.reshape(owners * slot_count, table.shape[1])
     row_ids = jnp.arange(owners * slot_count, dtype=jnp.int32)
     order_key = (row_ids % slot_count) * owners + row_ids // slot_count
     segment = jnp.tile(slot_docs[0].astype(jnp.int32), owners)
-    rows_out = attend_rows(rows_in, segment, order_key)
-    back = lax.all_to_all(
-        rows_out.reshape(owners, slot_count, rows_out.shape[1]), DP, 0, 0, tiled=True
-    )
     targets = jnp.where(live_send, pick_rows, tok_rows).reshape(-1)
-    home = (
-        jnp.zeros((tok_rows, back.shape[2]), back.dtype)
-        .at[targets]
-        .set(back.reshape(owners * slot_count, back.shape[2]), mode="drop")
-    )
     out_w = q_w + 2 * DH
-    grad_queries = jnp.concatenate(
-        [home[:, g * out_w : g * out_w + q_w] for g in range(HK)], axis=1
-    )
-    grad_keys = jnp.concatenate(
-        [home[:, g * out_w + q_w : g * out_w + q_w + DH] for g in range(HK)], axis=1
-    )
-    grad_values = jnp.concatenate(
-        [home[:, g * out_w + q_w + DH : (g + 1) * out_w] for g in range(HK)], axis=1
-    )
     core = lax.axis_index(CORE)
     swap = [(0, 1), (1, 0)]
     blocks = hidden_in.reshape(tok_rows, chips, cores, -1)
@@ -143,10 +123,41 @@
     theirs = lax.dynamic_index_in_dim(blocks, 1 - core, axis=2, keepdims=False)
     from_partner = lax.ppermute(theirs, CORE, swap)
     hidden_pair = jnp.concatenate((mine, from_partner), axis=0).reshape(2 * tok_rows, -1)
-    grad_pair = jnp.concatenate((grad_values, lax.ppermute(grad_values, CORE, swap)), axis=0)
-    partial = jnp.einsum("td,tc->dc", hidden_pair, grad_pair, preferred_element_type=jnp.float32)
-    partial = partial.reshape(chips, partial.shape[0] // chips, partial.shape[1])
-    grad_wv = lax.all_to_all(partial, CHIP, 0, 0, tiled=True).sum(0) * grad_scale
+    n_kv = HK // PARTS
+    dq_parts, dk_parts, dv_parts, wv_parts = [], [], [], []
+    for part in range(PARTS):
+        q_cols = slice(part * n_kv * q_w, (part + 1) * n_kv * q_w)
+        kv_cols = slice(part * n_kv * DH, (part + 1) * n_kv * DH)
+        table = jnp.concatenate(
+            (queries[:, q_cols], keys[:, kv_cols], values[:, kv_cols], grad_attn[:, q_cols]), axis=1
+        )
+        rows_in = lax.all_to_all(table[pick_rows], DP, 0, 0, tiled=True)
+        rows_in = rows_in.reshape(owners * slot_count, table.shape[1])
+        rows_out = attend_rows(rows_in, segment, order_key, n_kv)
+        back = lax.all_to_all(
+            rows_out.reshape(owners, slot_count, rows_out.shape[1]), DP, 0, 0, tiled=True
+        )
+        home = (
+            jnp.zeros((tok_rows, back.shape[2]), back.dtype)
+            .at[targets]
+            .set(back.reshape(owners * slot_count, back.shape[2]), mode="drop")
+        )
+        dq_parts += [home[:, g * out_w : g * out_w + q_w] for g in range(n_kv)]
+        dk_parts += [home[:, g * out_w + q_w : g * out_w + q_w + DH] for g in range(n_kv)]
+        dv_part = jnp.concatenate(
+            [home[:, g * out_w + q_w + DH : (g + 1) * out_w] for g in range(n_kv)], axis=1
+        )
+        dv_parts.append(dv_part)
+        grad_pair = jnp.concatenate((dv_part, lax.ppermute(dv_part, CORE, swap)), axis=0)
+        partial = jnp.einsum(
+            "td,tc->dc", hidden_pair, grad_pair, preferred_element_type=jnp.float32
+        )
+        partial = partial.reshape(chips, partial.shape[0] // chips, partial.shape[1])
+        wv_parts.append(lax.all_to_all(partial, CHIP, 0, 0, tiled=True).sum(0) * grad_scale)
+    grad_queries = jnp.concatenate(dq_parts, axis=1)
+    grad_keys = jnp.concatenate(dk_parts, axis=1)
+    grad_values = jnp.concatenate(dv_parts, axis=1)
+    grad_wv = jnp.concatenate(wv_parts, axis=1)
     return (grad_queries, grad_keys, grad_values, grad_wv)
 
 

time: 263 us -> 242 us (0.920); the launches traced: 259 us -> 241 us
  waiting for transfers between devices: 150 us -> 95 us
  starting transfers between devices: 24.6 us -> 43.7 us
  local copies, waits for them, and re-layouts: 47.7 us -> 62.4 us
    all_to_all x1 -> x2, waiting for transfers between devices: 61.3 us -> 38.7 us  [local(): rows_in = lax.all_to_all(table[pick_rows], DP, 0, 0, tiled=True)]
    all_to_all x1 -> x2, waiting for transfers between devices: 34.3 us -> 12.2 us  [local(): lax.all_to_all(rows_out.reshape(owners, slot_count, rows_out.shape[1]), D...]
    all_to_all x1 -> x2, waiting for transfers between devices: 53.8 us -> 42.8 us  [local(): lax.all_to_all(partial, CHIP, 0, 0, tiled=True).sum(0) * grad_scale]
    all_to_all x1 -> x2, starting transfers between devices: 7.21 us -> 16.2 us  [local(): lax.all_to_all(rows_out.reshape(owners, slot_count, rows_out.shape[1]), D...]
    all_to_all x1 -> x2, starting transfers between devices: 5.66 us -> 10.8 us  [local(): lax.all_to_all(partial, CHIP, 0, 0, tiled=True).sum(0) * grad_scale]
    reshape x1 -> x2, local copies, waits for them, and re-layouts: 2.39 us -> 7.51 us  [local(): back.reshape(owners * slot_count, back.shape[2])]
    all_to_all x1 -> x2, starting transfers between devices: 11.6 us -> 16.3 us  [local(): rows_in = lax.all_to_all(table[pick_rows], DP, 0, 0, tiled=True)]
    slice x1 -> x6, local copies, waits for them, and re-layouts: 0.08 us -> 3.9 us  [the longest x1 2.06 us: local(): grad_attn[:, q_cols]]
  transfers between devices with their start and end apart: 5 -> 9, of which waited for: 4 -> 6; matrix products, arithmetic and copies ran while one was open for 9% -> 25% of each run, Pallas kernels for 0% -> 10%
where the time goes in v8:
time: 242 us; the launch traced here: 241 us
  waiting for transfers between devices  95 us (39%)
  local copies, waits for them, and re-layouts  62.4 us (26%)
  starting transfers between devices  43.7 us (18%)
  Pallas kernels  24.6 us (10%)
  other arithmetic  10.3 us (4%)
  matrix products  4.07 us (2%)
    all_to_all x2, waiting for transfers between devices, local(): lax.all_to_all(partial, CHIP, 0, 0, tiled=True).sum(0) * grad_scale  42.8 us
    all_to_all x2, waiting for transfers between devices, local(): rows_in = lax.all_to_all(table[pick_rows], DP, 0, 0, tiled=True)  38.7 us
    pallas_call x2, Pallas kernels, attend_rows(): pl.pallas_call(attend_kernel, grid=(n_kv,), in_specs=[col, row, col, row,...  24.6 us
    gather x4, local copies, waits for them, and re-layouts, local(): rows_in = lax.all_to_all(table[pick_rows], DP, 0, 0, tiled=True)  18 us
    all_to_all x2, starting transfers between devices, local(): rows_in = lax.all_to_all(table[pick_rows], DP, 0, 0, tiled=True)  16.3 us
    all_to_all x2, starting transfers between devices, local(): lax.all_to_all(rows_out.reshape(owners, slot_count, rows_out.shape[1]), D...  16.2 us
    all_to_all x2, waiting for transfers between devices, local(): lax.all_to_all(rows_out.reshape(owners, slot_count, rows_out.shape[1]), D...  12.2 us
    all_to_all x2, starting transfers between devices, local(): lax.all_to_all(partial, CHIP, 0, 0, tiled=True).sum(0) * grad_scale  10.8 us
  transfers between devices with their start and end apart: 9, of which 6 were waited for; matrix products, arithmetic and copies ran while one was open for 25% of the time, Pallas kernels for 10%

profile of v8, /device:TPU:0, one launch (start us, length us, event | category | flops | bytes accessed | tf_op | source)
XLA Modules:
  0.0 240.9 jit_solution(2595182673669631748)
XLA Ops:
  0.7 0.8 compare_select_fusion.1
  1.5 2.1 fusion.29
  3.5 0.0 copy-done.6
  3.6 0.7 fusion.34
  4.2 0.0 copy-done.5
  4.2 1.1 fusion.28
  5.3 0.1 copy.17
  5.4 0.1 reshape.192
  5.5 1.5 pad_maximum_fusion.1
  7.1 3.5 %gather_fusion.1 = bf16[512,2560]{1,0:T(8,128)(2,1)} fusion(bf16[256,2560]{1,0:T(8,128)(2,1)S(1)} %get-tuple-element.29, s32[1024]{0:T(1024)S(1)} %pad_clamp_fusion), kind=kCustom, calls=%fused_computation.1 | custom fusion | bytes 5244928 | tf_op jit(solution)/shard_map/gather | solution.py:134
  10.6 5.5 %reshape.199 = bf16[128,4,2560]{2,1,0:T(4,128)(2,1)} reshape(bf16[512,2560]{1,0:T(8,128)(2,1)} %gather_fusion.1) | data formatting | bytes 5242880 | tf_op jit(solution)/shard_map/gather | solution.py:134
  16.1 11.6 %all-to-all-start.2 = ((bf16[128,4,2560]{2,1,0:T(4,128)(2,1)}), bf16[128,4,2560]{2,1,0:T(4,128)(2,1)}, u32[]{:S(2)}, u32[]{:S(2)}) async-start(bf16[128,4,2560]{2,1,0:T(4,128)(2,1)} %reshape.199), calls=%async_computation.2 | async-start | bytes 5242880 | tf_op jit(solution)/shard_map/all_to_all | solution.py:134
  27.7 3.5 %gather_fusion = bf16[512,2560]{1,0:T(8,128)(2,1)} fusion(bf16[256,2560]{1,0:T(8,128)(2,1)S(1)} %get-tuple-element.28, s32[1024]{0:T(1024)S(1)} %pad_clamp_fusion), kind=kCustom, calls=%fused_computation | custom fusion | bytes 5244928 | tf_op jit(solution)/shard_map/gather | solution.py:134
  31.2 5.5 %reshape.191 = bf16[128,4,2560]{2,1,0:T(4,128)(2,1)} reshape(bf16[512,2560]{1,0:T(8,128)(2,1)} %gather_fusion) | data formatting | bytes 5242880 | tf_op jit(solution)/shard_map/gather | solution.py:134
  36.8 26.8 %all-to-all-done.2 = bf16[128,4,2560]{2,1,0:T(4,128)(2,1)} async-done(((bf16[128,4,2560]{2,1,0:T(4,128)(2,1)}), bf16[128,4,2560]{2,1,0:T(4,128)(2,1)}, u32[]{:S(2)}, u32[]{:S(2)}) %all-to-all-start.2) | async-done | bytes 2621472 | tf_op jit(solution)/shard_map/all_to_all | solution.py:134
  63.6 4.7 %all-to-all-start = ((bf16[128,4,2560]{2,1,0:T(4,128)(2,1)}), bf16[128,4,2560]{2,1,0:T(4,128)(2,1)S(1)}, u32[]{:S(2)}, u32[]{:S(2)}) async-start(bf16[128,4,2560]{2,1,0:T(4,128)(2,1)} %reshape.191), calls=%async_computation | async-start | bytes 5242880 | tf_op jit(solution)/shard_map/all_to_all | solution.py:134
  68.2 0.0 copy-done.8
  68.3 0.8 reshape_tile.10.seg_col_ref
  69.1 0.7 reshape_tile.9.seg_row_ref
  69.8 0.6 fusion.25.key_row_ref
  70.4 0.8 fusion.10.key_col_ref
  71.1 5.3 %reshape.186.q_ref.k_ref.v_ref.o_ref = bf16[512,2560]{1,0:T(8,128)(2,1)} reshape(bf16[128,4,2560]{2,1,0:T(4,128)(2,1)} %all-to-all-done.2) | data formatting | bytes 5242880 | tf_op jit(solution)/shard_map/reshape | solution.py:135
  76.4 12.3 %shard_map.103 = bf16[512,1536]{1,0:T(8,128)(2,1)} custom-call(s32[512,1]{1,0:T(8,128)} %reshape_tile.10.seg_col_ref, s32[1,512]{1,0:T(1,128)} %reshape_tile.9.seg_row_ref, s32[512,1]{1,0:T(8,128)} %fusion.10.key_col_ref, s32[1,512]{1,0:T(1,128)} %fusion.25.key_row_ref, bf16[512,2560]{1,0:T(8,128)(2,1)} %reshape.186.q_ref.k_ref.v_ref.o_ref, ...), custom_call_target="tpu_custom_call" | custom-call | tf_op jit(solution)/shard_map/pallas_call | solution.py:70
  88.7 3.9 %reshape.187 = bf16[128,4,1536]{2,1,0:T(4,128)(2,1)} reshape(bf16[512,1536]{1,0:T(8,128)(2,1)} %shard_map.103) | data formatting | bytes 3145728 | tf_op jit(solution)/shard_map/reshape | solution.py:138
  92.6 11.9 %all-to-all-done = bf16[128,4,2560]{2,1,0:T(4,128)(2,1)S(1)} async-done(((bf16[128,4,2560]{2,1,0:T(4,128)(2,1)}), bf16[128,4,2560]{2,1,0:T(4,128)(2,1)S(1)}, u32[]{:S(2)}, u32[]{:S(2)}) %all-to-all-start) | async-done | bytes 2621472 | tf_op jit(solution)/shard_map/all_to_all | solution.py:134
  104.4 5.9 %all-to-all-start.3 = ((bf16[128,4,1536]{2,1,0:T(4,128)(2,1)}), bf16[128,4,1536]{2,1,0:T(4,128)(2,1)}, u32[]{:S(2)}, u32[]{:S(2)}) async-start(bf16[128,4,1536]{2,1,0:T(4,128)(2,1)} %reshape.187), calls=%async_computation.3 | async-start | bytes 3145728 | tf_op jit(solution)/shard_map/all_to_all | solution.py:137
  110.3 4.1 %copy.20 = bf16[256,4096]{0,1:T(8,128)(2,1)} copy(bf16[256,4096]{1,0:T(8,128)(2,1)} %param.7) | data formatting | bytes 4194304 | tf_op args[0]
  114.4 3.1 %constant_dynamic-slice_fusion = (bf16[256,64,1,32]{0,3,2,1:T(8,128)(2,1)}, bf16[256,64,32]{0,2,1:T(8,128)(2,1)}) fusion(bf16[256,64,2,32]{0,3,2,1:T(8,128)(2,1)} %bitcast.24, s32[]{:T(128)S(6)} %select_n.85, s32[]{:T(128)S(6)} %select_n.86), kind=kLoop, calls=%fused_computation.57 | loop fusion | bytes 4194312 | tf_op jit(solution)/shard_map/jit(dynamic_index_in_dim)/dynamic_slice | solution.py:122
  117.6 0.0 collective-permute-start
  117.6 2.2 reshape.183.q_ref.k_ref.v_ref.o_ref
  119.8 12.3 %shard_map.102 = bf16[512,1536]{1,0:T(8,128)(2,1)} custom-call(s32[512,1]{1,0:T(8,128)} %reshape_tile.10.seg_col_ref, s32[1,512]{1,0:T(1,128)} %reshape_tile.9.seg_row_ref, s32[512,1]{1,0:T(8,128)} %fusion.10.key_col_ref, s32[1,512]{1,0:T(1,128)} %fusion.25.key_row_ref, bf16[512,2560]{1,0:T(8,128)(2,1)} %reshape.183.q_ref.k_ref.v_ref.o_ref, ...), custom_call_target="tpu_custom_call" | custom-call | tf_op jit(solution)/shard_map/pallas_call | solution.py:70
  132.1 3.9 %reshape.184 = bf16[128,4,1536]{2,1,0:T(4,128)(2,1)} reshape(bf16[512,1536]{1,0:T(8,128)(2,1)} %shard_map.102) | data formatting | bytes 3145728 | tf_op jit(solution)/shard_map/reshape | solution.py:138
  135.9 0.0 all-to-all-done.3
  135.9 10.3 %all-to-all-start.1 = ((bf16[128,4,1536]{2,1,0:T(4,128)(2,1)}), bf16[128,4,1536]{2,1,0:T(4,128)(2,1)}, u32[]{:S(2)}, u32[]{:S(2)}) async-start(bf16[128,4,1536]{2,1,0:T(4,128)(2,1)} %reshape.184), calls=%async_computation.1 | async-start | bytes 3145728 | tf_op jit(solution)/shard_map/all_to_all | solution.py:137
  146.2 0.1 copy.13
  146.3 0.1 reshape.228
  146.5 0.1 fusion.13
  146.6 0.0 copy-start
  146.6 3.8 %reshape.218 = bf16[512,1536]{1,0:T(8,128)(2,1)} reshape(bf16[128,4,1536]{2,1,0:T(4,128)(2,1)} %all-to-all-done.3) | data formatting | bytes 3145728 | tf_op jit(solution)/shard_map/reshape | solution.py:143
  150.4 3.9 %scatter_custom_fusion.1 = bf16[256,1536]{1,0:T(8,128)(2,1)S(1)} fusion(s32[512]{0:T(512)S(1)} %fusion.13, bf16[512,1536]{1,0:T(8,128)(2,1)} %reshape.218, bf16[]{:T(256)} %constant.51.clone.1), kind=kCustom, calls=%fused_computation.18 | custom fusion | bytes 786944 | tf_op jit(solution)/shard_map/scatter | solution.py:143
  154.5 0.3 collective-permute-start.2
  154.8 0.0 collective-permute-done
  154.8 0.5 copy-done.1
  155.3 1.4 pad_maximum_fusion
  156.6 0.0 collective-permute-done.2
  156.6 2.0 fusion.19
  158.7 12.2 %all-to-all-done.1 = bf16[128,4,1536]{2,1,0:T(4,128)(2,1)} async-done(((bf16[128,4,1536]{2,1,0:T(4,128)(2,1)}), bf16[128,4,1536]{2,1,0:T(4,128)(2,1)}, u32[]{:S(2)}, u32[]{:S(2)}) %all-to-all-start.1) | async-done | bytes 1572896 | tf_op jit(solution)/shard_map/all_to_all | solution.py:137
  170.8 5.6 %all-to-all-start.5 = ((f32[64,32,256]{2,1,0:T(8,128)}), f32[64,32,256]{2,1,0:T(8,128)}, u32[]{:S(2)}, u32[]{:S(2)}) async-start(f32[64,32,256]{2,1,0:T(8,128)} %fusion.19), calls=%async_computation.5 | async-start | bytes 4194304 | tf_op jit(solution)/shard_map/all_to_all | solution.py:156
  176.4 3.7 %reshape.210 = bf16[512,1536]{1,0:T(8,128)(2,1)} reshape(bf16[128,4,1536]{2,1,0:T(4,128)(2,1)} %all-to-all-done.1) | data formatting | bytes 3145728 | tf_op jit(solution)/shard_map/reshape | solution.py:143
  180.1 3.9 %scatter_custom_fusion = bf16[256,1536]{1,0:T(8,128)(2,1)S(1)} fusion(s32[512]{0:T(512)S(1)} %fusion.13, bf16[512,1536]{1,0:T(8,128)(2,1)} %reshape.210, bf16[]{:T(256)} %constant.51.clone.1), kind=kCustom, calls=%fused_computation.20 | custom fusion | bytes 786944 | tf_op jit(solution)/shard_map/scatter | solution.py:143
  184.1 0.0 copy-start.3
  184.2 0.1 collective-permute-start.1
  184.3 1.3 collective-permute-done.1
  185.6 2.1 fusion.14
  187.6 18.0 %all-to-all-done.5 = f32[64,32,256]{2,1,0:T(8,128)} async-done(((f32[64,32,256]{2,1,0:T(8,128)}), f32[64,32,256]{2,1,0:T(8,128)}, u32[]{:S(2)}, u32[]{:S(2)}) %all-to-all-start.5) | async-done | bytes 2097184 | tf_op jit(solution)/shard_map/all_to_all | solution.py:156
  205.6 5.2 %all-to-all-start.4 = ((f32[64,32,256]{2,1,0:T(8,128)}), f32[64,32,256]{2,1,0:T(8,128)S(1)}, u32[]{:S(2)}, u32[]{:S(2)}) async-start(f32[64,32,256]{2,1,0:T(8,128)} %fusion.14), calls=%async_computation.4 | async-start | bytes 4194304 | tf_op jit(solution)/shard_map/all_to_all | solution.py:156
  210.9 0.0 copy-start.4
  210.9 0.7 pad_maximum_fusion.5
  211.6 0.7 pad_maximum_fusion.4
  212.5 1.1 pad_maximum_fusion.3
  213.6 1.7 reduce_sum.19
  215.3 24.8 %all-to-all-done.4 = f32[64,32,256]{2,1,0:T(8,128)S(1)} async-done(((f32[64,32,256]{2,1,0:T(8,128)}), f32[64,32,256]{2,1,0:T(8,128)S(1)}, u32[]{:S(2)}, u32[]{:S(2)}) %all-to-all-start.4) | async-done | bytes 2097184 | tf_op jit(solution)/shard_map/all_to_all | solution.py:156
  240.1 0.1 reduce_sum.18
  240.2 0.6 pad_maximum_fusion.8
  (22 shorter events, 0.3 us)
Async XLA Ops:
  0.6 2.9 %copy-start.6 = (bf16[256,512]{1,0:T(8,128)(2,1)S(1)}, bf16[256,512]{1,0:T(8,128)(2,1)}, u32[]{:S(2)}) copy-start(bf16[256,512]{1,0:T(8,128)(2,1)} %param.10) | copy-start | bytes 786436
  0.6 2.9 %copy-start.7 = (bf16[256,512]{1,0:T(8,128)(2,1)S(1)}, bf16[256,512]{1,0:T(8,128)(2,1)}, u32[]{:S(2)}) copy-start(bf16[256,512]{1,0:T(8,128)(2,1)} %param.9) | copy-start | bytes 786436
  0.7 3.6 %copy-start.5 = (bf16[256,2048]{1,0:T(8,128)(2,1)S(1)}, bf16[256,2048]{1,0:T(8,128)(2,1)}, u32[]{:S(2)}) copy-start(bf16[256,2048]{1,0:T(8,128)(2,1)} %param.8) | copy-start | bytes 3145732
  16.1 47.5 %all-to-all-start.2 = ((bf16[128,4,2560]{2,1,0:T(4,128)(2,1)}), bf16[128,4,2560]{2,1,0:T(4,128)(2,1)}, u32[]{:S(2)}, u32[]{:S(2)}) async-start(bf16[128,4,2560]{2,1,0:T(4,128)(2,1)} %reshape.199), calls=%async_computation.2 | async-start | bytes 5242880 | tf_op jit(solution)/shard_map/all_to_all | solution.py:134
  36.8 31.5 %copy-start.8 = (s32[1,4]{1,0:T(1,128)S(1)}, s32[1,4]{1,0:T(1,128)}, u32[]{:S(2)}) copy-start(s32[1,4]{1,0:T(1,128)} %param.13) | copy-start | bytes 52
  63.6 40.9 %all-to-all-start = ((bf16[128,4,2560]{2,1,0:T(4,128)(2,1)}), bf16[128,4,2560]{2,1,0:T(4,128)(2,1)S(1)}, u32[]{:S(2)}, u32[]{:S(2)}) async-start(bf16[128,4,2560]{2,1,0:T(4,128)(2,1)} %reshape.191), calls=%async_computation | async-start | bytes 5242880 | tf_op jit(solution)/shard_map/all_to_all | solution.py:134
  104.4 31.5 %all-to-all-start.3 = ((bf16[128,4,1536]{2,1,0:T(4,128)(2,1)}), bf16[128,4,1536]{2,1,0:T(4,128)(2,1)}, u32[]{:S(2)}, u32[]{:S(2)}) async-start(bf16[128,4,1536]{2,1,0:T(4,128)(2,1)} %reshape.187), calls=%async_computation.3 | async-start | bytes 3145728 | tf_op jit(solution)/shard_map/all_to_all | solution.py:137
  117.6 37.2 %collective-permute-start = (bf16[256,64,32]{0,2,1:T(8,128)(2,1)}, bf16[256,64,32]{0,2,1:T(8,128)(2,1)}, u32[]{:S(2)}, u32[]{:S(2)}) collective-permute-start(bf16[256,64,32]{0,2,1:T(8,128)(2,1)} %get-tuple-element.5), channel_id=1, source_target_pairs={{0,1},{1,0},{2,3},{3,2},{4,5},{5,4},{6,7},{7,6},{8,9},{9,8},{10,11... | collective-permute-start | bytes 3145736 | tf_op jit(solution)/shard_map/ppermute | solution.py:124
  135.9 34.9 %all-to-all-start.1 = ((bf16[128,4,1536]{2,1,0:T(4,128)(2,1)}), bf16[128,4,1536]{2,1,0:T(4,128)(2,1)}, u32[]{:S(2)}, u32[]{:S(2)}) async-start(bf16[128,4,1536]{2,1,0:T(4,128)(2,1)} %reshape.184), calls=%async_computation.1 | async-start | bytes 3145728 | tf_op jit(solution)/shard_map/all_to_all | solution.py:137
  146.6 8.7 %copy-start = (bf16[256,64,1,32]{0,3,2,1:T(8,128)(2,1)S(1)}, bf16[256,64,1,32]{0,3,2,1:T(8,128)(2,1)}, u32[]{:S(2)}) copy-start(bf16[256,64,1,32]{0,3,2,1:T(8,128)(2,1)} %get-tuple-element.4) | copy-start | bytes 3145732
  154.4 0.9 copy-start.1
  154.5 2.2 collective-permute-start.2
  170.8 34.8 %all-to-all-start.5 = ((f32[64,32,256]{2,1,0:T(8,128)}), f32[64,32,256]{2,1,0:T(8,128)}, u32[]{:S(2)}, u32[]{:S(2)}) async-start(f32[64,32,256]{2,1,0:T(8,128)} %fusion.19), calls=%async_computation.5 | async-start | bytes 4194304 | tf_op jit(solution)/shard_map/all_to_all | solution.py:156
  184.1 1.5 copy-start.3
  184.2 1.4 collective-permute-start.1
  187.6 24.7 %copy-start.2 = (bf16[256,1536]{1,0:T(8,128)(2,1)S(1)}, bf16[256,1536]{1,0:T(8,128)(2,1)}, u32[]{:S(2)}) copy-start(bf16[256,1536]{1,0:T(8,128)(2,1)} %copy-done.1) | copy-start | bytes 2359300
  205.6 34.5 %all-to-all-start.4 = ((f32[64,32,256]{2,1,0:T(8,128)}), f32[64,32,256]{2,1,0:T(8,128)S(1)}, u32[]{:S(2)}, u32[]{:S(2)}) async-start(f32[64,32,256]{2,1,0:T(8,128)} %fusion.14), calls=%async_computation.4 | async-start | bytes 4194304 | tf_op jit(solution)/shard_map/all_to_all | solution.py:156
  210.9 1.5 copy-start.4

commit v9 on v8

--- a/solution.py
+++ b/solution.py
@@ -152,12 +152,12 @@
         partial = jnp.einsum(
             "td,tc->dc", hidden_pair, grad_pair, preferred_element_type=jnp.float32
         )
-        partial = partial.reshape(chips, partial.shape[0] // chips, partial.shape[1])
-        wv_parts.append(lax.all_to_all(partial, CHIP, 0, 0, tiled=True).sum(0) * grad_scale)
+        wv_parts.append(partial.reshape(chips, partial.shape[0] // chips, partial.shape[1]))
     grad_queries = jnp.concatenate(dq_parts, axis=1)
     grad_keys = jnp.concatenate(dk_parts, axis=1)
     grad_values = jnp.concatenate(dv_parts, axis=1)
-    grad_wv = jnp.concatenate(wv_parts, axis=1)
+    partial = jnp.concatenate(wv_parts, axis=2)
+    grad_wv = lax.all_to_all(partial, CHIP, 0, 0, tiled=True).sum(0) * grad_scale
     return (grad_queries, grad_keys, grad_values, grad_wv)
 
 

time: 242 us -> 247 us (1.021)
  the two profiles are of different devices: /device:TPU:0 before, /device:TPU:2 now
where the time goes in v9:
time: 247 us; the launch traced here: 245 us
  waiting for transfers between devices  110 us (45%)
  local copies, waits for them, and re-layouts  61.5 us (25%)
  starting transfers between devices  35.2 us (14%)
  Pallas kernels  24.7 us (10%)
  other arithmetic  12.1 us (5%)
    all_to_all x1, waiting for transfers between devices, local(): lax.all_to_all(partial, CHIP, 0, 0, tiled=True).sum(0) * grad_scale  55.7 us
    all_to_all x2, waiting for transfers between devices, local(): rows_in = lax.all_to_all(table[pick_rows], DP, 0, 0, tiled=True)  38 us
    pallas_call x2, Pallas kernels, attend_rows(): pl.pallas_call(attend_kernel, grid=(n_kv,), in_specs=[col, row, col, row,...  24.7 us
    gather x4, local copies, waits for them, and re-layouts, local(): rows_in = lax.all_to_all(table[pick_rows], DP, 0, 0, tiled=True)  18.1 us
    all_to_all x2, starting transfers between devices, local(): rows_in = lax.all_to_all(table[pick_rows], DP, 0, 0, tiled=True)  15.8 us
    all_to_all x2, waiting for transfers between devices, local(): lax.all_to_all(rows_out.reshape(owners, slot_count, rows_out.shape[1]), D...  12.8 us
    all_to_all x2, starting transfers between devices, local(): lax.all_to_all(rows_out.reshape(owners, slot_count, rows_out.shape[1]), D...  12 us
    scatter x2, local copies, waits for them, and re-layouts, local(): home = jnp.zeros((tok_rows, back.shape[2]), back.dtype).at[targets].set(b...  8.81 us
  transfers between devices with their start and end apart: 8, of which 7 were waited for; matrix products, arithmetic and copies ran while one was open for 18% of the time, Pallas kernels for 10%

profile of v9, /device:TPU:2, one launch (start us, length us, event | category | flops | bytes accessed | tf_op | source)
XLA Modules:
  0.0 245.3 jit_solution(11217098961883099004)
XLA Ops:
  0.6 0.0 copy-start.1
  0.6 0.8 compare_select_fusion.1
  1.4 0.1 copy.17
  1.5 0.1 reshape.192
  1.7 1.0 fusion.34
  2.6 1.0 fusion.35
  3.6 1.3 fusion.28
  4.9 0.0 copy-done.1
  4.9 0.1 fusion.29
  5.0 0.2 pad_maximum_fusion.2
  5.2 3.5 %gather_fusion = bf16[512,2560]{1,0:T(8,128)(2,1)} fusion(bf16[256,2560]{1,0:T(8,128)(2,1)S(1)} %get-tuple-element.28, s32[1024]{0:T(1024)S(1)} %pad_clamp_fusion), kind=kCustom, calls=%fused_computation | custom fusion | bytes 5244928 | tf_op jit(solution)/shard_map/gather | solution.py:134
  8.7 5.5 %reshape.191 = bf16[128,4,2560]{2,1,0:T(4,128)(2,1)} reshape(bf16[512,2560]{1,0:T(8,128)(2,1)} %gather_fusion) | data formatting | bytes 5242880 | tf_op jit(solution)/shard_map/gather | solution.py:134
  14.3 10.9 %all-to-all-start = ((bf16[128,4,2560]{2,1,0:T(4,128)(2,1)}), bf16[128,4,2560]{2,1,0:T(4,128)(2,1)}, u32[]{:S(2)}, u32[]{:S(2)}) async-start(bf16[128,4,2560]{2,1,0:T(4,128)(2,1)} %reshape.191), calls=%async_computation | async-start | bytes 5242880 | tf_op jit(solution)/shard_map/all_to_all | solution.py:134
  25.2 3.5 %gather_fusion.1 = bf16[512,2560]{1,0:T(8,128)(2,1)} fusion(bf16[256,2560]{1,0:T(8,128)(2,1)S(1)} %get-tuple-element.29, s32[1024]{0:T(1024)S(1)} %pad_clamp_fusion), kind=kCustom, calls=%fused_computation.1 | custom fusion | bytes 5244928 | tf_op jit(solution)/shard_map/gather | solution.py:134
  28.7 5.5 %reshape.199 = bf16[128,4,2560]{2,1,0:T(4,128)(2,1)} reshape(bf16[512,2560]{1,0:T(8,128)(2,1)} %gather_fusion.1) | data formatting | bytes 5242880 | tf_op jit(solution)/shard_map/gather | solution.py:134
  34.3 0.0 copy-start.3
  34.3 26.5 %all-to-all-done = bf16[128,4,2560]{2,1,0:T(4,128)(2,1)} async-done(((bf16[128,4,2560]{2,1,0:T(4,128)(2,1)}), bf16[128,4,2560]{2,1,0:T(4,128)(2,1)}, u32[]{:S(2)}, u32[]{:S(2)}) %all-to-all-start) | async-done | bytes 2621472 | tf_op jit(solution)/shard_map/all_to_all | solution.py:134
  60.7 4.9 %all-to-all-start.2 = ((bf16[128,4,2560]{2,1,0:T(4,128)(2,1)}), bf16[128,4,2560]{2,1,0:T(4,128)(2,1)S(1)}, u32[]{:S(2)}, u32[]{:S(2)}) async-start(bf16[128,4,2560]{2,1,0:T(4,128)(2,1)} %reshape.199), calls=%async_computation.2 | async-start | bytes 5242880 | tf_op jit(solution)/shard_map/all_to_all | solution.py:134
  65.7 0.0 copy-done.3
  65.7 0.7 reshape_tile.9.seg_row_ref
  66.4 0.8 reshape_tile.10.seg_col_ref
  67.2 0.6 fusion.25.key_row_ref
  67.8 0.8 fusion.10.key_col_ref
  68.5 5.3 %reshape.183.q_ref.k_ref.v_ref.o_ref = bf16[512,2560]{1,0:T(8,128)(2,1)} reshape(bf16[128,4,2560]{2,1,0:T(4,128)(2,1)} %all-to-all-done) | data formatting | bytes 5242880 | tf_op jit(solution)/shard_map/reshape | solution.py:135
  73.8 12.3 %shard_map.102 = bf16[512,1536]{1,0:T(8,128)(2,1)} custom-call(s32[512,1]{1,0:T(8,128)} %reshape_tile.10.seg_col_ref, s32[1,512]{1,0:T(1,128)} %reshape_tile.9.seg_row_ref, s32[512,1]{1,0:T(8,128)} %fusion.10.key_col_ref, s32[1,512]{1,0:T(1,128)} %fusion.25.key_row_ref, bf16[512,2560]{1,0:T(8,128)(2,1)} %reshape.183.q_ref.k_ref.v_ref.o_ref, ...), custom_call_target="tpu_custom_call" | custom-call | tf_op jit(solution)/shard_map/pallas_call | solution.py:70
  86.2 3.9 %reshape.184 = bf16[128,4,1536]{2,1,0:T(4,128)(2,1)} reshape(bf16[512,1536]{1,0:T(8,128)(2,1)} %shard_map.102) | data formatting | bytes 3145728 | tf_op jit(solution)/shard_map/reshape | solution.py:138
  90.1 11.6 %all-to-all-done.2 = bf16[128,4,2560]{2,1,0:T(4,128)(2,1)S(1)} async-done(((bf16[128,4,2560]{2,1,0:T(4,128)(2,1)}), bf16[128,4,2560]{2,1,0:T(4,128)(2,1)S(1)}, u32[]{:S(2)}, u32[]{:S(2)}) %all-to-all-start.2) | async-done | bytes 2621472 | tf_op jit(solution)/shard_map/all_to_all | solution.py:134
  101.6 6.1 %all-to-all-start.1 = ((bf16[128,4,1536]{2,1,0:T(4,128)(2,1)}), bf16[128,4,1536]{2,1,0:T(4,128)(2,1)}, u32[]{:S(2)}, u32[]{:S(2)}) async-start(bf16[128,4,1536]{2,1,0:T(4,128)(2,1)} %reshape.184), calls=%async_computation.1 | async-start | bytes 3145728 | tf_op jit(solution)/shard_map/all_to_all | solution.py:137
  107.7 2.3 reshape.186.q_ref.k_ref.v_ref.o_ref
  109.9 12.3 %shard_map.103 = bf16[512,1536]{1,0:T(8,128)(2,1)} custom-call(s32[512,1]{1,0:T(8,128)} %reshape_tile.10.seg_col_ref, s32[1,512]{1,0:T(1,128)} %reshape_tile.9.seg_row_ref, s32[512,1]{1,0:T(8,128)} %fusion.10.key_col_ref, s32[1,512]{1,0:T(1,128)} %fusion.25.key_row_ref, bf16[512,2560]{1,0:T(8,128)(2,1)} %reshape.186.q_ref.k_ref.v_ref.o_ref, ...), custom_call_target="tpu_custom_call" | custom-call | tf_op jit(solution)/shard_map/pallas_call | solution.py:70
  122.3 3.9 %reshape.187 = bf16[128,4,1536]{2,1,0:T(4,128)(2,1)} reshape(bf16[512,1536]{1,0:T(8,128)(2,1)} %shard_map.103) | data formatting | bytes 3145728 | tf_op jit(solution)/shard_map/reshape | solution.py:138
  126.2 5.9 %all-to-all-done.1 = bf16[128,4,1536]{2,1,0:T(4,128)(2,1)} async-done(((bf16[128,4,1536]{2,1,0:T(4,128)(2,1)}), bf16[128,4,1536]{2,1,0:T(4,128)(2,1)}, u32[]{:S(2)}, u32[]{:S(2)}) %all-to-all-start.1) | async-done | bytes 1572896 | tf_op jit(solution)/shard_map/all_to_all | solution.py:137
  132.1 5.9 %all-to-all-start.3 = ((bf16[128,4,1536]{2,1,0:T(4,128)(2,1)}), bf16[128,4,1536]{2,1,0:T(4,128)(2,1)}, u32[]{:S(2)}, u32[]{:S(2)}) async-start(bf16[128,4,1536]{2,1,0:T(4,128)(2,1)} %reshape.187), calls=%async_computation.3 | async-start | bytes 3145728 | tf_op jit(solution)/shard_map/all_to_all | solution.py:137
  138.0 3.3 %copy.20 = bf16[256,4096]{0,1:T(8,128)(2,1)S(1)} copy(bf16[256,4096]{1,0:T(8,128)(2,1)} %param.7) | data formatting | bytes 4194304 | tf_op args[0]
  141.3 1.2 constant_dynamic-slice_fusion
  142.5 0.1 collective-permute-start
  142.6 0.1 copy.13
  142.7 0.1 reshape.228
  142.8 0.1 fusion.13
  143.0 2.4 collective-permute-done
  145.4 1.0 copy-done.2
  146.3 1.4 pad_maximum_fusion.1
  147.7 3.7 %reshape.210 = bf16[512,1536]{1,0:T(8,128)(2,1)} reshape(bf16[128,4,1536]{2,1,0:T(4,128)(2,1)} %all-to-all-done.1) | data formatting | bytes 3145728 | tf_op jit(solution)/shard_map/reshape | solution.py:143
  151.4 4.2 %scatter_custom_fusion = bf16[256,1536]{1,0:T(8,128)(2,1)S(1)} fusion(s32[512]{0:T(512)S(1)} %fusion.13, bf16[512,1536]{1,0:T(8,128)(2,1)} %reshape.210, bf16[]{:T(256)} %constant.51.clone.1), kind=kCustom, calls=%fused_computation.21 | custom fusion | bytes 786944 | tf_op jit(solution)/shard_map/scatter | solution.py:143
  155.6 6.9 %all-to-all-done.3 = bf16[128,4,1536]{2,1,0:T(4,128)(2,1)} async-done(((bf16[128,4,1536]{2,1,0:T(4,128)(2,1)}), bf16[128,4,1536]{2,1,0:T(4,128)(2,1)}, u32[]{:S(2)}, u32[]{:S(2)}) %all-to-all-start.3) | async-done | bytes 1572896 | tf_op jit(solution)/shard_map/all_to_all | solution.py:137
  162.4 3.7 %reshape.218 = bf16[512,1536]{1,0:T(8,128)(2,1)} reshape(bf16[128,4,1536]{2,1,0:T(4,128)(2,1)} %all-to-all-done.3) | data formatting | bytes 3145728 | tf_op jit(solution)/shard_map/reshape | solution.py:143
  166.2 4.6 %scatter_custom_fusion.1 = bf16[256,1536]{1,0:T(8,128)(2,1)} fusion(s32[512]{0:T(512)S(1)} %fusion.13, bf16[512,1536]{1,0:T(8,128)(2,1)} %reshape.218, bf16[]{:T(256)} %constant.51.clone.1), kind=kCustom, calls=%fused_computation.19 | custom fusion | bytes 786944 | tf_op jit(solution)/shard_map/scatter | solution.py:143
  170.8 1.0 fusion.31
  171.8 0.1 collective-permute-start.2
  172.0 0.6 collective-permute-start.1
  172.5 0.7 collective-permute-done.2
  173.2 0.7 fusion.19
  173.9 0.0 collective-permute-done.1
  173.9 0.7 fusion.14
  174.7 2.5 %pad_maximum_fusion = f32[64,32,512]{2,1,0:T(8,128)} fusion(f32[64,32,256]{2,1,0:T(8,128)S(1)} %fusion.19, f32[64,32,256]{2,1,0:T(8,128)S(1)} %fusion.14), kind=kLoop, calls=%fused_computation.4 | loop fusion | flops 1048576 | bytes 8388608 | tf_op jit(solution)/shard_map/concatenate | solution.py:159
  177.2 6.6 %all-to-all-start.4 = ((f32[64,32,512]{2,1,0:T(8,128)}), f32[64,32,512]{2,1,0:T(8,128)}, u32[]{:S(2)}, u32[]{:S(2)}) async-start(f32[64,32,512]{2,1,0:T(8,128)} %pad_maximum_fusion), calls=%async_computation.4 | async-start | bytes 8388608 | tf_op jit(solution)/shard_map/all_to_all | solution.py:160
  183.8 0.0 copy-start
  183.8 0.7 pad_maximum_fusion.6
  184.5 0.7 pad_maximum_fusion.5
  185.3 0.0 copy-done
  185.3 1.1 pad_maximum_fusion.4
  186.4 55.7 %all-to-all-done.4 = f32[64,32,512]{2,1,0:T(8,128)} async-done(((f32[64,32,512]{2,1,0:T(8,128)}), f32[64,32,512]{2,1,0:T(8,128)}, u32[]{:S(2)}, u32[]{:S(2)}) %all-to-all-start.4) | async-done | bytes 4194336 | tf_op jit(solution)/shard_map/all_to_all | solution.py:160
  242.1 2.5 %reduce_sum.9 = f32[32,512]{1,0:T(8,128)S(1)} reduce(f32[64,32,512]{2,1,0:T(8,128)} %all-to-all-done.4, f32[]{:T(128)} %constant.61.clone.1), dimensions={0}, to_apply=%region_2.3 | reduce | flops 1032192 | bytes 4259844 | tf_op jit(solution)/shard_map/reduce_sum | solution.py:160
  244.6 0.6 broadcast_multiply_fusion
  (8 shorter events, 0.2 us)
Async XLA Ops:
  0.6 4.3 %copy-start.1 = (bf16[256,2048]{1,0:T(8,128)(2,1)S(1)}, bf16[256,2048]{1,0:T(8,128)(2,1)}, u32[]{:S(2)}) copy-start(bf16[256,2048]{1,0:T(8,128)(2,1)} %param.11) | copy-start | bytes 3145732
  14.3 46.5 %all-to-all-start = ((bf16[128,4,2560]{2,1,0:T(4,128)(2,1)}), bf16[128,4,2560]{2,1,0:T(4,128)(2,1)}, u32[]{:S(2)}, u32[]{:S(2)}) async-start(bf16[128,4,2560]{2,1,0:T(4,128)(2,1)} %reshape.191), calls=%async_computation | async-start | bytes 5242880 | tf_op jit(solution)/shard_map/all_to_all | solution.py:134
  34.3 31.4 %copy-start.3 = (s32[1,4]{1,0:T(1,128)S(1)}, s32[1,4]{1,0:T(1,128)}, u32[]{:S(2)}) copy-start(s32[1,4]{1,0:T(1,128)} %param.13) | copy-start | bytes 52
  60.7 40.9 %all-to-all-start.2 = ((bf16[128,4,2560]{2,1,0:T(4,128)(2,1)}), bf16[128,4,2560]{2,1,0:T(4,128)(2,1)S(1)}, u32[]{:S(2)}, u32[]{:S(2)}) async-start(bf16[128,4,2560]{2,1,0:T(4,128)(2,1)} %reshape.199), calls=%async_computation.2 | async-start | bytes 5242880 | tf_op jit(solution)/shard_map/all_to_all | solution.py:134
  101.6 30.5 %all-to-all-start.1 = ((bf16[128,4,1536]{2,1,0:T(4,128)(2,1)}), bf16[128,4,1536]{2,1,0:T(4,128)(2,1)}, u32[]{:S(2)}, u32[]{:S(2)}) async-start(bf16[128,4,1536]{2,1,0:T(4,128)(2,1)} %reshape.184), calls=%async_computation.1 | async-start | bytes 3145728 | tf_op jit(solution)/shard_map/all_to_all | solution.py:137
  132.1 30.3 %all-to-all-start.3 = ((bf16[128,4,1536]{2,1,0:T(4,128)(2,1)}), bf16[128,4,1536]{2,1,0:T(4,128)(2,1)}, u32[]{:S(2)}, u32[]{:S(2)}) async-start(bf16[128,4,1536]{2,1,0:T(4,128)(2,1)} %reshape.187), calls=%async_computation.3 | async-start | bytes 3145728 | tf_op jit(solution)/shard_map/all_to_all | solution.py:137
  142.5 2.9 %collective-permute-start = (bf16[256,64,32]{0,2,1:T(8,128)(2,1)}, bf16[256,64,32]{0,2,1:T(8,128)(2,1)S(1)}, u32[]{:S(2)}, u32[]{:S(2)}) collective-permute-start(bf16[256,64,32]{0,2,1:T(8,128)(2,1)} %get-tuple-element.5), channel_id=1, source_target_pairs={{0,1},{1,0},{2,3},{3,2},{4,5},{5,4},{6,7},{7,6},{8,9},{9,8},{10,11... | collective-permute-start | bytes 3145736 | tf_op jit(solution)/shard_map/ppermute | solution.py:124
  145.3 1.0 copy-start.2
  171.8 1.4 collective-permute-start.2
  172.0 2.0 collective-permute-start.1
  177.2 65.0 %all-to-all-start.4 = ((f32[64,32,512]{2,1,0:T(8,128)}), f32[64,32,512]{2,1,0:T(8,128)}, u32[]{:S(2)}, u32[]{:S(2)}) async-start(f32[64,32,512]{2,1,0:T(8,128)} %pad_maximum_fusion), calls=%async_computation.4 | async-start | bytes 8388608 | tf_op jit(solution)/shard_map/all_to_all | solution.py:160
  183.8 1.5 copy-start

commit v10 on v8

--- a/solution.py
+++ b/solution.py
@@ -63,7 +63,7 @@
     row_count = rows_in.shape[0]
     q_w = (HQ // HK) * DH
     out_w = q_w + 2 * DH
-    k_at, v_at, o_at = n_kv * q_w // DH, n_kv * q_w // DH + n_kv, (n_kv + 2 * n_kv * DH // q_w)
+    o_at, k_at, v_at = n_kv, 2 * n_kv * q_w // DH, 2 * n_kv * q_w // DH + n_kv
     whole = lambda g: (0, 0)
     col = pl.BlockSpec((row_count, 1), whole)
     row = pl.BlockSpec((1, row_count), whole)
@@ -98,7 +98,7 @@
 
 CHIP, CORE = "chip", "core"
 DP = (CHIP, CORE)
-PARTS = 2
+PARTS = ((0, 1), (1, HK - 1))
 
 
 def local(hidden_in, queries, keys, values, grad_attn, send_rows, slot_docs):
@@ -123,13 +123,12 @@
     theirs = lax.dynamic_index_in_dim(blocks, 1 - core, axis=2, keepdims=False)
     from_partner = lax.ppermute(theirs, CORE, swap)
     hidden_pair = jnp.concatenate((mine, from_partner), axis=0).reshape(2 * tok_rows, -1)
-    n_kv = HK // PARTS
     dq_parts, dk_parts, dv_parts, wv_parts = [], [], [], []
-    for part in range(PARTS):
-        q_cols = slice(part * n_kv * q_w, (part + 1) * n_kv * q_w)
-        kv_cols = slice(part * n_kv * DH, (part + 1) * n_kv * DH)
+    for first, n_kv in PARTS:
+        q_cols = slice(first * q_w, (first + n_kv) * q_w)
+        kv_cols = slice(first * DH, (first + n_kv) * DH)
         table = jnp.concatenate(
-            (queries[:, q_cols], keys[:, kv_cols], values[:, kv_cols], grad_attn[:, q_cols]), axis=1
+            (queries[:, q_cols], grad_attn[:, q_cols], keys[:, kv_cols], values[:, kv_cols]), axis=1
         )
         rows_in = lax.all_to_all(table[pick_rows], DP, 0, 0, tiled=True)
         rows_in = rows_in.reshape(owners * slot_count, table.shape[1])

time: 242 us -> 252 us (1.041)
  waiting for transfers between devices: 95 us -> 101 us
    all_to_all x2, waiting for transfers between devices: 38.7 us -> 44.8 us  [local(): rows_in = lax.all_to_all(table[pick_rows], DP, 0, 0, tiled=True)]
    all_to_all x2, waiting for transfers between devices: 12.2 us -> 17.4 us  [local(): lax.all_to_all(rows_out.reshape(owners, slot_count, rows_out.shape[1]), D...]
    all_to_all x2, waiting for transfers between devices: 42.8 us -> 37.7 us  [local(): lax.all_to_all(partial, CHIP, 0, 0, tiled=True).sum(0) * grad_scale]
    gather x4, local copies, waits for them, and re-layouts: 18 us -> 15.3 us  [local(): rows_in = lax.all_to_all(table[pick_rows], DP, 0, 0, tiled=True)]
    unnamed x19 -> x17, local copies, waits for them, and re-layouts: 4.6 us -> 5.18 us
  transfers between devices with their start and end apart: 9 -> 9, of which waited for: 6 -> 6; matrix products, arithmetic and copies ran while one was open for 25% -> 26% of each run, Pallas kernels for 10% -> 10%
where the time goes in v10:
time: 252 us; the launch traced here: 250 us
  waiting for transfers between devices  101 us (40%)
  local copies, waits for them, and re-layouts  62.8 us (25%)
  starting transfers between devices  46 us (18%)
  Pallas kernels  24.5 us (10%)
  other arithmetic  9.51 us (4%)
  matrix products  4.56 us (2%)
    all_to_all x2, waiting for transfers between devices, local(): rows_in = lax.all_to_all(table[pick_rows], DP, 0, 0, tiled=True)  44.8 us
    all_to_all x2, waiting for transfers between devices, local(): lax.all_to_all(partial, CHIP, 0, 0, tiled=True).sum(0) * grad_scale  37.7 us
    pallas_call x2, Pallas kernels, attend_rows(): pl.pallas_call(attend_kernel, grid=(n_kv,), in_specs=[col, row, col, row,...  24.5 us
    all_to_all x2, waiting for transfers between devices, local(): lax.all_to_all(rows_out.reshape(owners, slot_count, rows_out.shape[1]), D...  17.4 us
    all_to_all x2, starting transfers between devices, local(): rows_in = lax.all_to_all(table[pick_rows], DP, 0, 0, tiled=True)  16.9 us
    gather x4, local copies, waits for them, and re-layouts, local(): rows_in = lax.all_to_all(table[pick_rows], DP, 0, 0, tiled=True)  15.3 us
    all_to_all x2, starting transfers between devices, local(): lax.all_to_all(rows_out.reshape(owners, slot_count, rows_out.shape[1]), D...  15.2 us
    all_to_all x2, starting transfers between devices, local(): lax.all_to_all(partial, CHIP, 0, 0, tiled=True).sum(0) * grad_scale  13.3 us
  transfers between devices with their start and end apart: 9, of which 6 were waited for; matrix products, arithmetic and copies ran while one was open for 26% of the time, Pallas kernels for 10%

profile of v10, /device:TPU:0, one launch (start us, length us, event | category | flops | bytes accessed | tf_op | source)
XLA Modules:
  0.0 249.6 jit_solution(6452722582806240149)
XLA Ops:
  0.6 0.7 compare_select_fusion.1
  1.3 0.1 copy.17
  1.4 0.1 reshape.192
  1.6 0.8 slice.62
  2.4 0.8 slice.63
  3.2 1.0 slice.60
  4.2 1.0 slice.61
  5.2 0.1 pad_maximum_fusion.3
  5.2 2.1 gather_fusion
  7.4 1.3 reshape.191
  8.7 11.2 %all-to-all-start = ((bf16[128,4,1280]{2,1,0:T(4,128)(2,1)}), bf16[128,4,1280]{2,1,0:T(4,128)(2,1)S(1)}, u32[]{:S(2)}, u32[]{:S(2)}) async-start(bf16[128,4,1280]{2,1,0:T(4,128)(2,1)} %reshape.191), calls=%async_computation | async-start | bytes 2621440 | tf_op jit(solution)/shard_map/all_to_all | solution.py:133
  20.0 1.1 slice-done
  21.0 0.2 slice-done.1
  21.3 0.0 slice-done.3
  21.3 0.1 slice-done.4
  21.4 0.1 pad_maximum_fusion.1
  21.5 4.4 %gather_fusion.1 = bf16[512,3840]{1,0:T(8,128)(2,1)} fusion(bf16[256,3840]{1,0:T(8,128)(2,1)S(1)} %pad_maximum_fusion.1, s32[1024]{0:T(1024)S(1)} %pad_clamp_fusion), kind=kCustom, calls=%fused_computation.1 | custom fusion | bytes 7866368 | tf_op jit(solution)/shard_map/gather | solution.py:133
  25.9 7.4 %reshape.199 = bf16[128,4,3840]{2,1,0:T(4,128)(2,1)} reshape(bf16[512,3840]{1,0:T(8,128)(2,1)} %gather_fusion.1) | data formatting | bytes 7864320 | tf_op jit(solution)/shard_map/gather | solution.py:133
  33.3 8.8 %all-to-all-done = bf16[128,4,1280]{2,1,0:T(4,128)(2,1)S(1)} async-done(((bf16[128,4,1280]{2,1,0:T(4,128)(2,1)}), bf16[128,4,1280]{2,1,0:T(4,128)(2,1)S(1)}, u32[]{:S(2)}, u32[]{:S(2)}) %all-to-all-start) | async-done | bytes 1310752 | tf_op jit(solution)/shard_map/all_to_all | solution.py:133
  42.1 5.8 %all-to-all-start.2 = ((bf16[128,4,3840]{2,1,0:T(4,128)(2,1)}), bf16[128,4,3840]{2,1,0:T(4,128)(2,1)}, u32[]{:S(2)}, u32[]{:S(2)}) async-start(bf16[128,4,3840]{2,1,0:T(4,128)(2,1)} %reshape.199), calls=%async_computation.2 | async-start | bytes 7864320 | tf_op jit(solution)/shard_map/all_to_all | solution.py:133
  47.9 0.7 reshape_tile.9.seg_row_ref
  48.5 0.8 reshape_tile.10.seg_col_ref
  49.4 0.6 fusion.25.key_row_ref
  50.0 0.8 fusion.15.key_col_ref
  50.7 1.3 reshape.183.q_ref.k_ref.v_ref.o_ref
  52.0 7.3 %shard_map.102 = bf16[512,768]{1,0:T(8,128)(2,1)} custom-call(s32[512,1]{1,0:T(8,128)} %reshape_tile.10.seg_col_ref, s32[1,512]{1,0:T(1,128)} %reshape_tile.9.seg_row_ref, s32[512,1]{1,0:T(8,128)} %fusion.15.key_col_ref, s32[1,512]{1,0:T(1,128)} %fusion.25.key_row_ref, bf16[512,1280]{1,0:T(8,128)(2,1)} %reshape.183.q_ref.k_ref.v_ref.o_ref, ...), custom_call_target="tpu_custom_call" | custom-call | tf_op jit(solution)/shard_map/pallas_call | solution.py:70
  59.3 2.4 reshape.184
  61.7 36.1 %all-to-all-done.2 = bf16[128,4,3840]{2,1,0:T(4,128)(2,1)} async-done(((bf16[128,4,3840]{2,1,0:T(4,128)(2,1)}), bf16[128,4,3840]{2,1,0:T(4,128)(2,1)}, u32[]{:S(2)}, u32[]{:S(2)}) %all-to-all-start.2) | async-done | bytes 3932192 | tf_op jit(solution)/shard_map/all_to_all | solution.py:133
  97.8 5.1 %all-to-all-start.1 = ((bf16[128,4,768]{2,1,0:T(4,128)(2,1)}), bf16[128,4,768]{2,1,0:T(4,128)(2,1)S(1)}, u32[]{:S(2)}, u32[]{:S(2)}) async-start(bf16[128,4,768]{2,1,0:T(4,128)(2,1)} %reshape.184), calls=%async_computation.1 | async-start | bytes 1572864 | tf_op jit(solution)/shard_map/all_to_all | solution.py:136
  102.9 7.1 %reshape.186.q_ref.k_ref.v_ref.o_ref = bf16[512,3840]{1,0:T(8,128)(2,1)} reshape(bf16[128,4,3840]{2,1,0:T(4,128)(2,1)} %all-to-all-done.2) | data formatting | bytes 7864320 | tf_op jit(solution)/shard_map/reshape | solution.py:134
  110.0 17.2 %shard_map.103 = bf16[512,2304]{1,0:T(8,128)(2,1)} custom-call(s32[512,1]{1,0:T(8,128)} %reshape_tile.10.seg_col_ref, s32[1,512]{1,0:T(1,128)} %reshape_tile.9.seg_row_ref, s32[512,1]{1,0:T(8,128)} %fusion.15.key_col_ref, s32[1,512]{1,0:T(1,128)} %fusion.25.key_row_ref, bf16[512,3840]{1,0:T(8,128)(2,1)} %reshape.186.q_ref.k_ref.v_ref.o_ref, ...), custom_call_target="tpu_custom_call" | custom-call | tf_op jit(solution)/shard_map/pallas_call | solution.py:70
  127.3 5.0 %reshape.187 = bf16[128,4,2304]{2,1,0:T(4,128)(2,1)} reshape(bf16[512,2304]{1,0:T(8,128)(2,1)} %shard_map.103) | data formatting | bytes 4718592 | tf_op jit(solution)/shard_map/reshape | solution.py:137
  132.3 0.9 copy-done.1
  133.2 10.1 %all-to-all-start.3 = ((bf16[128,4,2304]{2,1,0:T(4,128)(2,1)}), bf16[128,4,2304]{2,1,0:T(4,128)(2,1)}, u32[]{:S(2)}, u32[]{:S(2)}) async-start(bf16[128,4,2304]{2,1,0:T(4,128)(2,1)} %reshape.187), calls=%async_computation.3 | async-start | bytes 4718592 | tf_op jit(solution)/shard_map/all_to_all | solution.py:136
  143.2 3.3 %copy.20 = bf16[256,4096]{0,1:T(8,128)(2,1)S(1)} copy(bf16[256,4096]{1,0:T(8,128)(2,1)} %param.7) | data formatting | bytes 4194304 | tf_op args[0]
  146.5 1.2 constant_dynamic-slice_fusion
  147.7 0.1 copy.13
  147.8 0.1 reshape.228
  147.9 0.1 fusion.18
  148.1 2.3 reshape.210
  150.4 3.3 %scatter_custom_fusion = bf16[256,768]{1,0:T(8,128)(2,1)S(1)} fusion(s32[512]{0:T(512)S(1)} %fusion.18, bf16[512,768]{1,0:T(8,128)(2,1)} %reshape.210, bf16[]{:T(256)} %constant.53.clone.1), kind=kCustom, calls=%fused_computation.37 | custom fusion | bytes 393728 | tf_op jit(solution)/shard_map/scatter | solution.py:142
  153.7 0.7 fusion.30
  154.4 0.5 collective-permute-start.1
  154.9 1.0 copy-done.4
  155.8 1.4 pad_maximum_fusion
  157.2 1.7 fusion.21
  158.9 17.4 %all-to-all-done.3 = bf16[128,4,2304]{2,1,0:T(4,128)(2,1)} async-done(((bf16[128,4,2304]{2,1,0:T(4,128)(2,1)}), bf16[128,4,2304]{2,1,0:T(4,128)(2,1)}, u32[]{:S(2)}, u32[]{:S(2)}) %all-to-all-start.3) | async-done | bytes 2359328 | tf_op jit(solution)/shard_map/all_to_all | solution.py:136
  176.3 5.7 %all-to-all-start.4 = ((f32[64,32,128]{2,1,0:T(8,128)}), f32[64,32,128]{2,1,0:T(8,128)}, u32[]{:S(2)}, u32[]{:S(2)}) async-start(f32[64,32,128]{2,1,0:T(8,128)} %fusion.21), calls=%async_computation.4 | async-start | bytes 2097152 | tf_op jit(solution)/shard_map/all_to_all | solution.py:155
  182.0 4.8 %reshape.218 = bf16[512,2304]{1,0:T(8,128)(2,1)} reshape(bf16[128,4,2304]{2,1,0:T(4,128)(2,1)} %all-to-all-done.3) | data formatting | bytes 4718592 | tf_op jit(solution)/shard_map/reshape | solution.py:142
  186.9 5.3 %scatter_custom_fusion.1 = bf16[256,2304]{1,0:T(8,128)(2,1)S(1)} fusion(s32[512]{0:T(512)S(1)} %fusion.18, bf16[512,2304]{1,0:T(8,128)(2,1)} %reshape.218, bf16[]{:T(256)} %constant.53.clone.1), kind=kCustom, calls=%fused_computation.10 | custom fusion | bytes 1180160 | tf_op jit(solution)/shard_map/scatter | solution.py:142
  192.1 0.8 fusion.28
  193.0 0.1 collective-permute-start.2
  193.1 1.4 collective-permute-done.2
  194.5 2.9 %fusion.6 = f32[64,32,384]{2,1,0:T(8,128)} fusion(bf16[64,32,512]{2,1,0:T(8,128)(2,1)S(1)} %bitcast.25, bf16[256,384]{1,0:T(8,128)(2,1)S(1)} %collective-permute-done.2, bf16[256,128]{1,0:T(8,128)(2,1)S(1)} %get-tuple-element.7, bf16[256,128]{1,0:T(8,128)(2,1)S(1)} %get-tuple-element.8, bf16[256,128]{1,0:T(8,128)(2,1)S(1)} %get-tuple-element.6), kind=kOutput, calls=%fused_computation.20 | convolution fusion | flops 806879232 | bytes 5636096 | tf_op jit(solution)/shard_map/td,tc->dc/dot_general | solution.py:151
  197.4 2.7 %all-to-all-done.4 = f32[64,32,128]{2,1,0:T(8,128)} async-done(((f32[64,32,128]{2,1,0:T(8,128)}), f32[64,32,128]{2,1,0:T(8,128)}, u32[]{:S(2)}, u32[]{:S(2)}) %all-to-all-start.4) | async-done | bytes 1048608 | tf_op jit(solution)/shard_map/all_to_all | solution.py:155
  200.1 7.6 %all-to-all-start.5 = ((f32[64,32,384]{2,1,0:T(8,128)}), f32[64,32,384]{2,1,0:T(8,128)S(1)}, u32[]{:S(2)}, u32[]{:S(2)}) async-start(f32[64,32,384]{2,1,0:T(8,128)} %fusion.6), calls=%async_computation.5 | async-start | bytes 6291456 | tf_op jit(solution)/shard_map/all_to_all | solution.py:155
  207.7 1.4 reduce_sum.18
  209.1 0.6 broadcast_multiply_fusion.1
  209.7 1.8 pad_maximum_fusion.4
  211.5 1.2 fusion.29
  212.7 1.1 pad_maximum_fusion.2
  213.8 35.0 %all-to-all-done.5 = f32[64,32,384]{2,1,0:T(8,128)S(1)} async-done(((f32[64,32,384]{2,1,0:T(8,128)}), f32[64,32,384]{2,1,0:T(8,128)S(1)}, u32[]{:S(2)}, u32[]{:S(2)}) %all-to-all-start.5) | async-done | bytes 3145760 | tf_op jit(solution)/shard_map/all_to_all | solution.py:155
  248.8 0.2 reduce_sum.19
  249.0 0.6 pad_maximum_fusion.7
  (28 shorter events, 0.1 us)
Async XLA Ops:
  8.7 33.3 %all-to-all-start = ((bf16[128,4,1280]{2,1,0:T(4,128)(2,1)}), bf16[128,4,1280]{2,1,0:T(4,128)(2,1)S(1)}, u32[]{:S(2)}, u32[]{:S(2)}) async-start(bf16[128,4,1280]{2,1,0:T(4,128)(2,1)} %reshape.191), calls=%async_computation | async-start | bytes 2621440 | tf_op jit(solution)/shard_map/all_to_all | solution.py:133
  19.9 1.1 slice-start
  19.9 1.4 slice-start.1
  19.9 1.4 slice-start.3
  19.9 1.4 slice-start.4
  33.3 14.5 %copy-start.7 = (s32[1,4]{1,0:T(1,128)S(1)}, s32[1,4]{1,0:T(1,128)}, u32[]{:S(2)}) copy-start(s32[1,4]{1,0:T(1,128)} %param.13) | copy-start | bytes 52
  42.1 55.7 %all-to-all-start.2 = ((bf16[128,4,3840]{2,1,0:T(4,128)(2,1)}), bf16[128,4,3840]{2,1,0:T(4,128)(2,1)}, u32[]{:S(2)}, u32[]{:S(2)}) async-start(bf16[128,4,3840]{2,1,0:T(4,128)(2,1)} %reshape.199), calls=%async_computation.2 | async-start | bytes 7864320 | tf_op jit(solution)/shard_map/all_to_all | solution.py:133
  97.8 34.5 %all-to-all-start.1 = ((bf16[128,4,768]{2,1,0:T(4,128)(2,1)}), bf16[128,4,768]{2,1,0:T(4,128)(2,1)S(1)}, u32[]{:S(2)}, u32[]{:S(2)}) async-start(bf16[128,4,768]{2,1,0:T(4,128)(2,1)} %reshape.184), calls=%async_computation.1 | async-start | bytes 1572864 | tf_op jit(solution)/shard_map/all_to_all | solution.py:136
  132.3 0.9 copy-start.1
  133.2 43.1 %all-to-all-start.3 = ((bf16[128,4,2304]{2,1,0:T(4,128)(2,1)}), bf16[128,4,2304]{2,1,0:T(4,128)(2,1)}, u32[]{:S(2)}, u32[]{:S(2)}) async-start(bf16[128,4,2304]{2,1,0:T(4,128)(2,1)} %reshape.187), calls=%async_computation.3 | async-start | bytes 4718592 | tf_op jit(solution)/shard_map/all_to_all | solution.py:136
  147.7 7.2 %collective-permute-start = (bf16[256,64,32]{0,2,1:T(8,128)(2,1)}, bf16[256,64,32]{0,2,1:T(8,128)(2,1)S(1)}, u32[]{:S(2)}, u32[]{:S(2)}) collective-permute-start(bf16[256,64,32]{0,2,1:T(8,128)(2,1)} %get-tuple-element.5), channel_id=1, source_target_pairs={{0,1},{1,0},{2,3},{3,2},{4,5},{5,4},{6,7},{7,6},{8,9},{9,8},{10,11... | collective-permute-start | bytes 3145736 | tf_op jit(solution)/shard_map/ppermute | solution.py:124
  153.7 1.2 copy-start.2
  154.4 2.9 %copy-start.5 = (bf16[256,128]{1,0:T(8,128)(2,1)}, bf16[256,128]{1,0:T(8,128)(2,1)S(1)}, u32[]{:S(2)}) copy-start(bf16[256,128]{1,0:T(8,128)(2,1)S(1)} %get-tuple-element.15) | copy-start | bytes 196612
  154.4 2.9 %collective-permute-start.1 = (bf16[256,128]{1,0:T(8,128)(2,1)S(1)}, bf16[256,128]{1,0:T(8,128)(2,1)S(1)}, u32[]{:S(2)}, u32[]{:S(2)}) collective-permute-start(bf16[256,128]{1,0:T(8,128)(2,1)S(1)} %get-tuple-element.15), channel_id=1, source_target_pairs={{0,1},{1,0},{2,3},{3,2},{4,5},{5,4},{6,7},{7,6},{8,9},{9,8},{10,11... | collective-permute-start | bytes 196616 | tf_op jit(solution)/shard_map/ppermute | solution.py:150
  154.9 1.0 copy-start.4
  176.3 23.9 %all-to-all-start.4 = ((f32[64,32,128]{2,1,0:T(8,128)}), f32[64,32,128]{2,1,0:T(8,128)}, u32[]{:S(2)}, u32[]{:S(2)}) async-start(f32[64,32,128]{2,1,0:T(8,128)} %fusion.21), calls=%async_computation.4 | async-start | bytes 2097152 | tf_op jit(solution)/shard_map/all_to_all | solution.py:155
  192.1 5.3 %copy-start = (bf16[256,2304]{1,0:T(8,128)(2,1)}, bf16[256,2304]{1,0:T(8,128)(2,1)S(1)}, u32[]{:S(2)}) copy-start(bf16[256,2304]{1,0:T(8,128)(2,1)S(1)} %scatter_custom_fusion.1) | copy-start | bytes 3538948
  193.0 4.4 %copy-start.3 = (bf16[256,128]{1,0:T(8,128)(2,1)}, bf16[256,128]{1,0:T(8,128)(2,1)S(1)}, u32[]{:S(2)}) copy-start(bf16[256,128]{1,0:T(8,128)(2,1)S(1)} %get-tuple-element.8) | copy-start | bytes 196612
  193.0 1.5 collective-permute-start.2
  200.1 48.6 %all-to-all-start.5 = ((f32[64,32,384]{2,1,0:T(8,128)}), f32[64,32,384]{2,1,0:T(8,128)S(1)}, u32[]{:S(2)}, u32[]{:S(2)}) async-start(f32[64,32,384]{2,1,0:T(8,128)} %fusion.6), calls=%async_computation.5 | async-start | bytes 6291456 | tf_op jit(solution)/shard_map/all_to_all | solution.py:155
  207.7 5.0 %slice-start.2 = ((bf16[256,768]{1,0:T(8,128)(2,1)}), bf16[256,512]{1,0:T(8,128)(2,1)S(1)}, s32[]{:S(2)}) async-start(bf16[256,768]{1,0:T(8,128)(2,1)} %copy-done.2), calls=%async_computation.8 | async-start | bytes 524288 | tf_op jit(solution)/shard_map/slice | solution.py:144
  213.8 35.2 %copy-start.6 = (f32[32,128]{1,0:T(8,128)S(1)}, f32[32,128]{1,0:T(8,128)}, u32[]{:S(2)}) copy-start(f32[32,128]{1,0:T(8,128)} %broadcast_multiply_fusion.1) | copy-start | bytes 49156

commit v11 on v10

--- a/solution.py
+++ b/solution.py
@@ -98,7 +98,7 @@
 
 CHIP, CORE = "chip", "core"
 DP = (CHIP, CORE)
-PARTS = ((0, 1), (1, HK - 1))
+PARTS = ((0, HK - 1), (HK - 1, 1))
 
 
 def local(hidden_in, queries, keys, values, grad_attn, send_rows, slot_docs):

time: 252 us -> 252 us (level)
  no operation moved by 1% of the time
where the time goes in v11:
time: 252 us; the launch traced here: 250 us
  waiting for transfers between devices  101 us (40%)
  local copies, waits for them, and re-layouts  62.8 us (25%)
  starting transfers between devices  46 us (18%)
  Pallas kernels  24.5 us (10%)
  other arithmetic  9.51 us (4%)
  matrix products  4.56 us (2%)
    all_to_all x2, waiting for transfers between devices, local(): rows_in = lax.all_to_all(table[pick_rows], DP, 0, 0, tiled=True)  44.8 us
    all_to_all x2, waiting for transfers between devices, local(): lax.all_to_all(partial, CHIP, 0, 0, tiled=True).sum(0) * grad_scale  37.7 us
    pallas_call x2, Pallas kernels, attend_rows(): pl.pallas_call(attend_kernel, grid=(n_kv,), in_specs=[col, row, col, row,...  24.5 us
    all_to_all x2, waiting for transfers between devices, local(): lax.all_to_all(rows_out.reshape(owners, slot_count, rows_out.shape[1]), D...  17.3 us
    all_to_all x2, starting transfers between devices, local(): rows_in = lax.all_to_all(table[pick_rows], DP, 0, 0, tiled=True)  16.9 us
    gather x4, local copies, waits for them, and re-layouts, local(): rows_in = lax.all_to_all(table[pick_rows], DP, 0, 0, tiled=True)  15.3 us
    all_to_all x2, starting transfers between devices, local(): lax.all_to_all(rows_out.reshape(owners, slot_count, rows_out.shape[1]), D...  15.2 us
    all_to_all x2, starting transfers between devices, local(): lax.all_to_all(partial, CHIP, 0, 0, tiled=True).sum(0) * grad_scale  13.3 us
  transfers between devices with their start and end apart: 9, of which 6 were waited for; matrix products, arithmetic and copies ran while one was open for 26% of the time, Pallas kernels for 10%

profile of v11, /device:TPU:0, one launch (start us, length us, event | category | flops | bytes accessed | tf_op | source)
XLA Modules:
  0.0 249.6 jit_solution(16194093808539186394)
XLA Ops:
  0.6 0.7 compare_select_fusion.1
  1.3 0.1 copy.17
  1.4 0.1 reshape.192
  1.6 0.8 slice.69
  2.4 0.8 slice.70
  3.2 1.0 slice.67
  4.2 1.0 slice.68
  5.2 0.1 pad_maximum_fusion.3
  5.2 2.1 gather_fusion.1
  7.4 1.3 reshape.199
  8.7 11.2 %all-to-all-start.2 = ((bf16[128,4,1280]{2,1,0:T(4,128)(2,1)}), bf16[128,4,1280]{2,1,0:T(4,128)(2,1)S(1)}, u32[]{:S(2)}, u32[]{:S(2)}) async-start(bf16[128,4,1280]{2,1,0:T(4,128)(2,1)} %reshape.199), calls=%async_computation.2 | async-start | bytes 2621440 | tf_op jit(solution)/shard_map/all_to_all | solution.py:133
  20.0 1.1 slice-done
  21.0 0.2 slice-done.1
  21.3 0.0 slice-done.3
  21.3 0.1 slice-done.4
  21.4 0.1 pad_maximum_fusion.1
  21.5 4.4 %gather_fusion = bf16[512,3840]{1,0:T(8,128)(2,1)} fusion(bf16[256,3840]{1,0:T(8,128)(2,1)S(1)} %pad_maximum_fusion.1, s32[1024]{0:T(1024)S(1)} %pad_clamp_fusion), kind=kCustom, calls=%fused_computation | custom fusion | bytes 7866368 | tf_op jit(solution)/shard_map/gather | solution.py:133
  25.9 7.4 %reshape.191 = bf16[128,4,3840]{2,1,0:T(4,128)(2,1)} reshape(bf16[512,3840]{1,0:T(8,128)(2,1)} %gather_fusion) | data formatting | bytes 7864320 | tf_op jit(solution)/shard_map/gather | solution.py:133
  33.3 8.8 %all-to-all-done.2 = bf16[128,4,1280]{2,1,0:T(4,128)(2,1)S(1)} async-done(((bf16[128,4,1280]{2,1,0:T(4,128)(2,1)}), bf16[128,4,1280]{2,1,0:T(4,128)(2,1)S(1)}, u32[]{:S(2)}, u32[]{:S(2)}) %all-to-all-start.2) | async-done | bytes 1310752 | tf_op jit(solution)/shard_map/all_to_all | solution.py:133
  42.1 5.8 %all-to-all-start = ((bf16[128,4,3840]{2,1,0:T(4,128)(2,1)}), bf16[128,4,3840]{2,1,0:T(4,128)(2,1)}, u32[]{:S(2)}, u32[]{:S(2)}) async-start(bf16[128,4,3840]{2,1,0:T(4,128)(2,1)} %reshape.191), calls=%async_computation | async-start | bytes 7864320 | tf_op jit(solution)/shard_map/all_to_all | solution.py:133
  47.9 0.7 reshape_tile.9.seg_row_ref
  48.5 0.8 reshape_tile.10.seg_col_ref
  49.4 0.6 fusion.25.key_row_ref
  50.0 0.8 fusion.15.key_col_ref
  50.7 1.3 reshape.186.q_ref.k_ref.v_ref.o_ref
  52.0 7.3 %shard_map.103 = bf16[512,768]{1,0:T(8,128)(2,1)} custom-call(s32[512,1]{1,0:T(8,128)} %reshape_tile.10.seg_col_ref, s32[1,512]{1,0:T(1,128)} %reshape_tile.9.seg_row_ref, s32[512,1]{1,0:T(8,128)} %fusion.15.key_col_ref, s32[1,512]{1,0:T(1,128)} %fusion.25.key_row_ref, bf16[512,1280]{1,0:T(8,128)(2,1)} %reshape.186.q_ref.k_ref.v_ref.o_ref, ...), custom_call_target="tpu_custom_call" | custom-call | tf_op jit(solution)/shard_map/pallas_call | solution.py:70
  59.3 2.4 reshape.187
  61.7 36.1 %all-to-all-done = bf16[128,4,3840]{2,1,0:T(4,128)(2,1)} async-done(((bf16[128,4,3840]{2,1,0:T(4,128)(2,1)}), bf16[128,4,3840]{2,1,0:T(4,128)(2,1)}, u32[]{:S(2)}, u32[]{:S(2)}) %all-to-all-start) | async-done | bytes 3932192 | tf_op jit(solution)/shard_map/all_to_all | solution.py:133
  97.8 5.1 %all-to-all-start.3 = ((bf16[128,4,768]{2,1,0:T(4,128)(2,1)}), bf16[128,4,768]{2,1,0:T(4,128)(2,1)S(1)}, u32[]{:S(2)}, u32[]{:S(2)}) async-start(bf16[128,4,768]{2,1,0:T(4,128)(2,1)} %reshape.187), calls=%async_computation.3 | async-start | bytes 1572864 | tf_op jit(solution)/shard_map/all_to_all | solution.py:136
  102.9 7.1 %reshape.183.q_ref.k_ref.v_ref.o_ref = bf16[512,3840]{1,0:T(8,128)(2,1)} reshape(bf16[128,4,3840]{2,1,0:T(4,128)(2,1)} %all-to-all-done) | data formatting | bytes 7864320 | tf_op jit(solution)/shard_map/reshape | solution.py:134
  110.0 17.2 %shard_map.102 = bf16[512,2304]{1,0:T(8,128)(2,1)} custom-call(s32[512,1]{1,0:T(8,128)} %reshape_tile.10.seg_col_ref, s32[1,512]{1,0:T(1,128)} %reshape_tile.9.seg_row_ref, s32[512,1]{1,0:T(8,128)} %fusion.15.key_col_ref, s32[1,512]{1,0:T(1,128)} %fusion.25.key_row_ref, bf16[512,3840]{1,0:T(8,128)(2,1)} %reshape.183.q_ref.k_ref.v_ref.o_ref, ...), custom_call_target="tpu_custom_call" | custom-call | tf_op jit(solution)/shard_map/pallas_call | solution.py:70
  127.3 5.0 %reshape.184 = bf16[128,4,2304]{2,1,0:T(4,128)(2,1)} reshape(bf16[512,2304]{1,0:T(8,128)(2,1)} %shard_map.102) | data formatting | bytes 4718592 | tf_op jit(solution)/shard_map/reshape | solution.py:137
  132.3 0.9 copy-done.1
  133.2 10.1 %all-to-all-start.1 = ((bf16[128,4,2304]{2,1,0:T(4,128)(2,1)}), bf16[128,4,2304]{2,1,0:T(4,128)(2,1)}, u32[]{:S(2)}, u32[]{:S(2)}) async-start(bf16[128,4,2304]{2,1,0:T(4,128)(2,1)} %reshape.184), calls=%async_computation.1 | async-start | bytes 4718592 | tf_op jit(solution)/shard_map/all_to_all | solution.py:136
  143.2 3.3 %copy.20 = bf16[256,4096]{0,1:T(8,128)(2,1)S(1)} copy(bf16[256,4096]{1,0:T(8,128)(2,1)} %param.7) | data formatting | bytes 4194304 | tf_op args[0]
  146.5 1.2 constant_dynamic-slice_fusion
  147.7 0.1 copy.13
  147.8 0.1 reshape.228
  147.9 0.1 fusion.18
  148.1 2.3 reshape.218
  150.4 3.3 %scatter_custom_fusion.1 = bf16[256,768]{1,0:T(8,128)(2,1)S(1)} fusion(s32[512]{0:T(512)S(1)} %fusion.18, bf16[512,768]{1,0:T(8,128)(2,1)} %reshape.218, bf16[]{:T(256)} %constant.53.clone.1), kind=kCustom, calls=%fused_computation.37 | custom fusion | bytes 393728 | tf_op jit(solution)/shard_map/scatter | solution.py:142
  153.7 0.7 fusion.30
  154.4 0.5 collective-permute-start.2
  154.9 1.0 copy-done.4
  155.8 1.4 pad_maximum_fusion
  157.2 1.7 fusion.21
  158.9 17.3 %all-to-all-done.1 = bf16[128,4,2304]{2,1,0:T(4,128)(2,1)} async-done(((bf16[128,4,2304]{2,1,0:T(4,128)(2,1)}), bf16[128,4,2304]{2,1,0:T(4,128)(2,1)}, u32[]{:S(2)}, u32[]{:S(2)}) %all-to-all-start.1) | async-done | bytes 2359328 | tf_op jit(solution)/shard_map/all_to_all | solution.py:136
  176.3 5.7 %all-to-all-start.5 = ((f32[64,32,128]{2,1,0:T(8,128)}), f32[64,32,128]{2,1,0:T(8,128)}, u32[]{:S(2)}, u32[]{:S(2)}) async-start(f32[64,32,128]{2,1,0:T(8,128)} %fusion.21), calls=%async_computation.5 | async-start | bytes 2097152 | tf_op jit(solution)/shard_map/all_to_all | solution.py:155
  182.0 4.8 %reshape.210 = bf16[512,2304]{1,0:T(8,128)(2,1)} reshape(bf16[128,4,2304]{2,1,0:T(4,128)(2,1)} %all-to-all-done.1) | data formatting | bytes 4718592 | tf_op jit(solution)/shard_map/reshape | solution.py:142
  186.9 5.3 %scatter_custom_fusion = bf16[256,2304]{1,0:T(8,128)(2,1)S(1)} fusion(s32[512]{0:T(512)S(1)} %fusion.18, bf16[512,2304]{1,0:T(8,128)(2,1)} %reshape.210, bf16[]{:T(256)} %constant.53.clone.1), kind=kCustom, calls=%fused_computation.10 | custom fusion | bytes 1180160 | tf_op jit(solution)/shard_map/scatter | solution.py:142
  192.1 0.8 fusion.28
  193.0 0.1 collective-permute-start.1
  193.1 1.4 collective-permute-done.1
  194.5 2.9 %fusion.6 = f32[64,32,384]{2,1,0:T(8,128)} fusion(bf16[64,32,512]{2,1,0:T(8,128)(2,1)S(1)} %bitcast.25, bf16[256,384]{1,0:T(8,128)(2,1)S(1)} %collective-permute-done.1, bf16[256,128]{1,0:T(8,128)(2,1)S(1)} %get-tuple-element.7, bf16[256,128]{1,0:T(8,128)(2,1)S(1)} %get-tuple-element.8, bf16[256,128]{1,0:T(8,128)(2,1)S(1)} %get-tuple-element.6), kind=kOutput, calls=%fused_computation.20 | convolution fusion | flops 806879232 | bytes 5636096 | tf_op jit(solution)/shard_map/td,tc->dc/dot_general | solution.py:151
  197.4 2.7 %all-to-all-done.5 = f32[64,32,128]{2,1,0:T(8,128)} async-done(((f32[64,32,128]{2,1,0:T(8,128)}), f32[64,32,128]{2,1,0:T(8,128)}, u32[]{:S(2)}, u32[]{:S(2)}) %all-to-all-start.5) | async-done | bytes 1048608 | tf_op jit(solution)/shard_map/all_to_all | solution.py:155
  200.1 7.5 %all-to-all-start.4 = ((f32[64,32,384]{2,1,0:T(8,128)}), f32[64,32,384]{2,1,0:T(8,128)S(1)}, u32[]{:S(2)}, u32[]{:S(2)}) async-start(f32[64,32,384]{2,1,0:T(8,128)} %fusion.6), calls=%async_computation.4 | async-start | bytes 6291456 | tf_op jit(solution)/shard_map/all_to_all | solution.py:155
  207.7 1.4 reduce_sum.19
  209.1 0.6 broadcast_multiply_fusion.1
  209.7 1.8 pad_maximum_fusion.4
  211.5 1.2 fusion.29
  212.7 1.1 pad_maximum_fusion.2
  213.8 35.0 %all-to-all-done.4 = f32[64,32,384]{2,1,0:T(8,128)S(1)} async-done(((f32[64,32,384]{2,1,0:T(8,128)}), f32[64,32,384]{2,1,0:T(8,128)S(1)}, u32[]{:S(2)}, u32[]{:S(2)}) %all-to-all-start.4) | async-done | bytes 3145760 | tf_op jit(solution)/shard_map/all_to_all | solution.py:155
  248.8 0.2 reduce_sum.18
  248.9 0.6 pad_maximum_fusion.7
  (28 shorter events, 0.1 us)
Async XLA Ops:
  8.7 33.3 %all-to-all-start.2 = ((bf16[128,4,1280]{2,1,0:T(4,128)(2,1)}), bf16[128,4,1280]{2,1,0:T(4,128)(2,1)S(1)}, u32[]{:S(2)}, u32[]{:S(2)}) async-start(bf16[128,4,1280]{2,1,0:T(4,128)(2,1)} %reshape.199), calls=%async_computation.2 | async-start | bytes 2621440 | tf_op jit(solution)/shard_map/all_to_all | solution.py:133
  19.9 1.1 slice-start
  19.9 1.4 slice-start.1
  19.9 1.4 slice-start.3
  19.9 1.4 slice-start.4
  33.3 14.5 %copy-start.7 = (s32[1,4]{1,0:T(1,128)S(1)}, s32[1,4]{1,0:T(1,128)}, u32[]{:S(2)}) copy-start(s32[1,4]{1,0:T(1,128)} %param.13) | copy-start | bytes 52
  42.1 55.7 %all-to-all-start = ((bf16[128,4,3840]{2,1,0:T(4,128)(2,1)}), bf16[128,4,3840]{2,1,0:T(4,128)(2,1)}, u32[]{:S(2)}, u32[]{:S(2)}) async-start(bf16[128,4,3840]{2,1,0:T(4,128)(2,1)} %reshape.191), calls=%async_computation | async-start | bytes 7864320 | tf_op jit(solution)/shard_map/all_to_all | solution.py:133
  97.8 34.5 %all-to-all-start.3 = ((bf16[128,4,768]{2,1,0:T(4,128)(2,1)}), bf16[128,4,768]{2,1,0:T(4,128)(2,1)S(1)}, u32[]{:S(2)}, u32[]{:S(2)}) async-start(bf16[128,4,768]{2,1,0:T(4,128)(2,1)} %reshape.187), calls=%async_computation.3 | async-start | bytes 1572864 | tf_op jit(solution)/shard_map/all_to_all | solution.py:136
  132.3 0.9 copy-start.1
  133.2 43.1 %all-to-all-start.1 = ((bf16[128,4,2304]{2,1,0:T(4,128)(2,1)}), bf16[128,4,2304]{2,1,0:T(4,128)(2,1)}, u32[]{:S(2)}, u32[]{:S(2)}) async-start(bf16[128,4,2304]{2,1,0:T(4,128)(2,1)} %reshape.184), calls=%async_computation.1 | async-start | bytes 4718592 | tf_op jit(solution)/shard_map/all_to_all | solution.py:136
  147.7 7.2 %collective-permute-start = (bf16[256,64,32]{0,2,1:T(8,128)(2,1)}, bf16[256,64,32]{0,2,1:T(8,128)(2,1)S(1)}, u32[]{:S(2)}, u32[]{:S(2)}) collective-permute-start(bf16[256,64,32]{0,2,1:T(8,128)(2,1)} %get-tuple-element.5), channel_id=1, source_target_pairs={{0,1},{1,0},{2,3},{3,2},{4,5},{5,4},{6,7},{7,6},{8,9},{9,8},{10,11... | collective-permute-start | bytes 3145736 | tf_op jit(solution)/shard_map/ppermute | solution.py:124
  153.7 1.2 copy-start.2
  154.4 2.9 %copy-start.5 = (bf16[256,128]{1,0:T(8,128)(2,1)}, bf16[256,128]{1,0:T(8,128)(2,1)S(1)}, u32[]{:S(2)}) copy-start(bf16[256,128]{1,0:T(8,128)(2,1)S(1)} %get-tuple-element.15) | copy-start | bytes 196612
  154.4 2.9 %collective-permute-start.2 = (bf16[256,128]{1,0:T(8,128)(2,1)S(1)}, bf16[256,128]{1,0:T(8,128)(2,1)S(1)}, u32[]{:S(2)}, u32[]{:S(2)}) collective-permute-start(bf16[256,128]{1,0:T(8,128)(2,1)S(1)} %get-tuple-element.15), channel_id=1, source_target_pairs={{0,1},{1,0},{2,3},{3,2},{4,5},{5,4},{6,7},{7,6},{8,9},{9,8},{10,11... | collective-permute-start | bytes 196616 | tf_op jit(solution)/shard_map/ppermute | solution.py:150
  154.9 1.0 copy-start.4
  176.3 23.9 %all-to-all-start.5 = ((f32[64,32,128]{2,1,0:T(8,128)}), f32[64,32,128]{2,1,0:T(8,128)}, u32[]{:S(2)}, u32[]{:S(2)}) async-start(f32[64,32,128]{2,1,0:T(8,128)} %fusion.21), calls=%async_computation.5 | async-start | bytes 2097152 | tf_op jit(solution)/shard_map/all_to_all | solution.py:155
  192.1 5.3 %copy-start = (bf16[256,2304]{1,0:T(8,128)(2,1)}, bf16[256,2304]{1,0:T(8,128)(2,1)S(1)}, u32[]{:S(2)}) copy-start(bf16[256,2304]{1,0:T(8,128)(2,1)S(1)} %scatter_custom_fusion) | copy-start | bytes 3538948
  192.9 4.4 %copy-start.3 = (bf16[256,128]{1,0:T(8,128)(2,1)}, bf16[256,128]{1,0:T(8,128)(2,1)S(1)}, u32[]{:S(2)}) copy-start(bf16[256,128]{1,0:T(8,128)(2,1)S(1)} %get-tuple-element.8) | copy-start | bytes 196612
  193.0 1.5 collective-permute-start.1
  200.1 48.6 %all-to-all-start.4 = ((f32[64,32,384]{2,1,0:T(8,128)}), f32[64,32,384]{2,1,0:T(8,128)S(1)}, u32[]{:S(2)}, u32[]{:S(2)}) async-start(f32[64,32,384]{2,1,0:T(8,128)} %fusion.6), calls=%async_computation.4 | async-start | bytes 6291456 | tf_op jit(solution)/shard_map/all_to_all | solution.py:155
  207.7 5.0 %slice-start.2 = ((bf16[256,768]{1,0:T(8,128)(2,1)}), bf16[256,512]{1,0:T(8,128)(2,1)S(1)}, s32[]{:S(2)}) async-start(bf16[256,768]{1,0:T(8,128)(2,1)} %copy-done.2), calls=%async_computation.8 | async-start | bytes 524288 | tf_op jit(solution)/shard_map/slice | solution.py:144
  213.8 35.2 %copy-start.6 = (f32[32,128]{1,0:T(8,128)S(1)}, f32[32,128]{1,0:T(8,128)}, u32[]{:S(2)}) copy-start(f32[32,128]{1,0:T(8,128)} %broadcast_multiply_fusion.1) | copy-start | bytes 49156
